TPU v7x, 512 devices: a whole 4x8x8 slice. The times are simulated.
512 devices in a mesh: stretch: 32 (over y_hi, z), head: 8 (over x, y_lo), cfg: 2 (over core).
Axes of the slice: x: 4, y: 8 (y_hi: 4, y_lo: 2; y = y_hi * 2 + y_lo), z: 8, core: 2. Of those that a mesh axis runs over, the one named last changes fastest.
Arguments:
- queries: bfloat16 [57344, 5120], P(('cfg', 'stretch', 'head')), parts along dimension 0, may hold values from -6 to 6
- keys: bfloat16 [57344, 5120], P(('cfg', 'stretch', 'head')), parts along dimension 0, may hold values from -6 to 6
- values: bfloat16 [57344, 5120], P(('cfg', 'stretch', 'head')), parts along dimension 0, may hold values from -6 to 6
- frames: int32 [32], replicated, may hold values from 4 to 7, as said below
- motion: int32 [32], replicated, may hold values from 0 to 4, as said below
Outputs:
- attended: bfloat16 [57344, 5120], P(('cfg', 'stretch', 'head')), parts along dimension 0
There are 2 independent parts, one for each index of `cfg`. A program takes and returns all parts, laid end to end along the dimension named above; an argument that names none is the same for every part. Nothing has to cross between parts.
Inputs may be any that keep to these rules, and one draw needn't show every extreme that they name: Every stretch holds at least 4 frames; some stretch holds 7. `motion`: stretch 0 takes none; some stretch takes 4.
All inputs are finite; a program needn't handle non-finite values.
Results may differ from a plain program's by a relative error of at most 0.0046.
Values may be sent and summed in bfloat16 or wider, within the bound.
No kernel may reach another device: no remote copies, remote signals or barrier semaphores. Data moves between devices by JAX's collectives and lax.ppermute only.
A program may use at most 128 MiB of HBM per device.

v0:
```python
import math

import jax
import jax.numpy as jnp
from jax import lax
from jax.sharding import PartitionSpec as P

HD = 128
FT = 128
MOT_CAP = 4


NEG = -1e30


def from_behind(shard, axis, by):
    size = lax.axis_size(axis)
    pairs = [(i, i + by) for i in range(size) if 0 <= i + by < size]
    return lax.ppermute(shard, axis, pairs)


def head_block(q_head, k_head, v_head, key_live):
    scores = lax.dot_general(
        q_head, k_head, (((1,), (1,)), ((), ())), preferred_element_type=jnp.float32
    )
    scores = scores * (1.0 / math.sqrt(q_head.shape[1]))
    masked = jnp.where(key_live[None, :], scores, NEG)
    top = jnp.max(masked, axis=1)
    weights = jnp.where(key_live[None, :], jnp.exp(masked - top[:, None]), 0.0)
    total = jnp.sum(weights, axis=1)
    acc = jnp.dot(weights.astype(jnp.bfloat16), v_head, preferred_element_type=jnp.float32)
    return (top, total, acc)


def pick_head(array, index):
    return lax.dynamic_index_in_dim(array, index, 1, keepdims=False)


def own_part(queries, keys, values, key_live):
    rows, count, width = queries.shape
    start = (
        jnp.zeros((rows, count), jnp.float32),
        jnp.zeros((rows, count), jnp.float32),
        jnp.zeros((rows, count, width), jnp.float32),
    )

    def own_step(index, carry):
        tops, totals, accs = carry
        top, total, acc = head_block(
            pick_head(queries, index), pick_head(keys, index), pick_head(values, index), key_live
        )
        tops = lax.dynamic_update_index_in_dim(tops, top, index, 1)
        totals = lax.dynamic_update_index_in_dim(totals, total, index, 1)
        accs = lax.dynamic_update_index_in_dim(accs, acc, index, 1)
        return (tops, totals, accs)

    return lax.fori_loop(0, count, own_step, start)


def finish(queries, motion_keys, motion_values, motion_live, query_live, partial_value):
    tops, totals, accs = partial_value
    count = queries.shape[1]

    def finish_step(index, result):
        top, total, acc = head_block(
            pick_head(queries, index),
            pick_head(motion_keys, index),
            pick_head(motion_values, index),
            motion_live,
        )
        top_own = pick_head(tops, index)
        total_own = pick_head(totals, index)
        acc_own = pick_head(accs, index)
        peak = jnp.maximum(top_own, top)
        factor_own = jnp.exp(top_own - peak)
        factor_mot = jnp.exp(top - peak)
        mixed = (acc_own * factor_own[:, None] + acc * factor_mot[:, None]) / (
            total_own * factor_own + total * factor_mot
        )[:, None]
        mixed = jnp.where(query_live[:, None], mixed, 0.0).astype(jnp.bfloat16)
        return lax.dynamic_update_index_in_dim(result, mixed, index, 1)

    return lax.fori_loop(0, count, finish_step, jnp.zeros(queries.shape, jnp.bfloat16))


def body(queries, keys, values, frames, motion):
    rows, width = queries.shape
    groups = lax.axis_size("head")
    stretch_index = lax.axis_index("stretch")
    span = rows * groups
    tail = MOT_CAP * FT
    local = width // groups
    count_own = frames[stretch_index]
    spot = jnp.arange(span, dtype=jnp.int32) // FT
    slot = jnp.arange(tail, dtype=jnp.int32) // FT
    live = spot < count_own
    motion_live = slot >= MOT_CAP - motion[stretch_index]
    tail_begin = (count_own - MOT_CAP) * FT
    q_heads, k_heads, v_heads = (
        lax.all_to_all(queries, "head", split_axis=1, concat_axis=0, tiled=True),
        lax.all_to_all(keys, "head", split_axis=1, concat_axis=0, tiled=True),
        lax.all_to_all(values, "head", split_axis=1, concat_axis=0, tiled=True),
    )
    k_tail = lax.dynamic_slice_in_dim(k_heads, tail_begin, tail, 0)
    v_tail = lax.dynamic_slice_in_dim(v_heads, tail_begin, tail, 0)
    k_prior, v_prior = from_behind((k_tail, v_tail), "stretch", 1)
    count = local // HD
    q_shaped = q_heads.reshape(span, count, HD)
    partial_value = own_part(
        q_shaped, k_heads.reshape(span, count, HD), v_heads.reshape(span, count, HD), live
    )
    mixed = finish(
        q_shaped,
        k_prior.reshape(tail, count, HD),
        v_prior.reshape(tail, count, HD),
        motion_live,
        live,
        partial_value,
    )
    result = lax.all_to_all(
        mixed.reshape(span, local), "head", split_axis=0, concat_axis=1, tiled=True
    )
    return result


def solution(mesh):
    placed = (
        P(("cfg", "stretch", "head"), None),
        P(("cfg", "stretch", "head"), None),
        P(("cfg", "stretch", "head"), None),
        P(),
        P(),
    )
    return jax.shard_map(
        body,
        mesh=mesh,
        in_specs=placed,
        out_specs=P(("cfg", "stretch", "head"), None),
        check_vma=False,
    )
```

profile of v0, /device:TPU:56, one launch (start us, length us, event | category | flops | bytes accessed | tf_op | source)
XLA Modules:
  0.0 170.6 jit_solution(14587731562828951928)
XLA Ops:
  0.0 2.5 %copy.98 = bf16[14,8,8,640]{3,2,0,1:T(8,128)(2,1)} copy(bf16[14,8,8,640]{3,2,1,0:T(8,128)(2,1)} %bitcast.91) | data formatting | bytes 2293760 | tf_op jit(solution)/shard_map/all_to_all | solution.py:101
  2.5 5.8 %all-to-all-start.1 = ((bf16[112,8,640]{2,0,1:T(8,128)(2,1)}), bf16[112,8,640]{2,0,1:T(8,128)(2,1)S(1)}, u32[]{:S(2)}, u32[]{:S(2)}) async-start(bf16[112,8,640]{2,0,1:T(8,128)(2,1)} %bitcast.64), calls=%async_computation.1 | async-start | bytes 2293760 | tf_op jit(solution)/shard_map/all_to_all | solution.py:101
  9.3 14.5 %all-to-all-done.1 = bf16[112,8,640]{2,0,1:T(8,128)(2,1)S(1)} async-done(((bf16[112,8,640]{2,0,1:T(8,128)(2,1)}), bf16[112,8,640]{2,0,1:T(8,128)(2,1)S(1)}, u32[]{:S(2)}, u32[]{:S(2)}) %all-to-all-start.1) | async-done | bytes 1146912 | tf_op jit(solution)/shard_map/all_to_all | solution.py:101
  23.8 4.7 %all-to-all-start.2 = ((bf16[112,8,640]{2,0,1:T(8,128)(2,1)}), bf16[112,8,640]{2,0,1:T(8,128)(2,1)S(1)}, u32[]{:S(2)}, u32[]{:S(2)}) async-start(bf16[112,8,640]{2,0,1:T(8,128)(2,1)} %bitcast.63), calls=%async_computation.2 | async-start | bytes 2293760 | tf_op jit(solution)/shard_map/all_to_all | solution.py:102
  29.6 13.9 %all-to-all-done.2 = bf16[112,8,640]{2,0,1:T(8,128)(2,1)S(1)} async-done(((bf16[112,8,640]{2,0,1:T(8,128)(2,1)}), bf16[112,8,640]{2,0,1:T(8,128)(2,1)S(1)}, u32[]{:S(2)}, u32[]{:S(2)}) %all-to-all-start.2) | async-done | bytes 1146912 | tf_op jit(solution)/shard_map/all_to_all | solution.py:102
  43.5 4.6 %all-to-all-start = ((bf16[112,8,640]{2,0,1:T(8,128)(2,1)}), bf16[112,8,640]{2,0,1:T(8,128)(2,1)S(1)}, u32[]{:S(2)}, u32[]{:S(2)}) async-start(bf16[112,8,640]{2,0,1:T(8,128)(2,1)} %bitcast.65), calls=%async_computation | async-start | bytes 2293760 | tf_op jit(solution)/shard_map/all_to_all | solution.py:100
  51.4 4.3 %collective-permute-start = (bf16[512,640]{1,0:T(8,128)(2,1)}, bf16[512,640]{1,0:T(8,128)(2,1)}, u32[]{:S(2)}, u32[]{:S(2)}) collective-permute-start(bf16[512,640]{1,0:T(8,128)(2,1)} %constant_dynamic-slice_fusion.1), channel_id=1, source_target_pairs={{0,16},{16,32},{32,48},{48,64},{64,80},{80,96},{96,112},{112,128},... | collective-permute-start | bytes 1966088 | tf_op jit(solution)/shard_map/ppermute | solution.py:19
  56.6 4.3 %collective-permute-start.1 = (bf16[512,640]{1,0:T(8,128)(2,1)}, bf16[512,640]{1,0:T(8,128)(2,1)}, u32[]{:S(2)}, u32[]{:S(2)}) collective-permute-start(bf16[512,640]{1,0:T(8,128)(2,1)} %constant_dynamic-slice_fusion.2), channel_id=1, source_target_pairs={{0,16},{16,32},{32,48},{48,64},{64,80},{80,96},{96,112},{112,128},... | collective-permute-start | bytes 1966088 | tf_op jit(solution)/shard_map/ppermute | solution.py:19
  62.8 2.2 %reshape.59 = bf16[896,5,128]{2,1,0:T(8,128)(2,1)} reshape(bf16[8,112,640]{2,1,0:T(8,128)(2,1)S(1)} %bitcast.89) | data formatting | bytes 2293760 | tf_op jit(solution)/shard_map/reshape | solution.py:108
  66.6 2.2 %reshape.56 = bf16[896,5,128]{2,1,0:T(8,128)(2,1)} reshape(bf16[8,112,640]{2,1,0:T(8,128)(2,1)S(1)} %bitcast.85) | data formatting | bytes 2293760 | tf_op jit(solution)/shard_map/reshape | solution.py:110
  70.5 2.2 %reshape.57 = bf16[896,5,128]{2,1,0:T(8,128)(2,1)} reshape(bf16[8,112,640]{2,1,0:T(8,128)(2,1)S(1)} %bitcast.87) | data formatting | bytes 2293760 | tf_op jit(solution)/shard_map/reshape | solution.py:110
  74.4 21.3 %while.32 = (s32[]{:T(128)}, f32[896,5]{0,1:T(8,128)S(1)}, f32[896,5]{0,1:T(8,128)S(1)}, f32[896,5,128]{2,0,1:T(8,128)}, bf16[896,5,128]{2,0,1:T(8,128)(2,1)S(1)...) while((s32[]{:T(128)}, f32[896,5]{0,1:T(8,128)S(1)}, ...), condition=%wide.region_3.4_spmd.clone, body=%wide.region_0.3_spmd.clone.sunk | while | flops 421484672 | bytes 10830193 | solution.py:57
  79.9 1.9 %fusion.91 = f32[896,5,128]{2,0,1:T(8,128)} fusion(f32[896,5,128]{2,0,1:T(8,128)} %get-tuple-element.639, s32[]{:T(128)} %get-tuple-element.636, f32[896,896]{0,1:T(8,128)S(1)} %get-tuple-element.608, f32[896]{0:T(1024)S(1)} %get-tuple-element.607, pred[896]{0:T(1024)(128)(4,1)S(1)} %fusion.88, bf16[896,5,128]{2,0,1:T(8,128)(2,1)S(1)} %get-tuple-element.652), kind=kOutput, calls=%fused_computation.11.clone.1 | convolution fusion | flops 209534976 | bytes 3905536 | tf_op jit(solution)/shard_map/while/body/eval_jaxpr/dot_general | solution.py:31
  84.2 1.9 %fusion.91 = f32[896,5,128]{2,0,1:T(8,128)} fusion(f32[896,5,128]{2,0,1:T(8,128)} %get-tuple-element.639, s32[]{:T(128)} %get-tuple-element.636, f32[896,896]{0,1:T(8,128)S(1)} %get-tuple-element.608, f32[896]{0:T(1024)S(1)} %get-tuple-element.607, pred[896]{0:T(1024)(128)(4,1)S(1)} %fusion.88, bf16[896,5,128]{2,0,1:T(8,128)(2,1)S(1)} %get-tuple-element.652), kind=kOutput, calls=%fused_computation.11.clone.1 | convolution fusion | flops 209534976 | bytes 3905536 | tf_op jit(solution)/shard_map/while/body/eval_jaxpr/dot_general | solution.py:31
  88.4 1.9 %fusion.91 = f32[896,5,128]{2,0,1:T(8,128)} fusion(f32[896,5,128]{2,0,1:T(8,128)} %get-tuple-element.639, s32[]{:T(128)} %get-tuple-element.636, f32[896,896]{0,1:T(8,128)S(1)} %get-tuple-element.608, f32[896]{0:T(1024)S(1)} %get-tuple-element.607, pred[896]{0:T(1024)(128)(4,1)S(1)} %fusion.88, bf16[896,5,128]{2,0,1:T(8,128)(2,1)S(1)} %get-tuple-element.652), kind=kOutput, calls=%fused_computation.11.clone.1 | convolution fusion | flops 209534976 | bytes 3905536 | tf_op jit(solution)/shard_map/while/body/eval_jaxpr/dot_general | solution.py:31
  97.2 9.6 %collective-permute-done.1 = bf16[512,640]{1,0:T(8,128)(2,1)} collective-permute-done((bf16[512,640]{1,0:T(8,128)(2,1)}, bf16[512,640]{1,0:T(8,128)(2,1)}, u32[]{:S(2)}, u32[]{:S(2)}) %collective-permute-start.1) | collective-permute-done | bytes 655392 | tf_op jit(solution)/shard_map/ppermute | solution.py:19
  106.8 2.2 %copy.73 = bf16[512,640]{0,1:T(8,128)(2,1)} copy(bf16[512,640]{1,0:T(8,128)(2,1)} %collective-permute-done.1) | data formatting | bytes 1310720 | tf_op jit(solution)/shard_map/ppermute | solution.py:19
  109.0 20.2 %while.33 = (s32[]{:T(128)}, bf16[896,5,128]{2,0,1:T(8,128)(2,1)S(1)}, f32[896,5,128]{2,0,1:T(8,128)}, f32[896,5]{0,1:T(8,128)S(1)}, bf16[896,5,128]{2,0,1:T(8,1...) while((s32[]{:T(128)}, ...), condition=%wide.region_7.8_spmd.clone, body=%wide.region_4.7_spmd.clone.sunk | while | flops 241549184 | bytes 6757373 | solution.py:83
  110.7 2.3 %fusion.100 = bf16[896,5,128]{2,0,1:T(8,128)(2,1)S(1)} fusion(bf16[896,5,128]{2,0,1:T(8,128)(2,1)S(1)} %get-tuple-element.668, s32[]{:T(128)} %get-tuple-element.667, f32[896,512]{0,1:T(8,128)S(1)} %get-tuple-element.619, f32[896]{0:T(1024)S(1)} %get-tuple-element.620, pred[512]{0:T(512)(128)(4,1)S(1)} %fusion.94, ...), kind=kOutput, calls=%fused_computation.43.clone.1 | convolution fusion | flops 120422400 | bytes 2673152 | tf_op jit(solution)/shard_map/while/body/eval_jaxpr/dot_general | solution.py:31
  114.7 2.3 %fusion.100 = bf16[896,5,128]{2,0,1:T(8,128)(2,1)S(1)} fusion(bf16[896,5,128]{2,0,1:T(8,128)(2,1)S(1)} %get-tuple-element.668, s32[]{:T(128)} %get-tuple-element.667, f32[896,512]{0,1:T(8,128)S(1)} %get-tuple-element.619, f32[896]{0:T(1024)S(1)} %get-tuple-element.620, pred[512]{0:T(512)(128)(4,1)S(1)} %fusion.94, ...), kind=kOutput, calls=%fused_computation.43.clone.1 | convolution fusion | flops 120422400 | bytes 2673152 | tf_op jit(solution)/shard_map/while/body/eval_jaxpr/dot_general | solution.py:31
  118.7 2.3 %fusion.100 = bf16[896,5,128]{2,0,1:T(8,128)(2,1)S(1)} fusion(bf16[896,5,128]{2,0,1:T(8,128)(2,1)S(1)} %get-tuple-element.668, s32[]{:T(128)} %get-tuple-element.667, f32[896,512]{0,1:T(8,128)S(1)} %get-tuple-element.619, f32[896]{0:T(1024)S(1)} %get-tuple-element.620, pred[512]{0:T(512)(128)(4,1)S(1)} %fusion.94, ...), kind=kOutput, calls=%fused_computation.43.clone.1 | convolution fusion | flops 120422400 | bytes 2673152 | tf_op jit(solution)/shard_map/while/body/eval_jaxpr/dot_general | solution.py:31
  122.8 2.3 %fusion.100 = bf16[896,5,128]{2,0,1:T(8,128)(2,1)S(1)} fusion(bf16[896,5,128]{2,0,1:T(8,128)(2,1)S(1)} %get-tuple-element.668, s32[]{:T(128)} %get-tuple-element.667, f32[896,512]{0,1:T(8,128)S(1)} %get-tuple-element.619, f32[896]{0:T(1024)S(1)} %get-tuple-element.620, pred[512]{0:T(512)(128)(4,1)S(1)} %fusion.94, ...), kind=kOutput, calls=%fused_computation.43.clone.1 | convolution fusion | flops 120422400 | bytes 2673152 | tf_op jit(solution)/shard_map/while/body/eval_jaxpr/dot_general | solution.py:31
  126.8 2.3 %fusion.100 = bf16[896,5,128]{2,0,1:T(8,128)(2,1)S(1)} fusion(bf16[896,5,128]{2,0,1:T(8,128)(2,1)S(1)} %get-tuple-element.668, s32[]{:T(128)} %get-tuple-element.667, f32[896,512]{0,1:T(8,128)S(1)} %get-tuple-element.619, f32[896]{0:T(1024)S(1)} %get-tuple-element.620, pred[512]{0:T(512)(128)(4,1)S(1)} %fusion.94, ...), kind=kOutput, calls=%fused_computation.43.clone.1 | convolution fusion | flops 120422400 | bytes 2673152 | tf_op jit(solution)/shard_map/while/body/eval_jaxpr/dot_general | solution.py:31
  131.4 38.1 %all_to_all.73 = bf16[8,112,640]{2,1,0:T(8,128)(2,1)S(1)} all-to-all(bf16[8,112,640]{2,1,0:T(8,128)(2,1)S(1)} %reshape.58), channel_id=1, replica_groups=mesh['stretch'=32,'head'=8,'cfg'=2] {'head'}, dimensions={0} | all-to-all | bytes 2293760 | tf_op jit(solution)/shard_map/all_to_all | solution.py:120
  (96 shorter events, 40.3 us)
Async XLA Ops:
  0.0 8.2 %copy-start = (bf16[112,5120]{1,0:T(8,128)(2,1)S(1)}, bf16[112,5120]{1,0:T(8,128)(2,1)}, u32[]{:S(2)}) copy-start(bf16[112,5120]{1,0:T(8,128)(2,1)} %param.11) | copy-start | bytes 3440644
  2.5 21.3 %all-to-all-start.1 = ((bf16[112,8,640]{2,0,1:T(8,128)(2,1)}), bf16[112,8,640]{2,0,1:T(8,128)(2,1)S(1)}, u32[]{:S(2)}, u32[]{:S(2)}) async-start(bf16[112,8,640]{2,0,1:T(8,128)(2,1)} %bitcast.64), calls=%async_computation.1 | async-start | bytes 2293760 | tf_op jit(solution)/shard_map/all_to_all | solution.py:101
  9.3 19.2 %copy-start.1 = (bf16[112,5120]{1,0:T(8,128)(2,1)S(1)}, bf16[112,5120]{1,0:T(8,128)(2,1)}, u32[]{:S(2)}) copy-start(bf16[112,5120]{1,0:T(8,128)(2,1)} %param.9) | copy-start | bytes 3440644
  23.8 19.7 %all-to-all-start.2 = ((bf16[112,8,640]{2,0,1:T(8,128)(2,1)}), bf16[112,8,640]{2,0,1:T(8,128)(2,1)S(1)}, u32[]{:S(2)}, u32[]{:S(2)}) async-start(bf16[112,8,640]{2,0,1:T(8,128)(2,1)} %bitcast.63), calls=%async_computation.2 | async-start | bytes 2293760 | tf_op jit(solution)/shard_map/all_to_all | solution.py:102
  28.5 19.6 %copy-start.3 = (s32[32]{0:T(128)S(1)}, s32[32]{0:T(128)}, u32[]{:S(2)}) copy-start(s32[32]{0:T(128)} %param.12) | copy-start | bytes 388
  28.5 20.8 %copy-start.4 = (s32[32]{0:T(128)S(1)}, s32[32]{0:T(128)}, u32[]{:S(2)}) copy-start(s32[32]{0:T(128)} %param.13) | copy-start | bytes 388
  43.5 19.3 %all-to-all-start = ((bf16[112,8,640]{2,0,1:T(8,128)(2,1)}), bf16[112,8,640]{2,0,1:T(8,128)(2,1)S(1)}, u32[]{:S(2)}, u32[]{:S(2)}) async-start(bf16[112,8,640]{2,0,1:T(8,128)(2,1)} %bitcast.65), calls=%async_computation | async-start | bytes 2293760 | tf_op jit(solution)/shard_map/all_to_all | solution.py:100
  51.4 44.3 %collective-permute-start = (bf16[512,640]{1,0:T(8,128)(2,1)}, bf16[512,640]{1,0:T(8,128)(2,1)}, u32[]{:S(2)}, u32[]{:S(2)}) collective-permute-start(bf16[512,640]{1,0:T(8,128)(2,1)} %constant_dynamic-slice_fusion.1), channel_id=1, source_target_pairs={{0,16},{16,32},{32,48},{48,64},{64,80},{80,96},{96,112},{112,128},... | collective-permute-start | bytes 1966088 | tf_op jit(solution)/shard_map/ppermute | solution.py:19
  56.6 50.2 %collective-permute-start.1 = (bf16[512,640]{1,0:T(8,128)(2,1)}, bf16[512,640]{1,0:T(8,128)(2,1)}, u32[]{:S(2)}, u32[]{:S(2)}) collective-permute-start(bf16[512,640]{1,0:T(8,128)(2,1)} %constant_dynamic-slice_fusion.2), channel_id=1, source_target_pairs={{0,16},{16,32},{32,48},{48,64},{64,80},{80,96},{96,112},{112,128},... | collective-permute-start | bytes 1966088 | tf_op jit(solution)/shard_map/ppermute | solution.py:19
  95.7 13.2 %copy-start.2 = (bf16[896,5,128]{2,0,1:T(8,128)(2,1)S(1)}, bf16[896,5,128]{2,0,1:T(8,128)(2,1)}, u32[]{:S(2)}) copy-start(bf16[896,5,128]{2,0,1:T(8,128)(2,1)} %custom-call.3) | copy-start | bytes 3440644
where the time goes:
time: 171 us
  waiting for transfers between devices  39.8 us (23%)
  blocking collectives  38.1 us (22%)
  local copies, waits for them, and re-layouts  27.3 us (16%)
  matrix products  27 us (16%)
  starting transfers between devices  23.6 us (14%)
  other arithmetic  12.9 us (8%)
    all_to_all x1, blocking collectives, body(): lax.all_to_all(mixed.reshape(span, local), 'head', split_axis=0, concat_a...  38.1 us
    dot_general x10, matrix products, head_block(): jnp.dot(weights.astype(jnp.bfloat16), v_head, preferred_element_type=jnp....  21.2 us
    all_to_all x1, waiting for transfers between devices, body(): lax.all_to_all(keys, 'head', split_axis=1, concat_axis=0, tiled=True)  14.5 us
    all_to_all x1, waiting for transfers between devices, body(): lax.all_to_all(values, 'head', split_axis=1, concat_axis=0, tiled=True)  13.9 us
    ppermute x2, waiting for transfers between devices, from_behind(): return lax.ppermute(shard, axis, pairs)  9.62 us
    ppermute x2, starting transfers between devices, from_behind(): return lax.ppermute(shard, axis, pairs)  8.54 us
    reduce_sum x10, other arithmetic, head_block(): total = jnp.sum(weights, axis=1)  6.67 us
    lt x10, other arithmetic, body(): live = spot < count_own  5.8 us
  transfers between devices with their start and end apart: 5, of which 4 were waited for; matrix products, arithmetic and copies ran while one was open for 23% of the time, Pallas kernels for 0%

commit v1 on v0

v1 whole, which is shorter than its diff:
```python
import functools
import math

import jax
import jax.numpy as jnp
from jax import lax
from jax.experimental import pallas as pl
from jax.experimental.pallas import tpu as pltpu
from jax.sharding import PartitionSpec as P

HD = 128
FT = 128
MOT_CAP = 4

NEG = -1e30
TQ = 448


def from_behind(shard, axis, by):
    size = lax.axis_size(axis)
    pairs = [(i, i + by) for i in range(size) if 0 <= i + by < size]
    return lax.ppermute(shard, axis, pairs)


def softmax_part(q, k, v, live):
    scores = lax.dot_general(
        q, k, (((1,), (1,)), ((), ())), preferred_element_type=jnp.float32
    )
    scores = scores * (1.0 / math.sqrt(HD))
    masked = jnp.where(live, scores, NEG)
    top = jnp.max(masked, axis=1, keepdims=True)
    weights = jnp.where(live, jnp.exp(masked - top), 0.0)
    total = jnp.sum(weights, axis=1, keepdims=True)
    acc = jnp.dot(weights.astype(jnp.bfloat16), v, preferred_element_type=jnp.float32)
    return top, total, acc


def attend_kernel(counts, q_ref, k_ref, v_ref, mk_ref, mv_ref, o_ref):
    own_live = counts[0] * FT
    mot_start = (MOT_CAP - counts[1]) * FT
    row0 = pl.program_id(1) * TQ
    q = q_ref[...]
    span = k_ref.shape[0]
    tail = mk_ref.shape[0]
    key_live = lax.broadcasted_iota(jnp.int32, (1, span), 1) < own_live
    slot_live = lax.broadcasted_iota(jnp.int32, (1, tail), 1) >= mot_start
    top_own, total_own, acc_own = softmax_part(q, k_ref[...], v_ref[...], key_live)
    top_mot, total_mot, acc_mot = softmax_part(q, mk_ref[...], mv_ref[...], slot_live)
    peak = jnp.maximum(top_own, top_mot)
    factor_own = jnp.exp(top_own - peak)
    factor_mot = jnp.exp(top_mot - peak)
    mixed = (acc_own * factor_own + acc_mot * factor_mot) / (
        total_own * factor_own + total_mot * factor_mot
    )
    rows = row0 + lax.broadcasted_iota(jnp.int32, (TQ, 1), 0)
    o_ref[...] = jnp.where(rows < own_live, mixed, 0.0).astype(o_ref.dtype)


def attend(counts, q, k, v, mk, mv):
    span, local = q.shape
    tail = mk.shape[0]
    heads = local // HD
    grid = (heads, span // TQ)
    flops = heads * 4 * span * (span + tail) * HD
    cost = pl.CostEstimate(
        flops=flops,
        transcendentals=heads * span * (span + tail),
        bytes_accessed=(4 * span + 2 * tail) * local * 2,
    )
    return pl.pallas_call(
        attend_kernel,
        out_shape=jax.ShapeDtypeStruct((span, local), jnp.bfloat16),
        grid_spec=pltpu.PrefetchScalarGridSpec(
            num_scalar_prefetch=1,
            grid=grid,
            in_specs=[
                pl.BlockSpec((TQ, HD), lambda h, i, c: (i, h)),
                pl.BlockSpec((span, HD), lambda h, i, c: (0, h)),
                pl.BlockSpec((span, HD), lambda h, i, c: (0, h)),
                pl.BlockSpec((tail, HD), lambda h, i, c: (0, h)),
                pl.BlockSpec((tail, HD), lambda h, i, c: (0, h)),
            ],
            out_specs=pl.BlockSpec((TQ, HD), lambda h, i, c: (i, h)),
        ),
        compiler_params=pltpu.CompilerParams(
            dimension_semantics=("arbitrary", "arbitrary"),
        ),
        cost_estimate=cost,
    )(counts, q, k, v, mk, mv)


def body(queries, keys, values, frames, motion):
    stretch_index = lax.axis_index("stretch")
    tail = MOT_CAP * FT
    count_own = frames[stretch_index]
    counts = jnp.stack([count_own, motion[stretch_index]]).astype(jnp.int32)
    tail_begin = (count_own - MOT_CAP) * FT
    k_heads = lax.all_to_all(keys, "head", split_axis=1, concat_axis=0, tiled=True)
    v_heads = lax.all_to_all(values, "head", split_axis=1, concat_axis=0, tiled=True)
    k_tail = lax.dynamic_slice_in_dim(k_heads, tail_begin, tail, 0)
    v_tail = lax.dynamic_slice_in_dim(v_heads, tail_begin, tail, 0)
    k_prior, v_prior = from_behind((k_tail, v_tail), "stretch", 1)
    q_heads = lax.all_to_all(queries, "head", split_axis=1, concat_axis=0, tiled=True)
    mixed = attend(counts, q_heads, k_heads, v_heads, k_prior, v_prior)
    return lax.all_to_all(mixed, "head", split_axis=0, concat_axis=1, tiled=True)


def solution(mesh):
    placed = (
        P(("cfg", "stretch", "head"), None),
        P(("cfg", "stretch", "head"), None),
        P(("cfg", "stretch", "head"), None),
        P(),
        P(),
    )
    return jax.shard_map(
        body,
        mesh=mesh,
        in_specs=placed,
        out_specs=P(("cfg", "stretch", "head"), None),
        check_vma=False,
    )
```

time: 171 us -> 165 us (0.965)
  waiting for transfers between devices: 39.8 us -> 69.9 us
  matrix products: 27 us -> 0 us
  local copies, waits for them, and re-layouts: 27.3 us -> 8.76 us
  Pallas kernels: 0 us -> 17.5 us
  other arithmetic: 12.9 us -> 1.79 us
  blocking collectives: 38.1 us -> 42.1 us
    ppermute x2, waiting for transfers between devices: 9.62 us -> 40.1 us  [from_behind(): return lax.ppermute(shard, axis, pairs)]
    dot_general x20 -> x0, matrix products: 27 us -> none  [the longest x10 21.2 us: head_block(): jnp.dot(weights.astype(jnp.bfloat16), v_head, preferred_element_type=jnp....]
    pallas_call x0 -> x1, Pallas kernels: none -> 17.5 us  [attend(): pl.pallas_call(attend_kernel, out_shape=jax.ShapeDtypeStruct((span, local...]
    reshape x3 -> x0, local copies, waits for them, and re-layouts: 6.69 us -> none  [the longest x1 2.24 us: body(): k_heads.reshape(span, count, HD)]
    reduce_sum x10 -> x0, other arithmetic: 6.67 us -> none  [head_block(): total = jnp.sum(weights, axis=1)]
    lt x10 -> x0, other arithmetic: 5.8 us -> none  [body(): live = spot < count_own]
    unnamed x13 -> x16, local copies, waits for them, and re-layouts: 4.99 us -> 0.87 us
    all_to_all x1, blocking collectives: 38.1 us -> 42.1 us  [body(): lax.all_to_all(mixed, 'head', split_axis=0, concat_axis=1, tiled=True)]
  transfers between devices with their start and end apart: 5 -> 5, of which waited for: 4 -> 5; matrix products, arithmetic and copies ran while one was open for 23% -> 4% of each run, Pallas kernels for 0% -> 0%
where the time goes in v1:
time: 165 us
  waiting for transfers between devices  69.9 us (42%)
  blocking collectives  42.1 us (26%)
  starting transfers between devices  24 us (15%)
  Pallas kernels  17.5 us (11%)
  local copies, waits for them, and re-layouts  8.76 us (5%)
  other arithmetic  1.79 us (1%)
    all_to_all x1, blocking collectives, body(): lax.all_to_all(mixed, 'head', split_axis=0, concat_axis=1, tiled=True)  42.1 us
    ppermute x2, waiting for transfers between devices, from_behind(): return lax.ppermute(shard, axis, pairs)  40.1 us
    pallas_call x1, Pallas kernels, attend(): pl.pallas_call(attend_kernel, out_shape=jax.ShapeDtypeStruct((span, local...  17.5 us
    all_to_all x1, waiting for transfers between devices, body(): lax.all_to_all(keys, 'head', split_axis=1, concat_axis=0, tiled=True)  14.5 us
    all_to_all x1, waiting for transfers between devices, body(): lax.all_to_all(values, 'head', split_axis=1, concat_axis=0, tiled=True)  13.9 us
    ppermute x2, starting transfers between devices, from_behind(): return lax.ppermute(shard, axis, pairs)  8.55 us
    all_to_all x1, starting transfers between devices, body(): lax.all_to_all(keys, 'head', split_axis=1, concat_axis=0, tiled=True)  5.89 us
    all_to_all x1, starting transfers between devices, body(): lax.all_to_all(values, 'head', split_axis=1, concat_axis=0, tiled=True)  4.81 us
  transfers between devices with their start and end apart: 5, of which 5 were waited for; matrix products, arithmetic and copies ran while one was open for 4% of the time, Pallas kernels for 0%

profile of v1, /device:TPU:56, one launch (start us, length us, event | category | flops | bytes accessed | tf_op | source)
XLA Modules:
  0.0 164.8 jit_solution(641931409953679657)
XLA Ops:
  0.0 2.4 %copy.18 = bf16[14,8,8,640]{3,2,0,1:T(8,128)(2,1)} copy(bf16[14,8,8,640]{3,2,1,0:T(8,128)(2,1)} %bitcast.31) | data formatting | bytes 2293760 | tf_op jit(solution)/shard_map/all_to_all | solution.py:98
  2.4 5.9 %all-to-all-start.1 = ((bf16[112,8,640]{2,0,1:T(8,128)(2,1)}), bf16[112,8,640]{2,0,1:T(8,128)(2,1)S(1)}, u32[]{:S(2)}, u32[]{:S(2)}) async-start(bf16[112,8,640]{2,0,1:T(8,128)(2,1)} %bitcast.24), calls=%async_computation.1 | async-start | bytes 2293760 | tf_op jit(solution)/shard_map/all_to_all | solution.py:98
  8.3 1.1 copy.17
  9.4 14.5 %all-to-all-done.1 = bf16[112,8,640]{2,0,1:T(8,128)(2,1)S(1)} async-done(((bf16[112,8,640]{2,0,1:T(8,128)(2,1)}), bf16[112,8,640]{2,0,1:T(8,128)(2,1)S(1)}, u32[]{:S(2)}, u32[]{:S(2)}) %all-to-all-start.1) | async-done | bytes 1146912 | tf_op jit(solution)/shard_map/all_to_all | solution.py:98
  23.8 4.8 %all-to-all-start.2 = ((bf16[112,8,640]{2,0,1:T(8,128)(2,1)}), bf16[112,8,640]{2,0,1:T(8,128)(2,1)S(1)}, u32[]{:S(2)}, u32[]{:S(2)}) async-start(bf16[112,8,640]{2,0,1:T(8,128)(2,1)} %bitcast.23), calls=%async_computation.2 | async-start | bytes 2293760 | tf_op jit(solution)/shard_map/all_to_all | solution.py:99
  28.7 1.1 copy.19
  29.8 13.9 %all-to-all-done.2 = bf16[112,8,640]{2,0,1:T(8,128)(2,1)S(1)} async-done(((bf16[112,8,640]{2,0,1:T(8,128)(2,1)}), bf16[112,8,640]{2,0,1:T(8,128)(2,1)S(1)}, u32[]{:S(2)}, u32[]{:S(2)}) %all-to-all-start.2) | async-done | bytes 1146912 | tf_op jit(solution)/shard_map/all_to_all | solution.py:99
  43.7 4.8 %all-to-all-start = ((bf16[112,8,640]{2,0,1:T(8,128)(2,1)}), bf16[112,8,640]{2,0,1:T(8,128)(2,1)S(1)}, u32[]{:S(2)}, u32[]{:S(2)}) async-start(bf16[112,8,640]{2,0,1:T(8,128)(2,1)} %bitcast.25), calls=%async_computation | async-start | bytes 2293760 | tf_op jit(solution)/shard_map/all_to_all | solution.py:103
  48.4 0.6 dynamic_slice.12
  49.5 0.0 copy-start.7
  49.6 0.9 constant_dynamic-slice_fusion.1
  50.5 4.3 %collective-permute-start = (bf16[512,640]{1,0:T(8,128)(2,1)}, bf16[512,640]{1,0:T(8,128)(2,1)}, u32[]{:S(2)}, u32[]{:S(2)}) collective-permute-start(bf16[512,640]{1,0:T(8,128)(2,1)} %constant_dynamic-slice_fusion.1), channel_id=1, source_target_pairs={{0,16},{16,32},{32,48},{48,64},{64,80},{80,96},{96,112},{112,128},... | collective-permute-start | bytes 1966088 | tf_op jit(solution)/shard_map/ppermute | solution.py:22
  54.8 0.1 constant_dynamic-slice_fusion
  54.8 4.3 %collective-permute-start.1 = (bf16[512,640]{1,0:T(8,128)(2,1)S(1)}, bf16[512,640]{1,0:T(8,128)(2,1)S(1)}, u32[]{:S(2)}, u32[]{:S(2)}) collective-permute-start(bf16[512,640]{1,0:T(8,128)(2,1)S(1)} %constant_dynamic-slice_fusion), channel_id=1, source_target_pairs={{0,16},{16,32},{32,48},{48,64},{64,80},{80,96},{96,112},{112,128},... | collective-permute-start | bytes 1966088 | tf_op jit(solution)/shard_map/ppermute | solution.py:22
  59.1 0.7 dynamic_slice.13
  59.8 1.8 %pad_add_fusion.counts = s32[2]{0:T(128)} fusion(s32[1]{0:T(128)} %dynamic_slice.13, s32[1]{0:T(128)} %dynamic_slice.12), kind=kLoop, calls=%fused_computation.3 | loop fusion | flops 2 | bytes 16 | tf_op jit(solution)/shard_map/stack | solution.py:96
  61.6 1.5 all-to-all-done
  63.1 15.9 %collective-permute-done.mk_ref = bf16[512,640]{1,0:T(8,128)(2,1)} collective-permute-done((bf16[512,640]{1,0:T(8,128)(2,1)}, bf16[512,640]{1,0:T(8,128)(2,1)}, u32[]{:S(2)}, u32[]{:S(2)}) %collective-permute-start) | collective-permute-done | bytes 655392 | tf_op jit(solution)/shard_map/ppermute | solution.py:22
  78.9 24.2 %collective-permute-done.1.mv_ref = bf16[512,640]{1,0:T(8,128)(2,1)S(1)} collective-permute-done((bf16[512,640]{1,0:T(8,128)(2,1)S(1)}, bf16[512,640]{1,0:T(8,128)(2,1)S(1)}, u32[]{:S(2)}, u32[]{:S(2)}) %collective-permute-start.1) | collective-permute-done | bytes 655392 | tf_op jit(solution)/shard_map/ppermute | solution.py:22
  103.1 0.0 copy-done.4
  103.1 0.8 copy-done.5
  104.0 17.5 %shard_map.55 = bf16[896,640]{1,0:T(8,128)(2,1)} custom-call(s32[2]{0:T(128)} %pad_add_fusion.counts, bf16[896,640]{1,0:T(8,128)(2,1)} %bitcast.34, bf16[896,640]{1,0:T(8,128)(2,1)} %bitcast.28, bf16[896,640]{1,0:T(8,128)(2,1)} %bitcast.30, bf16[512,640]{1,0:T(8,128)(2,1)} %collective-permute-done.mk_ref, bf16[512,640]{1,0:T(8,128)(2,1)} %copy-done.5), custom_call_target="tpu_custom_call" | custom-call | flops 3229614080 | bytes 5898240 | tf_op jit(solution)/shard_map/pallas_call | solution.py:70
  121.5 42.1 %all_to_all.76 = bf16[8,112,640]{2,1,0:T(8,128)(2,1)S(1)} all-to-all(bf16[8,112,640]{2,1,0:T(8,128)(2,1)} %bitcast.35), channel_id=1, replica_groups=mesh['stretch'=32,'head'=8,'cfg'=2] {'head'}, dimensions={0} | all-to-all | bytes 2293760 | tf_op jit(solution)/shard_map/all_to_all | solution.py:105
  163.6 1.2 copy.13
  (13 shorter events, 0.0 us)
Async XLA Ops:
  2.4 5.9 %copy-start.2 = (bf16[112,5120]{1,0:T(8,128)(2,1)S(1)}, bf16[112,5120]{1,0:T(8,128)(2,1)}, u32[]{:S(2)}) copy-start(bf16[112,5120]{1,0:T(8,128)(2,1)} %param.7) | copy-start | bytes 3440644
  2.4 21.5 %all-to-all-start.1 = ((bf16[112,8,640]{2,0,1:T(8,128)(2,1)}), bf16[112,8,640]{2,0,1:T(8,128)(2,1)S(1)}, u32[]{:S(2)}, u32[]{:S(2)}) async-start(bf16[112,8,640]{2,0,1:T(8,128)(2,1)} %bitcast.24), calls=%async_computation.1 | async-start | bytes 2293760 | tf_op jit(solution)/shard_map/all_to_all | solution.py:98
  23.8 25.7 %copy-start = (bf16[112,8,640]{2,0,1:T(8,128)(2,1)}, bf16[112,8,640]{2,0,1:T(8,128)(2,1)S(1)}, u32[]{:S(2)}) copy-start(bf16[112,8,640]{2,0,1:T(8,128)(2,1)S(1)} %all-to-all-done.1) | copy-start | bytes 3440644
  23.8 4.8 %copy-start.3 = (bf16[112,5120]{1,0:T(8,128)(2,1)S(1)}, bf16[112,5120]{1,0:T(8,128)(2,1)}, u32[]{:S(2)}) copy-start(bf16[112,5120]{1,0:T(8,128)(2,1)} %param.5) | copy-start | bytes 3440644
  23.8 19.8 %all-to-all-start.2 = ((bf16[112,8,640]{2,0,1:T(8,128)(2,1)}), bf16[112,8,640]{2,0,1:T(8,128)(2,1)S(1)}, u32[]{:S(2)}, u32[]{:S(2)}) async-start(bf16[112,8,640]{2,0,1:T(8,128)(2,1)} %bitcast.23), calls=%async_computation.2 | async-start | bytes 2293760 | tf_op jit(solution)/shard_map/all_to_all | solution.py:99
  43.6 11.1 %copy-start.1 = (bf16[112,8,640]{2,0,1:T(8,128)(2,1)}, bf16[112,8,640]{2,0,1:T(8,128)(2,1)S(1)}, u32[]{:S(2)}) copy-start(bf16[112,8,640]{2,0,1:T(8,128)(2,1)S(1)} %all-to-all-done.2) | copy-start | bytes 3440644
  43.6 4.8 %copy-start.6 = (s32[32]{0:T(128)S(1)}, s32[32]{0:T(128)}, u32[]{:S(2)}) copy-start(s32[32]{0:T(128)} %param.8) | copy-start | bytes 388
  43.7 19.4 %all-to-all-start = ((bf16[112,8,640]{2,0,1:T(8,128)(2,1)}), bf16[112,8,640]{2,0,1:T(8,128)(2,1)S(1)}, u32[]{:S(2)}, u32[]{:S(2)}) async-start(bf16[112,8,640]{2,0,1:T(8,128)(2,1)} %bitcast.25), calls=%async_computation | async-start | bytes 2293760 | tf_op jit(solution)/shard_map/all_to_all | solution.py:103
  49.5 9.6 %copy-start.7 = (s32[32]{0:T(128)S(1)}, s32[32]{0:T(128)}, u32[]{:S(2)}) copy-start(s32[32]{0:T(128)} %param.9) | copy-start | bytes 388
  50.5 28.5 %collective-permute-start = (bf16[512,640]{1,0:T(8,128)(2,1)}, bf16[512,640]{1,0:T(8,128)(2,1)}, u32[]{:S(2)}, u32[]{:S(2)}) collective-permute-start(bf16[512,640]{1,0:T(8,128)(2,1)} %constant_dynamic-slice_fusion.1), channel_id=1, source_target_pairs={{0,16},{16,32},{32,48},{48,64},{64,80},{80,96},{96,112},{112,128},... | collective-permute-start | bytes 1966088 | tf_op jit(solution)/shard_map/ppermute | solution.py:22
  54.8 48.3 %collective-permute-start.1 = (bf16[512,640]{1,0:T(8,128)(2,1)S(1)}, bf16[512,640]{1,0:T(8,128)(2,1)S(1)}, u32[]{:S(2)}, u32[]{:S(2)}) collective-permute-start(bf16[512,640]{1,0:T(8,128)(2,1)S(1)} %constant_dynamic-slice_fusion), channel_id=1, source_target_pairs={{0,16},{16,32},{32,48},{48,64},{64,80},{80,96},{96,112},{112,128},... | collective-permute-start | bytes 1966088 | tf_op jit(solution)/shard_map/ppermute | solution.py:22
  63.1 40.1 %copy-start.4 = (bf16[112,8,640]{2,0,1:T(8,128)(2,1)}, bf16[112,8,640]{2,0,1:T(8,128)(2,1)S(1)}, u32[]{:S(2)}) copy-start(bf16[112,8,640]{2,0,1:T(8,128)(2,1)S(1)} %all-to-all-done) | copy-start | bytes 3440644
  103.1 0.8 copy-start.5

commit v2 on v1

v2 whole, which is shorter than its diff:
```python
import math

import jax
import jax.numpy as jnp
from jax import lax
from jax.experimental import pallas as pl
from jax.experimental.pallas import tpu as pltpu
from jax.sharding import PartitionSpec as P

HD = 128
FT = 128
MOT_CAP = 4

NEG = -1e30
TQ = 448


def from_behind(shard, axis, by):
    size = lax.axis_size(axis)
    pairs = [(i, i + by) for i in range(size) if 0 <= i + by < size]
    return lax.ppermute(shard, axis, pairs)


def softmax_part(q, k, v, live):
    scores = lax.dot_general(
        q, k, (((1,), (1,)), ((), ())), preferred_element_type=jnp.float32
    )
    scores = scores * (1.0 / math.sqrt(HD))
    masked = jnp.where(live, scores, NEG)
    top = jnp.max(masked, axis=1, keepdims=True)
    weights = jnp.exp(masked - top)
    total = jnp.sum(weights, axis=1, keepdims=True)
    acc = jnp.dot(weights.astype(jnp.bfloat16), v, preferred_element_type=jnp.float32)
    return top, total, acc


def own_kernel(counts, q_ref, k_ref, v_ref, acc_ref, top_ref, tot_ref):
    own_live = counts[0] * FT
    span = k_ref.shape[0]
    key_live = lax.broadcasted_iota(jnp.int32, (1, span), 1) < own_live
    top, total, acc = softmax_part(q_ref[...], k_ref[...], v_ref[...], key_live)
    acc_ref[...] = acc
    top_ref[...] = jnp.broadcast_to(top, top_ref.shape)
    tot_ref[...] = jnp.broadcast_to(total, tot_ref.shape)


def finish_kernel(counts, q_ref, mk_ref, mv_ref, acc_ref, top_ref, tot_ref, o_ref):
    own_live = counts[0] * FT
    mot_start = (MOT_CAP - counts[1]) * FT
    tail = mk_ref.shape[0]
    slot_live = lax.broadcasted_iota(jnp.int32, (1, tail), 1) >= mot_start
    top_mot, total_mot, acc_mot = softmax_part(
        q_ref[...], mk_ref[...], mv_ref[...], slot_live
    )
    top_own = top_ref[:, 0:1]
    total_own = tot_ref[:, 0:1]
    peak = jnp.maximum(top_own, top_mot)
    factor_own = jnp.exp(top_own - peak)
    factor_mot = jnp.exp(top_mot - peak)
    mixed = (acc_ref[...] * factor_own + acc_mot * factor_mot) / (
        total_own * factor_own + total_mot * factor_mot
    )
    rows = pl.program_id(1) * TQ + lax.broadcasted_iota(jnp.int32, (TQ, 1), 0)
    o_ref[...] = jnp.where(rows < own_live, mixed, 0.0).astype(o_ref.dtype)


def row_block(h, i, c):
    return (i, h)


def own_part(counts, q, kv):
    span, local = q.shape
    heads = local // HD
    part = jax.ShapeDtypeStruct((span, local), jnp.float32)
    cost = pl.CostEstimate(
        flops=heads * 4 * span * span * HD,
        transcendentals=heads * span * span,
        bytes_accessed=3 * span * local * 2 + 3 * span * local * 4,
    )
    return pl.pallas_call(
        own_kernel,
        out_shape=(part, part, part),
        grid_spec=pltpu.PrefetchScalarGridSpec(
            num_scalar_prefetch=1,
            grid=(heads, span // TQ),
            in_specs=[
                pl.BlockSpec((TQ, HD), row_block),
                pl.BlockSpec((None, span, HD), lambda h, i, c: (0, 0, h)),
                pl.BlockSpec((None, span, HD), lambda h, i, c: (1, 0, h)),
            ],
            out_specs=[pl.BlockSpec((TQ, HD), row_block)] * 3,
        ),
        compiler_params=pltpu.CompilerParams(
            dimension_semantics=("arbitrary", "arbitrary"),
        ),
        cost_estimate=cost,
    )(counts, q, kv, kv)


def finish_part(counts, q, kv_tail, acc, top, tot):
    span, local = q.shape
    tail = kv_tail.shape[1]
    heads = local // HD
    cost = pl.CostEstimate(
        flops=heads * 4 * span * tail * HD,
        transcendentals=heads * span * tail,
        bytes_accessed=2 * span * local * 2 + 2 * tail * local * 2 + 3 * span * local * 4,
    )
    return pl.pallas_call(
        finish_kernel,
        out_shape=jax.ShapeDtypeStruct((span, local), jnp.bfloat16),
        grid_spec=pltpu.PrefetchScalarGridSpec(
            num_scalar_prefetch=1,
            grid=(heads, span // TQ),
            in_specs=[
                pl.BlockSpec((TQ, HD), row_block),
                pl.BlockSpec((None, tail, HD), lambda h, i, c: (0, 0, h)),
                pl.BlockSpec((None, tail, HD), lambda h, i, c: (1, 0, h)),
                pl.BlockSpec((TQ, HD), row_block),
                pl.BlockSpec((TQ, HD), row_block),
                pl.BlockSpec((TQ, HD), row_block),
            ],
            out_specs=pl.BlockSpec((TQ, HD), row_block),
        ),
        compiler_params=pltpu.CompilerParams(
            dimension_semantics=("arbitrary", "arbitrary"),
        ),
        cost_estimate=cost,
    )(counts, q, kv_tail, kv_tail, acc, top, tot)


def body(queries, keys, values, frames, motion):
    stretch_index = lax.axis_index("stretch")
    tail = MOT_CAP * FT
    count_own = frames[stretch_index]
    counts = jnp.stack([count_own, motion[stretch_index]]).astype(jnp.int32)
    tail_begin = (count_own - MOT_CAP) * FT
    kv = jnp.stack([keys, values])
    kv_heads = lax.all_to_all(kv, "head", split_axis=2, concat_axis=1, tiled=True)
    kv_tail = lax.dynamic_slice_in_dim(kv_heads, tail_begin, tail, 1)
    kv_prior = from_behind(kv_tail, "stretch", 1)
    q_heads = lax.all_to_all(queries, "head", split_axis=1, concat_axis=0, tiled=True)
    acc, top, tot = own_part(counts, q_heads, kv_heads)
    mixed = finish_part(counts, q_heads, kv_prior, acc, top, tot)
    return lax.all_to_all(mixed, "head", split_axis=0, concat_axis=1, tiled=True)


def solution(mesh):
    placed = (
        P(("cfg", "stretch", "head"), None),
        P(("cfg", "stretch", "head"), None),
        P(("cfg", "stretch", "head"), None),
        P(),
        P(),
    )
    return jax.shard_map(
        body,
        mesh=mesh,
        in_specs=placed,
        out_specs=P(("cfg", "stretch", "head"), None),
        check_vma=False,
    )
```

time: 165 us -> 166 us (level)
  blocking collectives: 42.1 us -> 27.1 us
  Pallas kernels: 17.5 us -> 31.2 us
  starting transfers between devices: 24 us -> 15.4 us
  local copies, waits for them, and re-layouts: 8.76 us -> 16.6 us
  other arithmetic: 1.79 us -> 3.65 us
    all_to_all x1, blocking collectives: 42.1 us -> 27.1 us  [body(): lax.all_to_all(mixed, 'head', split_axis=0, concat_axis=1, tiled=True)]
    pallas_call x1 -> x2, Pallas kernels: 17.5 us -> 31.2 us  [the longest x1 17.2 us: finish_part(): pl.pallas_call(finish_kernel, out_shape=jax.ShapeDtypeStruct((span, local...]
    all_to_all x2 -> x1, starting transfers between devices: 10.7 us -> 5.76 us  [body(): lax.all_to_all(kv, 'head', split_axis=2, concat_axis=1, tiled=True)]
    another operation x0 -> x1, local copies, waits for them, and re-layouts: none -> 4.67 us  [body(): kv = jnp.stack([keys, values])]
    ppermute x2 -> x1, starting transfers between devices: 8.55 us -> 4.28 us  [from_behind(): return lax.ppermute(shard, axis, pairs)]
    another operation x0 -> x1, other arithmetic: none -> 1.81 us  [body(): kv = jnp.stack([keys, values])]
    all_to_all x2 -> x1, local copies, waits for them, and re-layouts: 3.46 us -> 4.72 us  [body(): lax.all_to_all(kv, 'head', split_axis=2, concat_axis=1, tiled=True)]
    ppermute x2 -> x1, waiting for transfers between devices: 40.1 us -> 41 us  [from_behind(): return lax.ppermute(shard, axis, pairs)]
  transfers between devices with their start and end apart: 5 -> 3, of which waited for: 5 -> 3; matrix products, arithmetic and copies ran while one was open for 4% -> 7% of each run, Pallas kernels for 0% -> 8%
where the time goes in v2:
time: 166 us; the launch traced here: 165 us
  waiting for transfers between devices  70.8 us (43%)
  Pallas kernels  31.2 us (19%)
  blocking collectives  27.1 us (16%)
  local copies, waits for them, and re-layouts  16.6 us (10%)
  starting transfers between devices  15.4 us (9%)
  other arithmetic  3.65 us (2%)
    ppermute x1, waiting for transfers between devices, from_behind(): return lax.ppermute(shard, axis, pairs)  41 us
    all_to_all x1, waiting for transfers between devices, body(): lax.all_to_all(kv, 'head', split_axis=2, concat_axis=1, tiled=True)  29 us
    all_to_all x1, blocking collectives, body(): lax.all_to_all(mixed, 'head', split_axis=0, concat_axis=1, tiled=True)  27.1 us
    pallas_call x1, Pallas kernels, finish_part(): pl.pallas_call(finish_kernel, out_shape=jax.ShapeDtypeStruct((span, local...  17.2 us
    pallas_call x1, Pallas kernels, own_part(): pl.pallas_call(own_kernel, out_shape=(part, part, part), grid_spec=pltpu....  14.1 us
    all_to_all x1, starting transfers between devices, body(): lax.all_to_all(kv, 'head', split_axis=2, concat_axis=1, tiled=True)  5.76 us
    all_to_all x1, starting transfers between devices, body(): lax.all_to_all(queries, 'head', split_axis=1, concat_axis=0, tiled=True)  5.34 us
    all_to_all x1, local copies, waits for them, and re-layouts, body(): lax.all_to_all(kv, 'head', split_axis=2, concat_axis=1, tiled=True)  4.72 us
  transfers between devices with their start and end apart: 3, of which 3 were waited for; matrix products, arithmetic and copies ran while one was open for 7% of the time, Pallas kernels for 8%

profile of v2, /device:TPU:56, one launch (start us, length us, event | category | flops | bytes accessed | tf_op | source)
XLA Modules:
  0.0 165.4 jit_solution(6091542548108565612)
XLA Ops:
  0.0 1.8 %pad_maximum_fusion = bf16[2,112,5120]{2,1,0:T(8,128)(2,1)S(1)} fusion(bf16[1,112,5120]{2,1,0:T(8,128)(2,1)} %bitcast.25, bf16[1,112,5120]{2,1,0:T(8,128)(2,1)} %bitcast.26), kind=kLoop, calls=%fused_computation | loop fusion | flops 1146880 | bytes 4587520 | tf_op jit(solution)/shard_map/stack | solution.py:138
  1.8 4.7 %copy.15 = bf16[2,112,5120]{1,0,2:T(2,128)(2,1)} copy(bf16[2,112,5120]{2,1,0:T(8,128)(2,1)S(1)} %pad_maximum_fusion) | data formatting | bytes 4587520 | tf_op jit(solution)/shard_map/stack | solution.py:138
  6.5 5.8 %all-to-all-start.1 = ((bf16[2,112,5120]{1,0,2:T(2,128)(2,1)}), bf16[2,112,5120]{1,0,2:T(2,128)(2,1)S(1)}, u32[]{:S(2)}, u32[]{:S(2)}) async-start(bf16[2,112,5120]{1,0,2:T(2,128)(2,1)} %copy.15), calls=%async_computation.1 | async-start | bytes 5242880 | tf_op jit(solution)/shard_map/all_to_all | solution.py:139
  12.2 2.4 %copy.21 = bf16[14,8,8,640]{3,2,0,1:T(8,128)(2,1)} copy(bf16[14,8,8,640]{3,2,1,0:T(8,128)(2,1)} %bitcast.27) | data formatting | bytes 2293760 | tf_op jit(solution)/shard_map/all_to_all | solution.py:142
  14.6 0.0 copy-start.1
  14.6 29.0 %all-to-all-done.1 = bf16[2,112,5120]{1,0,2:T(2,128)(2,1)S(1)} async-done(((bf16[2,112,5120]{1,0,2:T(2,128)(2,1)}), bf16[2,112,5120]{1,0,2:T(2,128)(2,1)S(1)}, u32[]{:S(2)}, u32[]{:S(2)}) %all-to-all-start.1) | async-done | bytes 2293792 | tf_op jit(solution)/shard_map/all_to_all | solution.py:139
  43.6 5.3 %all-to-all-start = ((bf16[112,8,640]{2,0,1:T(8,128)(2,1)}), bf16[112,8,640]{2,0,1:T(8,128)(2,1)}, u32[]{:S(2)}, u32[]{:S(2)}) async-start(bf16[112,8,640]{2,0,1:T(8,128)(2,1)} %bitcast.23), calls=%async_computation | async-start | bytes 2293760 | tf_op jit(solution)/shard_map/all_to_all | solution.py:142
  49.0 0.0 copy-done.1
  49.0 0.6 dynamic_slice.9
  50.1 4.7 %copy.16 = bf16[2,112,8,640]{3,1,2,0:T(8,128)(2,1)} copy(bf16[2,112,8,640]{1,0,3,2:T(2,128)(2,1)S(1)} %bitcast.18) | data formatting | bytes 4587520 | tf_op jit(solution)/shard_map/all_to_all | solution.py:139
  54.8 0.0 copy-start.2
  54.8 1.4 constant_dynamic-slice_fusion
  56.3 4.3 %collective-permute-start = (bf16[2,512,640]{2,1,0:T(8,128)(2,1)S(1)}, bf16[2,512,640]{2,1,0:T(8,128)(2,1)S(1)}, u32[]{:S(2)}, u32[]{:S(2)}) collective-permute-start(bf16[2,512,640]{2,1,0:T(8,128)(2,1)S(1)} %constant_dynamic-slice_fusion), channel_id=1, source_target_pairs={{0,16},{16,32},{32,48},{48,64},{64,80},{80,96},{96,112},{112,128},... | collective-permute-start | bytes 3932168 | tf_op jit(solution)/shard_map/ppermute | solution.py:21
  60.6 0.0 copy-done.2
  60.6 0.7 dynamic_slice.10
  61.2 1.8 %pad_add_fusion.counts = s32[2]{0:T(128)} fusion(s32[1]{0:T(128)} %dynamic_slice.10, s32[1]{0:T(128)} %dynamic_slice.9), kind=kLoop, calls=%fused_computation.2 | loop fusion | flops 2 | bytes 16 | tf_op jit(solution)/shard_map/stack | solution.py:136
  63.1 0.8 all-to-all-done
  63.8 14.1 %shard_map.55 = (f32[896,640]{1,0:T(8,128)}, f32[896,640]{1,0:T(8,128)}, f32[896,640]{1,0:T(8,128)}) custom-call(s32[2]{0:T(128)} %pad_add_fusion.counts, bf16[896,640]{1,0:T(8,128)(2,1)} %bitcast.1.q_ref, bf16[2,896,640]{2,1,0:T(8,128)(2,1)} %bitcast.20, bf16[2,896,640]{2,1,0:T(8,128)(2,1)} %bitcast.21), custom_call_target="tpu_custom_call" | custom-call | flops 2055208960 | bytes 10321920 | tf_op jit(solution)/shard_map/pallas_call | solution.py:80
  77.9 41.0 %collective-permute-done.mk_ref.mv_ref = bf16[2,512,640]{2,1,0:T(8,128)(2,1)S(1)} collective-permute-done((bf16[2,512,640]{2,1,0:T(8,128)(2,1)S(1)}, bf16[2,512,640]{2,1,0:T(8,128)(2,1)S(1)}, u32[]{:S(2)}, u32[]{:S(2)}) %collective-permute-start) | collective-permute-done | bytes 1310752 | tf_op jit(solution)/shard_map/ppermute | solution.py:21
  118.9 0.0 copy-start
  118.9 1.1 copy-done
  120.0 17.2 %shard_map.56 = bf16[896,640]{1,0:T(8,128)(2,1)} custom-call(s32[2]{0:T(128)} %pad_add_fusion.counts, bf16[896,640]{1,0:T(8,128)(2,1)} %bitcast.1.q_ref, bf16[2,512,640]{2,1,0:T(8,128)(2,1)} %copy-done, bf16[2,512,640]{2,1,0:T(8,128)(2,1)} %copy-done, f32[896,640]{1,0:T(8,128)} %get-tuple-element.8.acc_ref, f32[896,640]{1,0:T(8,128)} %get-tuple-element.9.top_ref, ...), custom_call_target="tpu_custom_call" | custom-call | flops 1174405120 | bytes 10485760 | tf_op jit(solution)/shard_map/pallas_call | solution.py:109
  137.2 27.1 %all_to_all.56 = bf16[8,112,640]{2,1,0:T(8,128)(2,1)S(1)} all-to-all(bf16[8,112,640]{2,1,0:T(8,128)(2,1)} %bitcast.22), channel_id=1, replica_groups=mesh['stretch'=32,'head'=8,'cfg'=2] {'head'}, dimensions={0} | all-to-all | bytes 2293760 | tf_op jit(solution)/shard_map/all_to_all | solution.py:145
  164.2 1.2 copy.19
Async XLA Ops:
  6.5 37.1 %all-to-all-start.1 = ((bf16[2,112,5120]{1,0,2:T(2,128)(2,1)}), bf16[2,112,5120]{1,0,2:T(2,128)(2,1)S(1)}, u32[]{:S(2)}, u32[]{:S(2)}) async-start(bf16[2,112,5120]{1,0,2:T(2,128)(2,1)} %copy.15), calls=%async_computation.1 | async-start | bytes 5242880 | tf_op jit(solution)/shard_map/all_to_all | solution.py:139
  14.6 34.4 %copy-start.1 = (s32[32]{0:T(128)S(1)}, s32[32]{0:T(128)}, u32[]{:S(2)}) copy-start(s32[32]{0:T(128)} %param.8) | copy-start | bytes 388
  43.6 20.2 %all-to-all-start = ((bf16[112,8,640]{2,0,1:T(8,128)(2,1)}), bf16[112,8,640]{2,0,1:T(8,128)(2,1)}, u32[]{:S(2)}, u32[]{:S(2)}) async-start(bf16[112,8,640]{2,0,1:T(8,128)(2,1)} %bitcast.23), calls=%async_computation | async-start | bytes 2293760 | tf_op jit(solution)/shard_map/all_to_all | solution.py:142
  54.8 5.7 %copy-start.2 = (s32[32]{0:T(128)S(1)}, s32[32]{0:T(128)}, u32[]{:S(2)}) copy-start(s32[32]{0:T(128)} %param.9) | copy-start | bytes 388
  56.3 62.6 %collective-permute-start = (bf16[2,512,640]{2,1,0:T(8,128)(2,1)S(1)}, bf16[2,512,640]{2,1,0:T(8,128)(2,1)S(1)}, u32[]{:S(2)}, u32[]{:S(2)}) collective-permute-start(bf16[2,512,640]{2,1,0:T(8,128)(2,1)S(1)} %constant_dynamic-slice_fusion), channel_id=1, source_target_pairs={{0,16},{16,32},{32,48},{48,64},{64,80},{80,96},{96,112},{112,128},... | collective-permute-start | bytes 3932168 | tf_op jit(solution)/shard_map/ppermute | solution.py:21
  118.9 1.1 copy-start

commit v3 on v2

--- a/solution.py
+++ b/solution.py
@@ -28,10 +28,10 @@
     scores = scores * (1.0 / math.sqrt(HD))
     masked = jnp.where(live, scores, NEG)
     top = jnp.max(masked, axis=1, keepdims=True)
-    weights = jnp.exp(masked - top)
-    total = jnp.sum(weights, axis=1, keepdims=True)
-    acc = jnp.dot(weights.astype(jnp.bfloat16), v, preferred_element_type=jnp.float32)
-    return top, total, acc
+    weights = jnp.exp(masked - top).astype(jnp.bfloat16)
+    v_ext = jnp.concatenate([v, jnp.ones_like(v)], axis=1)
+    both = jnp.dot(weights, v_ext, preferred_element_type=jnp.float32)
+    return top, both[:, HD : HD + 1], both[:, :HD]
 
 
 def own_kernel(counts, q_ref, k_ref, v_ref, acc_ref, top_ref, tot_ref):
@@ -68,7 +68,7 @@
     return (i, h)
 
 
-def own_part(counts, q, kv):
+def own_part(counts, q, k, v):
     span, local = q.shape
     heads = local // HD
     part = jax.ShapeDtypeStruct((span, local), jnp.float32)
@@ -85,8 +85,8 @@
             grid=(heads, span // TQ),
             in_specs=[
                 pl.BlockSpec((TQ, HD), row_block),
-                pl.BlockSpec((None, span, HD), lambda h, i, c: (0, 0, h)),
-                pl.BlockSpec((None, span, HD), lambda h, i, c: (1, 0, h)),
+                pl.BlockSpec((span, HD), lambda h, i, c: (0, h)),
+                pl.BlockSpec((span, HD), lambda h, i, c: (0, h)),
             ],
             out_specs=[pl.BlockSpec((TQ, HD), row_block)] * 3,
         ),
@@ -94,12 +94,12 @@
             dimension_semantics=("arbitrary", "arbitrary"),
         ),
         cost_estimate=cost,
-    )(counts, q, kv, kv)
+    )(counts, q, k, v)
 
 
-def finish_part(counts, q, kv_tail, acc, top, tot):
+def finish_part(counts, q, mk, mv, acc, top, tot):
     span, local = q.shape
-    tail = kv_tail.shape[1]
+    tail = mk.shape[0]
     heads = local // HD
     cost = pl.CostEstimate(
         flops=heads * 4 * span * tail * HD,
@@ -114,8 +114,8 @@
             grid=(heads, span // TQ),
             in_specs=[
                 pl.BlockSpec((TQ, HD), row_block),
-                pl.BlockSpec((None, tail, HD), lambda h, i, c: (0, 0, h)),
-                pl.BlockSpec((None, tail, HD), lambda h, i, c: (1, 0, h)),
+                pl.BlockSpec((tail, HD), lambda h, i, c: (0, h)),
+                pl.BlockSpec((tail, HD), lambda h, i, c: (0, h)),
                 pl.BlockSpec((TQ, HD), row_block),
                 pl.BlockSpec((TQ, HD), row_block),
                 pl.BlockSpec((TQ, HD), row_block),
@@ -126,7 +126,7 @@
             dimension_semantics=("arbitrary", "arbitrary"),
         ),
         cost_estimate=cost,
-    )(counts, q, kv_tail, kv_tail, acc, top, tot)
+    )(counts, q, mk, mv, acc, top, tot)
 
 
 def body(queries, keys, values, frames, motion):
@@ -135,13 +135,15 @@
     count_own = frames[stretch_index]
     counts = jnp.stack([count_own, motion[stretch_index]]).astype(jnp.int32)
     tail_begin = (count_own - MOT_CAP) * FT
-    kv = jnp.stack([keys, values])
-    kv_heads = lax.all_to_all(kv, "head", split_axis=2, concat_axis=1, tiled=True)
-    kv_tail = lax.dynamic_slice_in_dim(kv_heads, tail_begin, tail, 1)
-    kv_prior = from_behind(kv_tail, "stretch", 1)
+    k_heads = lax.all_to_all(keys, "head", split_axis=1, concat_axis=0, tiled=True)
+    k_tail = lax.dynamic_slice_in_dim(k_heads, tail_begin, tail, 0)
+    k_prior = from_behind(k_tail, "stretch", 1)
+    v_heads = lax.all_to_all(values, "head", split_axis=1, concat_axis=0, tiled=True)
+    v_tail = lax.dynamic_slice_in_dim(v_heads, tail_begin, tail, 0)
+    v_prior = from_behind(v_tail, "stretch", 1)
     q_heads = lax.all_to_all(queries, "head", split_axis=1, concat_axis=0, tiled=True)
-    acc, top, tot = own_part(counts, q_heads, kv_heads)
-    mixed = finish_part(counts, q_heads, kv_prior, acc, top, tot)
+    acc, top, tot = own_part(counts, q_heads, k_heads, v_heads)
+    mixed = finish_part(counts, q_heads, k_prior, v_prior, acc, top, tot)
     return lax.all_to_all(mixed, "head", split_axis=0, concat_axis=1, tiled=True)
 
 

time: 166 us -> 161 us (0.970)
  waiting for transfers between devices: 70.8 us -> 55 us
  blocking collectives: 27.1 us -> 41.7 us
  starting transfers between devices: 15.4 us -> 24 us
  local copies, waits for them, and re-layouts: 16.6 us -> 9.82 us
  Pallas kernels: 31.2 us -> 27.2 us
  other arithmetic: 3.65 us -> 1.83 us
    ppermute x1 -> x2, waiting for transfers between devices: 41 us -> 25.3 us  [from_behind(): return lax.ppermute(shard, axis, pairs)]
    all_to_all x1, blocking collectives: 27.1 us -> 41.7 us  [body(): lax.all_to_all(mixed, 'head', split_axis=0, concat_axis=1, tiled=True)]
    all_to_all x1 -> x2, starting transfers between devices: 5.76 us -> 10.7 us  [the longest x1 5.89 us: body(): lax.all_to_all(keys, 'head', split_axis=1, concat_axis=0, tiled=True)]
    another operation x1 -> x0, local copies, waits for them, and re-layouts: 4.67 us -> none  [body(): kv = jnp.stack([keys, values])]
    ppermute x1 -> x2, starting transfers between devices: 4.28 us -> 8.55 us  [from_behind(): return lax.ppermute(shard, axis, pairs)]
    pallas_call x1, Pallas kernels: 17.2 us -> 13.1 us  [finish_part(): pl.pallas_call(finish_kernel, out_shape=jax.ShapeDtypeStruct((span, local...]
    another operation x1 -> x0, other arithmetic: 1.81 us -> none  [body(): kv = jnp.stack([keys, values])]
    all_to_all x1 -> x2, local copies, waits for them, and re-layouts: 4.72 us -> 3.49 us  [the longest x1 2.36 us: body(): lax.all_to_all(keys, 'head', split_axis=1, concat_axis=0, tiled=True)]
  transfers between devices with their start and end apart: 3 -> 5, of which waited for: 3 -> 5; matrix products, arithmetic and copies ran while one was open for 7% -> 4% of each run, Pallas kernels for 8% -> 9%
where the time goes in v3:
time: 161 us; the launch traced here: 160 us
  waiting for transfers between devices  55 us (34%)
  blocking collectives  41.7 us (26%)
  Pallas kernels  27.2 us (17%)
  starting transfers between devices  24 us (15%)
  local copies, waits for them, and re-layouts  9.82 us (6%)
  other arithmetic  1.83 us (1%)
    all_to_all x1, blocking collectives, body(): lax.all_to_all(mixed, 'head', split_axis=0, concat_axis=1, tiled=True)  41.7 us
    ppermute x2, waiting for transfers between devices, from_behind(): return lax.ppermute(shard, axis, pairs)  25.3 us
    all_to_all x1, waiting for transfers between devices, body(): lax.all_to_all(keys, 'head', split_axis=1, concat_axis=0, tiled=True)  14.5 us
    pallas_call x1, Pallas kernels, own_part(): pl.pallas_call(own_kernel, out_shape=(part, part, part), grid_spec=pltpu....  14.2 us
    all_to_all x1, waiting for transfers between devices, body(): lax.all_to_all(values, 'head', split_axis=1, concat_axis=0, tiled=True)  13.9 us
    pallas_call x1, Pallas kernels, finish_part(): pl.pallas_call(finish_kernel, out_shape=jax.ShapeDtypeStruct((span, local...  13.1 us
    ppermute x2, starting transfers between devices, from_behind(): return lax.ppermute(shard, axis, pairs)  8.55 us
    all_to_all x1, starting transfers between devices, body(): lax.all_to_all(keys, 'head', split_axis=1, concat_axis=0, tiled=True)  5.89 us
  transfers between devices with their start and end apart: 5, of which 5 were waited for; matrix products, arithmetic and copies ran while one was open for 4% of the time, Pallas kernels for 9%

profile of v3, /device:TPU:56, one launch (start us, length us, event | category | flops | bytes accessed | tf_op | source)
XLA Modules:
  0.0 160.3 jit_solution(6705215776138971533)
XLA Ops:
  0.0 2.4 %copy.18 = bf16[14,8,8,640]{3,2,0,1:T(8,128)(2,1)} copy(bf16[14,8,8,640]{3,2,1,0:T(8,128)(2,1)} %bitcast.34) | data formatting | bytes 2293760 | tf_op jit(solution)/shard_map/all_to_all | solution.py:138
  2.4 5.9 %all-to-all-start.1 = ((bf16[112,8,640]{2,0,1:T(8,128)(2,1)}), bf16[112,8,640]{2,0,1:T(8,128)(2,1)S(1)}, u32[]{:S(2)}, u32[]{:S(2)}) async-start(bf16[112,8,640]{2,0,1:T(8,128)(2,1)} %bitcast.24), calls=%async_computation.1 | async-start | bytes 2293760 | tf_op jit(solution)/shard_map/all_to_all | solution.py:138
  8.3 1.1 copy.17
  9.4 14.5 %all-to-all-done.1 = bf16[112,8,640]{2,0,1:T(8,128)(2,1)S(1)} async-done(((bf16[112,8,640]{2,0,1:T(8,128)(2,1)}), bf16[112,8,640]{2,0,1:T(8,128)(2,1)S(1)}, u32[]{:S(2)}, u32[]{:S(2)}) %all-to-all-start.1) | async-done | bytes 1146912 | tf_op jit(solution)/shard_map/all_to_all | solution.py:138
  23.8 4.8 %all-to-all-start.2 = ((bf16[112,8,640]{2,0,1:T(8,128)(2,1)}), bf16[112,8,640]{2,0,1:T(8,128)(2,1)S(1)}, u32[]{:S(2)}, u32[]{:S(2)}) async-start(bf16[112,8,640]{2,0,1:T(8,128)(2,1)} %bitcast.23), calls=%async_computation.2 | async-start | bytes 2293760 | tf_op jit(solution)/shard_map/all_to_all | solution.py:141
  28.7 1.1 copy.19
  29.8 13.9 %all-to-all-done.2 = bf16[112,8,640]{2,0,1:T(8,128)(2,1)S(1)} async-done(((bf16[112,8,640]{2,0,1:T(8,128)(2,1)}), bf16[112,8,640]{2,0,1:T(8,128)(2,1)S(1)}, u32[]{:S(2)}, u32[]{:S(2)}) %all-to-all-start.2) | async-done | bytes 1146912 | tf_op jit(solution)/shard_map/all_to_all | solution.py:141
  43.7 4.8 %all-to-all-start = ((bf16[112,8,640]{2,0,1:T(8,128)(2,1)}), bf16[112,8,640]{2,0,1:T(8,128)(2,1)S(1)}, u32[]{:S(2)}, u32[]{:S(2)}) async-start(bf16[112,8,640]{2,0,1:T(8,128)(2,1)} %bitcast.25), calls=%async_computation | async-start | bytes 2293760 | tf_op jit(solution)/shard_map/all_to_all | solution.py:144
  48.4 0.6 dynamic_slice.12
  49.7 0.9 constant_dynamic-slice_fusion.1
  50.6 4.3 %collective-permute-start = (bf16[512,640]{1,0:T(8,128)(2,1)}, bf16[512,640]{1,0:T(8,128)(2,1)}, u32[]{:S(2)}, u32[]{:S(2)}) collective-permute-start(bf16[512,640]{1,0:T(8,128)(2,1)} %constant_dynamic-slice_fusion.1), channel_id=1, source_target_pairs={{0,16},{16,32},{32,48},{48,64},{64,80},{80,96},{96,112},{112,128},... | collective-permute-start | bytes 1966088 | tf_op jit(solution)/shard_map/ppermute | solution.py:21
  54.9 0.1 constant_dynamic-slice_fusion
  55.0 4.3 %collective-permute-start.1 = (bf16[512,640]{1,0:T(8,128)(2,1)S(1)}, bf16[512,640]{1,0:T(8,128)(2,1)S(1)}, u32[]{:S(2)}, u32[]{:S(2)}) collective-permute-start(bf16[512,640]{1,0:T(8,128)(2,1)S(1)} %constant_dynamic-slice_fusion), channel_id=1, source_target_pairs={{0,16},{16,32},{32,48},{48,64},{64,80},{80,96},{96,112},{112,128},... | collective-permute-start | bytes 1966088 | tf_op jit(solution)/shard_map/ppermute | solution.py:21
  59.3 0.6 dynamic_slice.13
  59.8 1.8 %pad_add_fusion.counts = s32[2]{0:T(128)} fusion(s32[1]{0:T(128)} %dynamic_slice.13, s32[1]{0:T(128)} %dynamic_slice.12), kind=kLoop, calls=%fused_computation.3 | loop fusion | flops 2 | bytes 16 | tf_op jit(solution)/shard_map/stack | solution.py:136
  61.7 1.4 all-to-all-done
  63.1 1.0 copy-done
  64.1 14.2 %shard_map.55 = (f32[896,640]{1,0:T(8,128)}, f32[896,640]{1,0:T(8,128)}, f32[896,640]{1,0:T(8,128)}) custom-call(s32[2]{0:T(128)} %pad_add_fusion.counts, bf16[896,640]{1,0:T(8,128)(2,1)} %bitcast.27, bf16[896,640]{1,0:T(8,128)(2,1)} %bitcast.31, bf16[896,640]{1,0:T(8,128)(2,1)} %bitcast.33), custom_call_target="tpu_custom_call" | custom-call | flops 2055208960 | bytes 10321920 | tf_op jit(solution)/shard_map/pallas_call | solution.py:80
  78.3 0.8 collective-permute-done.mk_ref
  79.1 24.5 %collective-permute-done.1.mv_ref = bf16[512,640]{1,0:T(8,128)(2,1)S(1)} collective-permute-done((bf16[512,640]{1,0:T(8,128)(2,1)S(1)}, bf16[512,640]{1,0:T(8,128)(2,1)S(1)}, u32[]{:S(2)}, u32[]{:S(2)}) %collective-permute-start.1) | collective-permute-done | bytes 655392 | tf_op jit(solution)/shard_map/ppermute | solution.py:21
  103.6 0.9 copy-done.5
  104.5 13.1 %shard_map.56 = bf16[896,640]{1,0:T(8,128)(2,1)} custom-call(s32[2]{0:T(128)} %pad_add_fusion.counts, bf16[896,640]{1,0:T(8,128)(2,1)} %bitcast.28, bf16[512,640]{1,0:T(8,128)(2,1)} %collective-permute-done.mk_ref, bf16[512,640]{1,0:T(8,128)(2,1)} %copy-done.5, f32[896,640]{1,0:T(8,128)} %get-tuple-element.8.acc_ref, f32[896,640]{1,0:T(8,128)} %get-tuple-element.9.top_ref, ...), custom_call_target="tpu_custom_call" | custom-call | flops 1174405120 | bytes 10485760 | tf_op jit(solution)/shard_map/pallas_call | solution.py:109
  117.5 41.7 %all_to_all.76 = bf16[8,112,640]{2,1,0:T(8,128)(2,1)S(1)} all-to-all(bf16[8,112,640]{2,1,0:T(8,128)(2,1)} %bitcast.29), channel_id=1, replica_groups=mesh['stretch'=32,'head'=8,'cfg'=2] {'head'}, dimensions={0} | all-to-all | bytes 2293760 | tf_op jit(solution)/shard_map/all_to_all | solution.py:147
  159.2 1.2 copy.13
  (14 shorter events, 0.0 us)
Async XLA Ops:
  2.4 5.9 %copy-start.3 = (bf16[112,5120]{1,0:T(8,128)(2,1)S(1)}, bf16[112,5120]{1,0:T(8,128)(2,1)}, u32[]{:S(2)}) copy-start(bf16[112,5120]{1,0:T(8,128)(2,1)} %param.7) | copy-start | bytes 3440644
  2.4 21.5 %all-to-all-start.1 = ((bf16[112,8,640]{2,0,1:T(8,128)(2,1)}), bf16[112,8,640]{2,0,1:T(8,128)(2,1)S(1)}, u32[]{:S(2)}, u32[]{:S(2)}) async-start(bf16[112,8,640]{2,0,1:T(8,128)(2,1)} %bitcast.24), calls=%async_computation.1 | async-start | bytes 2293760 | tf_op jit(solution)/shard_map/all_to_all | solution.py:138
  23.8 25.8 %copy-start.1 = (bf16[112,8,640]{2,0,1:T(8,128)(2,1)}, bf16[112,8,640]{2,0,1:T(8,128)(2,1)S(1)}, u32[]{:S(2)}) copy-start(bf16[112,8,640]{2,0,1:T(8,128)(2,1)S(1)} %all-to-all-done.1) | copy-start | bytes 3440644
  23.8 4.8 %copy-start.4 = (bf16[112,5120]{1,0:T(8,128)(2,1)S(1)}, bf16[112,5120]{1,0:T(8,128)(2,1)}, u32[]{:S(2)}) copy-start(bf16[112,5120]{1,0:T(8,128)(2,1)} %param.5) | copy-start | bytes 3440644
  23.8 19.8 %all-to-all-start.2 = ((bf16[112,8,640]{2,0,1:T(8,128)(2,1)}), bf16[112,8,640]{2,0,1:T(8,128)(2,1)S(1)}, u32[]{:S(2)}, u32[]{:S(2)}) async-start(bf16[112,8,640]{2,0,1:T(8,128)(2,1)} %bitcast.23), calls=%async_computation.2 | async-start | bytes 2293760 | tf_op jit(solution)/shard_map/all_to_all | solution.py:141
  43.6 11.3 %copy-start.2 = (bf16[112,8,640]{2,0,1:T(8,128)(2,1)}, bf16[112,8,640]{2,0,1:T(8,128)(2,1)S(1)}, u32[]{:S(2)}) copy-start(bf16[112,8,640]{2,0,1:T(8,128)(2,1)S(1)} %all-to-all-done.2) | copy-start | bytes 3440644
  43.6 4.8 %copy-start.6 = (s32[32]{0:T(128)S(1)}, s32[32]{0:T(128)}, u32[]{:S(2)}) copy-start(s32[32]{0:T(128)} %param.8) | copy-start | bytes 388
  43.7 19.4 %all-to-all-start = ((bf16[112,8,640]{2,0,1:T(8,128)(2,1)}), bf16[112,8,640]{2,0,1:T(8,128)(2,1)S(1)}, u32[]{:S(2)}, u32[]{:S(2)}) async-start(bf16[112,8,640]{2,0,1:T(8,128)(2,1)} %bitcast.25), calls=%async_computation | async-start | bytes 2293760 | tf_op jit(solution)/shard_map/all_to_all | solution.py:144
  49.7 9.6 %copy-start.7 = (s32[32]{0:T(128)S(1)}, s32[32]{0:T(128)}, u32[]{:S(2)}) copy-start(s32[32]{0:T(128)} %param.9) | copy-start | bytes 388
  50.6 28.5 %collective-permute-start = (bf16[512,640]{1,0:T(8,128)(2,1)}, bf16[512,640]{1,0:T(8,128)(2,1)}, u32[]{:S(2)}, u32[]{:S(2)}) collective-permute-start(bf16[512,640]{1,0:T(8,128)(2,1)} %constant_dynamic-slice_fusion.1), channel_id=1, source_target_pairs={{0,16},{16,32},{32,48},{48,64},{64,80},{80,96},{96,112},{112,128},... | collective-permute-start | bytes 1966088 | tf_op jit(solution)/shard_map/ppermute | solution.py:21
  55.0 48.6 %collective-permute-start.1 = (bf16[512,640]{1,0:T(8,128)(2,1)S(1)}, bf16[512,640]{1,0:T(8,128)(2,1)S(1)}, u32[]{:S(2)}, u32[]{:S(2)}) collective-permute-start(bf16[512,640]{1,0:T(8,128)(2,1)S(1)} %constant_dynamic-slice_fusion), channel_id=1, source_target_pairs={{0,16},{16,32},{32,48},{48,64},{64,80},{80,96},{96,112},{112,128},... | collective-permute-start | bytes 1966088 | tf_op jit(solution)/shard_map/ppermute | solution.py:21
  63.1 1.0 copy-start
  103.6 0.9 copy-start.5

commit v4 on v1

v4 whole, which is shorter than its diff:
```python
import math

import jax
import jax.numpy as jnp
from jax import lax
from jax.experimental import pallas as pl
from jax.experimental.pallas import tpu as pltpu
from jax.sharding import PartitionSpec as P

HD = 128
FT = 128
MOT_CAP = 4

NEG = -1e30
TQ = 448
COLS = 8


def from_behind(shard, axis, by):
    size = lax.axis_size(axis)
    pairs = [(i, i + by) for i in range(size) if 0 <= i + by < size]
    return lax.ppermute(shard, axis, pairs)


def scaled_scores(q, k, live):
    scores = lax.dot_general(
        q, k, (((1,), (1,)), ((), ())), preferred_element_type=jnp.float32
    )
    scores = scores * (1.0 / math.sqrt(HD))
    return jnp.where(live, scores, NEG)


def head_cols(h):
    return slice(h * HD, (h + 1) * HD)


def own_kernel(counts, q_ref, k_ref, v_ref, acc_ref, top_ref, tot_ref):
    own_live = counts[0] * FT
    span = k_ref.shape[0]
    key_live = lax.broadcasted_iota(jnp.int32, (1, span), 1) < own_live
    for h in range(acc_ref.shape[1] // HD):
        c = head_cols(h)
        masked = scaled_scores(q_ref[:, c], k_ref[:, c], key_live)
        top = jnp.max(masked, axis=1, keepdims=True)
        weights = jnp.exp(masked - top).astype(jnp.bfloat16)
        v = v_ref[:, c]
        v_ext = jnp.concatenate([v, jnp.ones_like(v)], axis=1)
        both = jnp.dot(weights, v_ext, preferred_element_type=jnp.float32)
        acc_ref[:, c] = both[:, :HD]
        top_ref[:, h : h + 1] = top
        tot_ref[:, h : h + 1] = both[:, HD : HD + 1]


def mscore_kernel(counts, q_ref, mk_ref, w_ref, top_ref, tot_ref):
    mot_start = (MOT_CAP - counts[1]) * FT
    tail = mk_ref.shape[0]
    slot_live = lax.broadcasted_iota(jnp.int32, (1, tail), 1) >= mot_start
    ones = jnp.ones((tail, HD), jnp.bfloat16)
    for h in range(q_ref.shape[1] // HD):
        c = head_cols(h)
        masked = scaled_scores(q_ref[:, c], mk_ref[:, c], slot_live)
        top = jnp.max(masked, axis=1, keepdims=True)
        weights = jnp.exp(masked - top).astype(jnp.bfloat16)
        w_ref[:, h * tail : (h + 1) * tail] = weights
        total = jnp.dot(weights, ones, preferred_element_type=jnp.float32)
        top_ref[:, h : h + 1] = top
        tot_ref[:, h : h + 1] = total[:, 0:1]


def merge_kernel(
    counts, w_ref, mv_ref, acc_ref, top_ref, tot_ref, mtop_ref, mtot_ref, o_ref
):
    own_live = counts[0] * FT
    tail = mv_ref.shape[0]
    rows = pl.program_id(0) * TQ + lax.broadcasted_iota(jnp.int32, (TQ, 1), 0)
    row_live = rows < own_live
    for h in range(o_ref.shape[1] // HD):
        c = head_cols(h)
        acc_mot = jnp.dot(
            w_ref[:, h * tail : (h + 1) * tail],
            mv_ref[:, c],
            preferred_element_type=jnp.float32,
        )
        top_own = top_ref[:, h : h + 1]
        top_mot = mtop_ref[:, h : h + 1]
        peak = jnp.maximum(top_own, top_mot)
        factor_own = jnp.exp(top_own - peak)
        factor_mot = jnp.exp(top_mot - peak)
        mixed = (acc_ref[:, c] * factor_own + acc_mot * factor_mot) / (
            tot_ref[:, h : h + 1] * factor_own + mtot_ref[:, h : h + 1] * factor_mot
        )
        o_ref[:, c] = jnp.where(row_live, mixed, 0.0).astype(o_ref.dtype)


def rows_of(width):
    return pl.BlockSpec((TQ, width), lambda i, c: (i, 0))


def whole(rows, width):
    return pl.BlockSpec((rows, width), lambda i, c: (0, 0))


def call(kernel, counts, operands, in_specs, outs, cost):
    span = operands[0].shape[0]
    shapes = [jax.ShapeDtypeStruct((span, w), t) for w, t in outs]
    return pl.pallas_call(
        kernel,
        out_shape=tuple(shapes),
        grid_spec=pltpu.PrefetchScalarGridSpec(
            num_scalar_prefetch=1,
            grid=(span // TQ,),
            in_specs=in_specs,
            out_specs=[rows_of(w) for w, _ in outs],
        ),
        compiler_params=pltpu.CompilerParams(dimension_semantics=("arbitrary",)),
        cost_estimate=cost,
    )(counts, *operands)


def body(queries, keys, values, frames, motion):
    stretch_index = lax.axis_index("stretch")
    tail = MOT_CAP * FT
    count_own = frames[stretch_index]
    counts = jnp.stack([count_own, motion[stretch_index]]).astype(jnp.int32)
    tail_begin = (count_own - MOT_CAP) * FT
    k_heads = lax.all_to_all(keys, "head", split_axis=1, concat_axis=0, tiled=True)
    v_heads = lax.all_to_all(values, "head", split_axis=1, concat_axis=0, tiled=True)
    k_tail = lax.dynamic_slice_in_dim(k_heads, tail_begin, tail, 0)
    v_tail = lax.dynamic_slice_in_dim(v_heads, tail_begin, tail, 0)
    k_prior = from_behind(k_tail, "stretch", 1)
    v_prior = from_behind(v_tail, "stretch", 1)
    q_heads = lax.all_to_all(queries, "head", split_axis=1, concat_axis=0, tiled=True)
    span, local = q_heads.shape
    heads = local // HD
    f32 = jnp.float32
    acc, top, tot = call(
        own_kernel,
        counts,
        (q_heads, k_heads, v_heads),
        [rows_of(local), whole(span, local), whole(span, local)],
        [(local, f32), (COLS, f32), (COLS, f32)],
        pl.CostEstimate(
            flops=heads * 2 * span * span * 3 * HD,
            transcendentals=heads * span * span,
            bytes_accessed=3 * span * local * 2 + span * local * 4,
        ),
    )
    w_mot, mtop, mtot = call(
        mscore_kernel,
        counts,
        (q_heads, k_prior),
        [rows_of(local), whole(tail, local)],
        [(heads * tail, jnp.bfloat16), (COLS, f32), (COLS, f32)],
        pl.CostEstimate(
            flops=heads * 2 * span * tail * 2 * HD,
            transcendentals=heads * span * tail,
            bytes_accessed=span * local * 2 + tail * local * 2 + span * heads * tail * 2,
        ),
    )
    (mixed,) = call(
        merge_kernel,
        counts,
        (w_mot, v_prior, acc, top, tot, mtop, mtot),
        [
            rows_of(heads * tail),
            whole(tail, local),
            rows_of(local),
            rows_of(COLS),
            rows_of(COLS),
            rows_of(COLS),
            rows_of(COLS),
        ],
        [(local, jnp.bfloat16)],
        pl.CostEstimate(
            flops=heads * 2 * span * tail * HD,
            transcendentals=2 * heads * span,
            bytes_accessed=span * heads * tail * 2 + span * local * 6 + tail * local * 2,
        ),
    )
    return lax.all_to_all(mixed, "head", split_axis=0, concat_axis=1, tiled=True)


def solution(mesh):
    placed = (
        P(("cfg", "stretch", "head"), None),
        P(("cfg", "stretch", "head"), None),
        P(("cfg", "stretch", "head"), None),
        P(),
        P(),
    )
    return jax.shard_map(
        body,
        mesh=mesh,
        in_specs=placed,
        out_specs=P(("cfg", "stretch", "head"), None),
        check_vma=False,
    )
```

time: 165 us -> 155 us (0.939)
  waiting for transfers between devices: 69.9 us -> 50.6 us
  Pallas kernels: 17.5 us -> 25.8 us
    ppermute x2, waiting for transfers between devices: 40.1 us -> 20.9 us  [from_behind(): return lax.ppermute(shard, axis, pairs)]
    pallas_call x1 -> x3, Pallas kernels: 17.5 us -> 25.8 us  [call(): pl.pallas_call(kernel, out_shape=tuple(shapes), grid_spec=pltpu.PrefetchS...]
  transfers between devices with their start and end apart: 5 -> 5, of which waited for: 5 -> 5; matrix products, arithmetic and copies ran while one was open for 4% -> 4% of each run, Pallas kernels for 0% -> 12%
where the time goes in v4:
time: 155 us
  waiting for transfers between devices  50.6 us (33%)
  blocking collectives  41.8 us (27%)
  Pallas kernels  25.8 us (17%)
  starting transfers between devices  24 us (15%)
  local copies, waits for them, and re-layouts  9.78 us (6%)
  other arithmetic  1.88 us (1%)
    all_to_all x1, blocking collectives, body(): lax.all_to_all(mixed, 'head', split_axis=0, concat_axis=1, tiled=True)  41.8 us
    pallas_call x3, Pallas kernels, call(): pl.pallas_call(kernel, out_shape=tuple(shapes), grid_spec=pltpu.PrefetchS...  25.8 us
    ppermute x2, waiting for transfers between devices, from_behind(): return lax.ppermute(shard, axis, pairs)  20.9 us
    all_to_all x1, waiting for transfers between devices, body(): lax.all_to_all(keys, 'head', split_axis=1, concat_axis=0, tiled=True)  14.5 us
    all_to_all x1, waiting for transfers between devices, body(): lax.all_to_all(values, 'head', split_axis=1, concat_axis=0, tiled=True)  13.9 us
    ppermute x2, starting transfers between devices, from_behind(): return lax.ppermute(shard, axis, pairs)  8.55 us
    all_to_all x1, starting transfers between devices, body(): lax.all_to_all(keys, 'head', split_axis=1, concat_axis=0, tiled=True)  5.89 us
    all_to_all x1, starting transfers between devices, body(): lax.all_to_all(values, 'head', split_axis=1, concat_axis=0, tiled=True)  4.81 us
  transfers between devices with their start and end apart: 5, of which 5 were waited for; matrix products, arithmetic and copies ran while one was open for 4% of the time, Pallas kernels for 12%

profile of v4, /device:TPU:56, one launch (start us, length us, event | category | flops | bytes accessed | tf_op | source)
XLA Modules:
  0.0 154.5 jit_solution(15157736210514237208)
XLA Ops:
  0.0 2.4 %copy.18 = bf16[14,8,8,640]{3,2,0,1:T(8,128)(2,1)} copy(bf16[14,8,8,640]{3,2,1,0:T(8,128)(2,1)} %bitcast.32) | data formatting | bytes 2293760 | tf_op jit(solution)/shard_map/all_to_all | solution.py:126
  2.4 5.9 %all-to-all-start.1 = ((bf16[112,8,640]{2,0,1:T(8,128)(2,1)}), bf16[112,8,640]{2,0,1:T(8,128)(2,1)S(1)}, u32[]{:S(2)}, u32[]{:S(2)}) async-start(bf16[112,8,640]{2,0,1:T(8,128)(2,1)} %bitcast.24), calls=%async_computation.1 | async-start | bytes 2293760 | tf_op jit(solution)/shard_map/all_to_all | solution.py:126
  8.3 1.1 copy.17
  9.4 14.5 %all-to-all-done.1 = bf16[112,8,640]{2,0,1:T(8,128)(2,1)S(1)} async-done(((bf16[112,8,640]{2,0,1:T(8,128)(2,1)}), bf16[112,8,640]{2,0,1:T(8,128)(2,1)S(1)}, u32[]{:S(2)}, u32[]{:S(2)}) %all-to-all-start.1) | async-done | bytes 1146912 | tf_op jit(solution)/shard_map/all_to_all | solution.py:126
  23.8 4.8 %all-to-all-start.2 = ((bf16[112,8,640]{2,0,1:T(8,128)(2,1)}), bf16[112,8,640]{2,0,1:T(8,128)(2,1)S(1)}, u32[]{:S(2)}, u32[]{:S(2)}) async-start(bf16[112,8,640]{2,0,1:T(8,128)(2,1)} %bitcast.23), calls=%async_computation.2 | async-start | bytes 2293760 | tf_op jit(solution)/shard_map/all_to_all | solution.py:127
  28.7 1.1 copy.19
  29.8 13.9 %all-to-all-done.2 = bf16[112,8,640]{2,0,1:T(8,128)(2,1)S(1)} async-done(((bf16[112,8,640]{2,0,1:T(8,128)(2,1)}), bf16[112,8,640]{2,0,1:T(8,128)(2,1)S(1)}, u32[]{:S(2)}, u32[]{:S(2)}) %all-to-all-start.2) | async-done | bytes 1146912 | tf_op jit(solution)/shard_map/all_to_all | solution.py:127
  43.7 4.8 %all-to-all-start = ((bf16[112,8,640]{2,0,1:T(8,128)(2,1)}), bf16[112,8,640]{2,0,1:T(8,128)(2,1)S(1)}, u32[]{:S(2)}, u32[]{:S(2)}) async-start(bf16[112,8,640]{2,0,1:T(8,128)(2,1)} %bitcast.25), calls=%async_computation | async-start | bytes 2293760 | tf_op jit(solution)/shard_map/all_to_all | solution.py:132
  48.4 0.6 dynamic_slice.12
  49.7 0.9 constant_dynamic-slice_fusion.1
  50.6 4.3 %collective-permute-start = (bf16[512,640]{1,0:T(8,128)(2,1)}, bf16[512,640]{1,0:T(8,128)(2,1)}, u32[]{:S(2)}, u32[]{:S(2)}) collective-permute-start(bf16[512,640]{1,0:T(8,128)(2,1)} %constant_dynamic-slice_fusion.1), channel_id=1, source_target_pairs={{0,16},{16,32},{32,48},{48,64},{64,80},{80,96},{96,112},{112,128},... | collective-permute-start | bytes 1966088 | tf_op jit(solution)/shard_map/ppermute | solution.py:22
  54.9 4.3 %collective-permute-start.1 = (bf16[512,640]{1,0:T(8,128)(2,1)S(1)}, bf16[512,640]{1,0:T(8,128)(2,1)S(1)}, u32[]{:S(2)}, u32[]{:S(2)}) collective-permute-start(bf16[512,640]{1,0:T(8,128)(2,1)S(1)} %constant_dynamic-slice_fusion), channel_id=1, source_target_pairs={{0,16},{16,32},{32,48},{48,64},{64,80},{80,96},{96,112},{112,128},... | collective-permute-start | bytes 1966088 | tf_op jit(solution)/shard_map/ppermute | solution.py:22
  59.2 0.6 dynamic_slice.13
  59.9 1.9 %pad_add_fusion.counts = s32[2]{0:T(128)} fusion(s32[1]{0:T(128)} %dynamic_slice.13, s32[1]{0:T(128)} %dynamic_slice.12), kind=kLoop, calls=%fused_computation.3 | loop fusion | flops 2 | bytes 16 | tf_op jit(solution)/shard_map/stack | solution.py:124
  61.7 1.3 all-to-all-done
  63.1 1.0 copy-done.4
  64.1 11.3 %shard_map.56 = (f32[896,640]{1,0:T(8,128)}, f32[896,8]{1,0:T(8,128)}, f32[896,8]{1,0:T(8,128)}) custom-call(s32[2]{0:T(128)} %pad_add_fusion.counts, bf16[896,640]{1,0:T(8,128)(2,1)} %bitcast.35, bf16[896,640]{1,0:T(8,128)(2,1)} %bitcast.29, bf16[896,640]{1,0:T(8,128)(2,1)} %bitcast.31), custom_call_target="tpu_custom_call" | custom-call | flops 3082813440 | bytes 5734400 | tf_op jit(solution)/shard_map/pallas_call | solution.py:106
  75.4 3.6 %collective-permute-done.mk_ref = bf16[512,640]{1,0:T(8,128)(2,1)} collective-permute-done((bf16[512,640]{1,0:T(8,128)(2,1)}, bf16[512,640]{1,0:T(8,128)(2,1)}, u32[]{:S(2)}, u32[]{:S(2)}) %collective-permute-start) | collective-permute-done | bytes 655392 | tf_op jit(solution)/shard_map/ppermute | solution.py:22
  79.0 7.2 %shard_map.55 = (bf16[896,2560]{1,0:T(8,128)(2,1)}, f32[896,8]{1,0:T(8,128)}, f32[896,8]{1,0:T(8,128)}) custom-call(s32[2]{0:T(128)} %pad_add_fusion.counts, bf16[896,640]{1,0:T(8,128)(2,1)} %bitcast.36, bf16[512,640]{1,0:T(8,128)(2,1)} %collective-permute-done.mk_ref), custom_call_target="tpu_custom_call" | custom-call | flops 1174405120 | bytes 6389760 | tf_op jit(solution)/shard_map/pallas_call | solution.py:106
  86.2 17.2 %collective-permute-done.1.mv_ref = bf16[512,640]{1,0:T(8,128)(2,1)S(1)} collective-permute-done((bf16[512,640]{1,0:T(8,128)(2,1)S(1)}, bf16[512,640]{1,0:T(8,128)(2,1)S(1)}, u32[]{:S(2)}, u32[]{:S(2)}) %collective-permute-start.1) | collective-permute-done | bytes 655392 | tf_op jit(solution)/shard_map/ppermute | solution.py:22
  103.5 0.8 copy-done.5
  104.3 7.3 %shard_map.57 = bf16[896,640]{1,0:T(8,128)(2,1)} custom-call(s32[2]{0:T(128)} %pad_add_fusion.counts, bf16[896,2560]{1,0:T(8,128)(2,1)} %get-tuple-element.11.w_ref, bf16[512,640]{1,0:T(8,128)(2,1)} %copy-done.5, f32[896,640]{1,0:T(8,128)} %get-tuple-element.12.acc_ref, f32[896,8]{1,0:T(8,128)} %get-tuple-element.13.top_ref, ...), custom_call_target="tpu_custom_call" | custom-call | flops 587202560 | bytes 8683520 | tf_op jit(solution)/shard_map/pallas_call | solution.py:106
  111.6 41.8 %all_to_all.76 = bf16[8,112,640]{2,1,0:T(8,128)(2,1)S(1)} all-to-all(bf16[8,112,640]{2,1,0:T(8,128)(2,1)} %bitcast.27), channel_id=1, replica_groups=mesh['stretch'=32,'head'=8,'cfg'=2] {'head'}, dimensions={0} | all-to-all | bytes 2293760 | tf_op jit(solution)/shard_map/all_to_all | solution.py:180
  153.4 1.2 copy.13
  (15 shorter events, 0.1 us)
Async XLA Ops:
  2.4 5.9 %copy-start.2 = (bf16[112,5120]{1,0:T(8,128)(2,1)S(1)}, bf16[112,5120]{1,0:T(8,128)(2,1)}, u32[]{:S(2)}) copy-start(bf16[112,5120]{1,0:T(8,128)(2,1)} %param.7) | copy-start | bytes 3440644
  2.4 21.5 %all-to-all-start.1 = ((bf16[112,8,640]{2,0,1:T(8,128)(2,1)}), bf16[112,8,640]{2,0,1:T(8,128)(2,1)S(1)}, u32[]{:S(2)}, u32[]{:S(2)}) async-start(bf16[112,8,640]{2,0,1:T(8,128)(2,1)} %bitcast.24), calls=%async_computation.1 | async-start | bytes 2293760 | tf_op jit(solution)/shard_map/all_to_all | solution.py:126
  23.8 25.8 %copy-start = (bf16[112,8,640]{2,0,1:T(8,128)(2,1)}, bf16[112,8,640]{2,0,1:T(8,128)(2,1)S(1)}, u32[]{:S(2)}) copy-start(bf16[112,8,640]{2,0,1:T(8,128)(2,1)S(1)} %all-to-all-done.1) | copy-start | bytes 3440644
  23.8 4.8 %copy-start.3 = (bf16[112,5120]{1,0:T(8,128)(2,1)S(1)}, bf16[112,5120]{1,0:T(8,128)(2,1)}, u32[]{:S(2)}) copy-start(bf16[112,5120]{1,0:T(8,128)(2,1)} %param.5) | copy-start | bytes 3440644
  23.8 19.8 %all-to-all-start.2 = ((bf16[112,8,640]{2,0,1:T(8,128)(2,1)}), bf16[112,8,640]{2,0,1:T(8,128)(2,1)S(1)}, u32[]{:S(2)}, u32[]{:S(2)}) async-start(bf16[112,8,640]{2,0,1:T(8,128)(2,1)} %bitcast.23), calls=%async_computation.2 | async-start | bytes 2293760 | tf_op jit(solution)/shard_map/all_to_all | solution.py:127
  43.6 11.2 %copy-start.1 = (bf16[112,8,640]{2,0,1:T(8,128)(2,1)}, bf16[112,8,640]{2,0,1:T(8,128)(2,1)S(1)}, u32[]{:S(2)}) copy-start(bf16[112,8,640]{2,0,1:T(8,128)(2,1)S(1)} %all-to-all-done.2) | copy-start | bytes 3440644
  43.6 4.8 %copy-start.6 = (s32[32]{0:T(128)S(1)}, s32[32]{0:T(128)}, u32[]{:S(2)}) copy-start(s32[32]{0:T(128)} %param.8) | copy-start | bytes 388
  43.7 19.4 %all-to-all-start = ((bf16[112,8,640]{2,0,1:T(8,128)(2,1)}), bf16[112,8,640]{2,0,1:T(8,128)(2,1)S(1)}, u32[]{:S(2)}, u32[]{:S(2)}) async-start(bf16[112,8,640]{2,0,1:T(8,128)(2,1)} %bitcast.25), calls=%async_computation | async-start | bytes 2293760 | tf_op jit(solution)/shard_map/all_to_all | solution.py:132
  49.7 9.6 %copy-start.7 = (s32[32]{0:T(128)S(1)}, s32[32]{0:T(128)}, u32[]{:S(2)}) copy-start(s32[32]{0:T(128)} %param.9) | copy-start | bytes 388
  50.6 28.5 %collective-permute-start = (bf16[512,640]{1,0:T(8,128)(2,1)}, bf16[512,640]{1,0:T(8,128)(2,1)}, u32[]{:S(2)}, u32[]{:S(2)}) collective-permute-start(bf16[512,640]{1,0:T(8,128)(2,1)} %constant_dynamic-slice_fusion.1), channel_id=1, source_target_pairs={{0,16},{16,32},{32,48},{48,64},{64,80},{80,96},{96,112},{112,128},... | collective-permute-start | bytes 1966088 | tf_op jit(solution)/shard_map/ppermute | solution.py:22
  54.9 48.5 %collective-permute-start.1 = (bf16[512,640]{1,0:T(8,128)(2,1)S(1)}, bf16[512,640]{1,0:T(8,128)(2,1)S(1)}, u32[]{:S(2)}, u32[]{:S(2)}) collective-permute-start(bf16[512,640]{1,0:T(8,128)(2,1)S(1)} %constant_dynamic-slice_fusion), channel_id=1, source_target_pairs={{0,16},{16,32},{32,48},{48,64},{64,80},{80,96},{96,112},{112,128},... | collective-permute-start | bytes 1966088 | tf_op jit(solution)/shard_map/ppermute | solution.py:22
  63.1 1.0 copy-start.4
  103.4 0.8 copy-start.5

commit v5 on v4

--- a/solution.py
+++ b/solution.py
@@ -1,3 +1,4 @@
+import functools
 import math
 
 import jax
@@ -86,9 +87,10 @@
         peak = jnp.maximum(top_own, top_mot)
         factor_own = jnp.exp(top_own - peak)
         factor_mot = jnp.exp(top_mot - peak)
-        mixed = (acc_ref[:, c] * factor_own + acc_mot * factor_mot) / (
+        scale = 1.0 / (
             tot_ref[:, h : h + 1] * factor_own + mtot_ref[:, h : h + 1] * factor_mot
         )
+        mixed = (acc_ref[:, c] * factor_own + acc_mot * factor_mot) * scale
         o_ref[:, c] = jnp.where(row_live, mixed, 0.0).astype(o_ref.dtype)
 
 
@@ -117,7 +119,21 @@
     )(counts, *operands)
 
 
-def body(queries, keys, values, frames, motion):
+def relay_plan(mesh):
+    where = [mesh.devices[c, 0, 0].coords for c in range(mesh.devices.shape[0])]
+    inner, first, second = [], [], []
+    for c in range(1, len(where)):
+        (xs, ys, zs), (xr, yr, zr) = where[c - 1], where[c]
+        via = [j for j, (x, y, z) in enumerate(where) if y == ys and z == zr]
+        if ys == yr or not via:
+            inner.append((c - 1, c))
+        else:
+            first.append((c - 1, via[0]))
+            second.append((via[0], c))
+    return inner, first, second
+
+
+def body(plan, queries, keys, values, frames, motion):
     stretch_index = lax.axis_index("stretch")
     tail = MOT_CAP * FT
     count_own = frames[stretch_index]
@@ -128,7 +144,17 @@
     k_tail = lax.dynamic_slice_in_dim(k_heads, tail_begin, tail, 0)
     v_tail = lax.dynamic_slice_in_dim(v_heads, tail_begin, tail, 0)
     k_prior = from_behind(k_tail, "stretch", 1)
-    v_prior = from_behind(v_tail, "stretch", 1)
+    inner, first, second = plan
+    half = tail // 2
+    v_near = from_behind(v_tail[:half], "stretch", 1)
+    v_far = v_tail[half:]
+    if first:
+        v_far = lax.ppermute(v_far, "stretch", inner) + lax.ppermute(
+            lax.ppermute(v_far, "stretch", first), "stretch", second
+        )
+    else:
+        v_far = from_behind(v_far, "stretch", 1)
+    v_prior = jnp.concatenate([v_near, v_far], axis=0)
     q_heads = lax.all_to_all(queries, "head", split_axis=1, concat_axis=0, tiled=True)
     span, local = q_heads.shape
     heads = local // HD
@@ -189,7 +215,7 @@
         P(),
     )
     return jax.shard_map(
-        body,
+        functools.partial(body, relay_plan(mesh)),
         mesh=mesh,
         in_specs=placed,
         out_specs=P(("cfg", "stretch", "head"), None),

time: 155 us -> 141 us (0.910)
  waiting for transfers between devices: 50.6 us -> 38.7 us
  blocking collectives: 41.8 us -> 33.1 us
  starting transfers between devices: 24 us -> 30.4 us
    ppermute x2, waiting for transfers between devices: 20.9 us -> 2.32 us  [from_behind(): return lax.ppermute(shard, axis, pairs)]
    all_to_all x1, blocking collectives: 41.8 us -> 33.1 us  [body(): lax.all_to_all(mixed, 'head', split_axis=0, concat_axis=1, tiled=True)]
    ppermute x0 -> x3, waiting for transfers between devices: none -> 8.02 us  [the longest x1 8.02 us: body(): lax.ppermute(lax.ppermute(v_far, 'stretch', first), 'stretch', second)]
    ppermute x0 -> x3, starting transfers between devices: none -> 6.98 us  [the longest x1 4.28 us: body(): lax.ppermute(v_far, 'stretch', inner)]
  transfers between devices with their start and end apart: 5 -> 8, of which waited for: 5 -> 4; matrix products, arithmetic and copies ran while one was open for 4% -> 5% of each run, Pallas kernels for 12% -> 13%
where the time goes in v5:
time: 141 us
  waiting for transfers between devices  38.7 us (27%)
  blocking collectives  33.1 us (23%)
  starting transfers between devices  30.4 us (22%)
  Pallas kernels  25.8 us (18%)
  local copies, waits for them, and re-layouts  9.06 us (6%)
  other arithmetic  2.94 us (2%)
    all_to_all x1, blocking collectives, body(): lax.all_to_all(mixed, 'head', split_axis=0, concat_axis=1, tiled=True)  33.1 us
    pallas_call x3, Pallas kernels, call(): pl.pallas_call(kernel, out_shape=tuple(shapes), grid_spec=pltpu.PrefetchS...  25.8 us
    all_to_all x1, waiting for transfers between devices, body(): lax.all_to_all(keys, 'head', split_axis=1, concat_axis=0, tiled=True)  14.5 us
    all_to_all x1, waiting for transfers between devices, body(): lax.all_to_all(values, 'head', split_axis=1, concat_axis=0, tiled=True)  13.9 us
    ppermute x1, waiting for transfers between devices, body(): lax.ppermute(lax.ppermute(v_far, 'stretch', first), 'stretch', second)  8.02 us
    ppermute x2, starting transfers between devices, from_behind(): return lax.ppermute(shard, axis, pairs)  7.92 us
    all_to_all x1, starting transfers between devices, body(): lax.all_to_all(keys, 'head', split_axis=1, concat_axis=0, tiled=True)  5.89 us
    all_to_all x1, starting transfers between devices, body(): lax.all_to_all(values, 'head', split_axis=1, concat_axis=0, tiled=True)  4.81 us
  transfers between devices with their start and end apart: 8, of which 4 were waited for; matrix products, arithmetic and copies ran while one was open for 5% of the time, Pallas kernels for 13%

profile of v5, /device:TPU:56, one launch (start us, length us, event | category | flops | bytes accessed | tf_op | source)
XLA Modules:
  0.0 140.8 jit_solution(9141405587576435676)
XLA Ops:
  0.0 2.4 %copy.18 = bf16[14,8,8,640]{3,2,0,1:T(8,128)(2,1)} copy(bf16[14,8,8,640]{3,2,1,0:T(8,128)(2,1)} %bitcast.32) | data formatting | bytes 2293760 | tf_op jit(solution)/shard_map/all_to_all | solution.py:142
  2.4 5.9 %all-to-all-start.1 = ((bf16[112,8,640]{2,0,1:T(8,128)(2,1)}), bf16[112,8,640]{2,0,1:T(8,128)(2,1)S(1)}, u32[]{:S(2)}, u32[]{:S(2)}) async-start(bf16[112,8,640]{2,0,1:T(8,128)(2,1)} %bitcast.24), calls=%async_computation.1 | async-start | bytes 2293760 | tf_op jit(solution)/shard_map/all_to_all | solution.py:142
  8.3 1.1 copy.17
  9.4 14.5 %all-to-all-done.1 = bf16[112,8,640]{2,0,1:T(8,128)(2,1)S(1)} async-done(((bf16[112,8,640]{2,0,1:T(8,128)(2,1)}), bf16[112,8,640]{2,0,1:T(8,128)(2,1)S(1)}, u32[]{:S(2)}, u32[]{:S(2)}) %all-to-all-start.1) | async-done | bytes 1146912 | tf_op jit(solution)/shard_map/all_to_all | solution.py:142
  23.8 4.8 %all-to-all-start.2 = ((bf16[112,8,640]{2,0,1:T(8,128)(2,1)}), bf16[112,8,640]{2,0,1:T(8,128)(2,1)S(1)}, u32[]{:S(2)}, u32[]{:S(2)}) async-start(bf16[112,8,640]{2,0,1:T(8,128)(2,1)} %bitcast.23), calls=%async_computation.2 | async-start | bytes 2293760 | tf_op jit(solution)/shard_map/all_to_all | solution.py:143
  28.7 1.1 copy.19
  29.8 13.9 %all-to-all-done.2 = bf16[112,8,640]{2,0,1:T(8,128)(2,1)S(1)} async-done(((bf16[112,8,640]{2,0,1:T(8,128)(2,1)}), bf16[112,8,640]{2,0,1:T(8,128)(2,1)S(1)}, u32[]{:S(2)}, u32[]{:S(2)}) %all-to-all-start.2) | async-done | bytes 1146912 | tf_op jit(solution)/shard_map/all_to_all | solution.py:143
  43.7 4.8 %all-to-all-start = ((bf16[112,8,640]{2,0,1:T(8,128)(2,1)}), bf16[112,8,640]{2,0,1:T(8,128)(2,1)S(1)}, u32[]{:S(2)}, u32[]{:S(2)}) async-start(bf16[112,8,640]{2,0,1:T(8,128)(2,1)} %bitcast.25), calls=%async_computation | async-start | bytes 2293760 | tf_op jit(solution)/shard_map/all_to_all | solution.py:158
  49.8 0.9 constant_dynamic-slice_fusion
  50.7 1.4 collective-permute-start.3
  52.2 4.3 %collective-permute-start = (bf16[512,640]{1,0:T(8,128)(2,1)S(1)}, bf16[512,640]{1,0:T(8,128)(2,1)}, u32[]{:S(2)}, u32[]{:S(2)}) collective-permute-start(bf16[512,640]{1,0:T(8,128)(2,1)S(1)} %constant_dynamic-slice_fusion.2), channel_id=1, source_target_pairs={{0,16},{16,32},{32,48},{48,64},{64,80},{80,96},{96,112},{112,128},... | collective-permute-start | bytes 1966088 | tf_op jit(solution)/shard_map/ppermute | solution.py:23
  57.2 4.3 %collective-permute-start.2 = (bf16[256,640]{1,0:T(8,128)(2,1)}, bf16[256,640]{1,0:T(8,128)(2,1)S(1)}, u32[]{:S(2)}, u32[]{:S(2)}) collective-permute-start(bf16[256,640]{1,0:T(8,128)(2,1)} %get-tuple-element.18), channel_id=1, source_target_pairs={{0,16},{16,32},{32,48},{48,64},{64,80},{80,96},{96,112},{128,144},... | collective-permute-start | bytes 983048 | tf_op jit(solution)/shard_map/ppermute | solution.py:152
  61.5 1.3 collective-permute-start.4
  62.8 2.0 %pad_add_fusion.counts = s32[2]{0:T(128)} fusion(s32[1]{0:T(128)} %dynamic_slice.13, s32[1]{0:T(128)} %dynamic_slice.12), kind=kLoop, calls=%fused_computation.7 | loop fusion | flops 2 | bytes 16 | tf_op jit(solution)/shard_map/stack | solution.py:140
  64.7 3.6 %collective-permute-start.1 = (bf16[256,640]{1,0:T(8,128)(2,1)}, bf16[256,640]{1,0:T(8,128)(2,1)S(1)}, u32[]{:S(2)}, u32[]{:S(2)}) collective-permute-start(bf16[256,640]{1,0:T(8,128)(2,1)} %get-tuple-element.17), channel_id=1, source_target_pairs={{0,16},{16,32},{32,48},{48,64},{64,80},{80,96},{96,112},{112,128},... | collective-permute-start | bytes 983048 | tf_op jit(solution)/shard_map/ppermute | solution.py:23
  68.4 1.0 copy-done.4
  69.4 11.4 %shard_map.56 = (f32[896,640]{1,0:T(8,128)}, f32[896,8]{1,0:T(8,128)}, f32[896,8]{1,0:T(8,128)}) custom-call(s32[2]{0:T(128)} %pad_add_fusion.counts, bf16[896,640]{1,0:T(8,128)(2,1)} %bitcast.35, bf16[896,640]{1,0:T(8,128)(2,1)} %bitcast.29, bf16[896,640]{1,0:T(8,128)(2,1)} %bitcast.31), custom_call_target="tpu_custom_call" | custom-call | flops 3082813440 | bytes 5734400 | tf_op jit(solution)/shard_map/pallas_call | solution.py:108
  80.7 8.0 %collective-permute-done.4 = bf16[256,640]{1,0:T(8,128)(2,1)S(1)} collective-permute-done((bf16[256,640]{1,0:T(8,128)(2,1)}, bf16[256,640]{1,0:T(8,128)(2,1)S(1)}, u32[]{:S(2)}, u32[]{:S(2)}) %collective-permute-start.4) | collective-permute-done | bytes 327712 | tf_op jit(solution)/shard_map/ppermute | solution.py:152
  88.9 7.2 %shard_map.55 = (bf16[896,2560]{1,0:T(8,128)(2,1)}, f32[896,8]{1,0:T(8,128)}, f32[896,8]{1,0:T(8,128)}) custom-call(s32[2]{0:T(128)} %pad_add_fusion.counts, bf16[896,640]{1,0:T(8,128)(2,1)} %bitcast.36, bf16[512,640]{1,0:T(8,128)(2,1)} %collective-permute-done.mk_ref), custom_call_target="tpu_custom_call" | custom-call | flops 1174405120 | bytes 6389760 | tf_op jit(solution)/shard_map/pallas_call | solution.py:108
  96.1 2.3 %collective-permute-done.1 = bf16[256,640]{1,0:T(8,128)(2,1)S(1)} collective-permute-done((bf16[256,640]{1,0:T(8,128)(2,1)}, bf16[256,640]{1,0:T(8,128)(2,1)S(1)}, u32[]{:S(2)}, u32[]{:S(2)}) %collective-permute-start.1) | collective-permute-done | bytes 327712 | tf_op jit(solution)/shard_map/ppermute | solution.py:23
  98.4 0.9 pad_maximum_fusion.mv_ref
  99.3 7.2 %shard_map.57 = bf16[896,640]{1,0:T(8,128)(2,1)} custom-call(s32[2]{0:T(128)} %pad_add_fusion.counts, bf16[896,2560]{1,0:T(8,128)(2,1)} %get-tuple-element.11.w_ref, bf16[512,640]{1,0:T(8,128)(2,1)} %pad_maximum_fusion.mv_ref, f32[896,640]{1,0:T(8,128)} %get-tuple-element.12.acc_ref, f32[896,8]{1,0:T(8,128)} %get-tuple-element.13.top_ref, ...), custom_call_target="tpu_custom_call" | custom-call | flops 587202560 | bytes 8683520 | tf_op jit(solution)/shard_map/pallas_call | solution.py:108
  106.5 33.1 %all_to_all.76 = bf16[8,112,640]{2,1,0:T(8,128)(2,1)S(1)} all-to-all(bf16[8,112,640]{2,1,0:T(8,128)(2,1)} %bitcast.27), channel_id=1, replica_groups=mesh['stretch'=32,'head'=8,'cfg'=2] {'head'}, dimensions={0} | all-to-all | bytes 2293760 | tf_op jit(solution)/shard_map/all_to_all | solution.py:206
  139.6 1.2 copy.13
  (21 shorter events, 1.5 us)
Async XLA Ops:
  2.4 5.9 %copy-start.2 = (bf16[112,5120]{1,0:T(8,128)(2,1)S(1)}, bf16[112,5120]{1,0:T(8,128)(2,1)}, u32[]{:S(2)}) copy-start(bf16[112,5120]{1,0:T(8,128)(2,1)} %param.7) | copy-start | bytes 3440644
  2.4 21.5 %all-to-all-start.1 = ((bf16[112,8,640]{2,0,1:T(8,128)(2,1)}), bf16[112,8,640]{2,0,1:T(8,128)(2,1)S(1)}, u32[]{:S(2)}, u32[]{:S(2)}) async-start(bf16[112,8,640]{2,0,1:T(8,128)(2,1)} %bitcast.24), calls=%async_computation.1 | async-start | bytes 2293760 | tf_op jit(solution)/shard_map/all_to_all | solution.py:142
  23.8 28.3 %copy-start = (bf16[112,8,640]{2,0,1:T(8,128)(2,1)}, bf16[112,8,640]{2,0,1:T(8,128)(2,1)S(1)}, u32[]{:S(2)}) copy-start(bf16[112,8,640]{2,0,1:T(8,128)(2,1)S(1)} %all-to-all-done.1) | copy-start | bytes 3440644
  23.8 4.8 %copy-start.3 = (bf16[112,5120]{1,0:T(8,128)(2,1)S(1)}, bf16[112,5120]{1,0:T(8,128)(2,1)}, u32[]{:S(2)}) copy-start(bf16[112,5120]{1,0:T(8,128)(2,1)} %param.5) | copy-start | bytes 3440644
  23.8 19.8 %all-to-all-start.2 = ((bf16[112,8,640]{2,0,1:T(8,128)(2,1)}), bf16[112,8,640]{2,0,1:T(8,128)(2,1)S(1)}, u32[]{:S(2)}, u32[]{:S(2)}) async-start(bf16[112,8,640]{2,0,1:T(8,128)(2,1)} %bitcast.23), calls=%async_computation.2 | async-start | bytes 2293760 | tf_op jit(solution)/shard_map/all_to_all | solution.py:143
  43.6 6.1 %copy-start.1 = (bf16[112,8,640]{2,0,1:T(8,128)(2,1)}, bf16[112,8,640]{2,0,1:T(8,128)(2,1)S(1)}, u32[]{:S(2)}) copy-start(bf16[112,8,640]{2,0,1:T(8,128)(2,1)S(1)} %all-to-all-done.2) | copy-start | bytes 3440644
  43.6 4.8 %copy-start.5 = (s32[32]{0:T(128)S(1)}, s32[32]{0:T(128)}, u32[]{:S(2)}) copy-start(s32[32]{0:T(128)} %param.8) | copy-start | bytes 388
  43.7 24.7 %all-to-all-start = ((bf16[112,8,640]{2,0,1:T(8,128)(2,1)}), bf16[112,8,640]{2,0,1:T(8,128)(2,1)S(1)}, u32[]{:S(2)}, u32[]{:S(2)}) async-start(bf16[112,8,640]{2,0,1:T(8,128)(2,1)} %bitcast.25), calls=%async_computation | async-start | bytes 2293760 | tf_op jit(solution)/shard_map/all_to_all | solution.py:158
  49.8 6.7 %copy-start.6 = (s32[32]{0:T(128)S(1)}, s32[32]{0:T(128)}, u32[]{:S(2)}) copy-start(s32[32]{0:T(128)} %param.9) | copy-start | bytes 388
  50.7 10.7 %collective-permute-start.3 = (bf16[256,640]{1,0:T(8,128)(2,1)}, bf16[256,640]{1,0:T(8,128)(2,1)}, u32[]{:S(2)}, u32[]{:S(2)}) collective-permute-start(bf16[256,640]{1,0:T(8,128)(2,1)} %get-tuple-element.18), channel_id=1, source_target_pairs={{112,0},{240,128},{368,256},{113,1},{241,129},{369,257},{114,2},{2... | collective-permute-start | bytes 983048 | tf_op jit(solution)/shard_map/ppermute | solution.py:153
  52.2 36.7 %collective-permute-start = (bf16[512,640]{1,0:T(8,128)(2,1)S(1)}, bf16[512,640]{1,0:T(8,128)(2,1)}, u32[]{:S(2)}, u32[]{:S(2)}) collective-permute-start(bf16[512,640]{1,0:T(8,128)(2,1)S(1)} %constant_dynamic-slice_fusion.2), channel_id=1, source_target_pairs={{0,16},{16,32},{32,48},{48,64},{64,80},{80,96},{96,112},{112,128},... | collective-permute-start | bytes 1966088 | tf_op jit(solution)/shard_map/ppermute | solution.py:23
  57.2 23.6 %collective-permute-start.2 = (bf16[256,640]{1,0:T(8,128)(2,1)}, bf16[256,640]{1,0:T(8,128)(2,1)S(1)}, u32[]{:S(2)}, u32[]{:S(2)}) collective-permute-start(bf16[256,640]{1,0:T(8,128)(2,1)} %get-tuple-element.18), channel_id=1, source_target_pairs={{0,16},{16,32},{32,48},{48,64},{64,80},{80,96},{96,112},{128,144},... | collective-permute-start | bytes 983048 | tf_op jit(solution)/shard_map/ppermute | solution.py:152
  61.5 27.3 %collective-permute-start.4 = (bf16[256,640]{1,0:T(8,128)(2,1)}, bf16[256,640]{1,0:T(8,128)(2,1)S(1)}, u32[]{:S(2)}, u32[]{:S(2)}) collective-permute-start(bf16[256,640]{1,0:T(8,128)(2,1)} %collective-permute-done.3), channel_id=1, source_target_pairs={{0,128},{128,256},{256,384},{1,129},{129,257},{257,385},{2,130},{1... | collective-permute-start | bytes 983048 | tf_op jit(solution)/shard_map/ppermute | solution.py:152
  64.7 33.7 %collective-permute-start.1 = (bf16[256,640]{1,0:T(8,128)(2,1)}, bf16[256,640]{1,0:T(8,128)(2,1)S(1)}, u32[]{:S(2)}, u32[]{:S(2)}) collective-permute-start(bf16[256,640]{1,0:T(8,128)(2,1)} %get-tuple-element.17), channel_id=1, source_target_pairs={{0,16},{16,32},{32,48},{48,64},{64,80},{80,96},{96,112},{112,128},... | collective-permute-start | bytes 983048 | tf_op jit(solution)/shard_map/ppermute | solution.py:23
  68.4 1.0 copy-start.4

commit v6 on v5

--- a/solution.py
+++ b/solution.py
@@ -52,45 +52,31 @@
         tot_ref[:, h : h + 1] = both[:, HD : HD + 1]
 
 
-def mscore_kernel(counts, q_ref, mk_ref, w_ref, top_ref, tot_ref):
+def finish_kernel(
+    counts, q_ref, mk_ref, mv_ref, acc_ref, top_ref, tot_ref, o_ref
+):
+    own_live = counts[0] * FT
     mot_start = (MOT_CAP - counts[1]) * FT
     tail = mk_ref.shape[0]
     slot_live = lax.broadcasted_iota(jnp.int32, (1, tail), 1) >= mot_start
-    ones = jnp.ones((tail, HD), jnp.bfloat16)
-    for h in range(q_ref.shape[1] // HD):
-        c = head_cols(h)
-        masked = scaled_scores(q_ref[:, c], mk_ref[:, c], slot_live)
-        top = jnp.max(masked, axis=1, keepdims=True)
-        weights = jnp.exp(masked - top).astype(jnp.bfloat16)
-        w_ref[:, h * tail : (h + 1) * tail] = weights
-        total = jnp.dot(weights, ones, preferred_element_type=jnp.float32)
-        top_ref[:, h : h + 1] = top
-        tot_ref[:, h : h + 1] = total[:, 0:1]
-
-
-def merge_kernel(
-    counts, w_ref, mv_ref, acc_ref, top_ref, tot_ref, mtop_ref, mtot_ref, o_ref
-):
-    own_live = counts[0] * FT
-    tail = mv_ref.shape[0]
     rows = pl.program_id(0) * TQ + lax.broadcasted_iota(jnp.int32, (TQ, 1), 0)
     row_live = rows < own_live
     for h in range(o_ref.shape[1] // HD):
         c = head_cols(h)
-        acc_mot = jnp.dot(
-            w_ref[:, h * tail : (h + 1) * tail],
-            mv_ref[:, c],
-            preferred_element_type=jnp.float32,
-        )
+        masked = scaled_scores(q_ref[:, c], mk_ref[:, c], slot_live)
+        top_mot = jnp.max(masked, axis=1, keepdims=True)
+        weights = jnp.exp(masked - top_mot).astype(jnp.bfloat16)
+        mv = mv_ref[:, c]
+        mv_ext = jnp.concatenate([mv, jnp.ones_like(mv)], axis=1)
+        both = jnp.dot(weights, mv_ext, preferred_element_type=jnp.float32)
         top_own = top_ref[:, h : h + 1]
-        top_mot = mtop_ref[:, h : h + 1]
         peak = jnp.maximum(top_own, top_mot)
         factor_own = jnp.exp(top_own - peak)
         factor_mot = jnp.exp(top_mot - peak)
         scale = 1.0 / (
-            tot_ref[:, h : h + 1] * factor_own + mtot_ref[:, h : h + 1] * factor_mot
+            tot_ref[:, h : h + 1] * factor_own + both[:, HD : HD + 1] * factor_mot
         )
-        mixed = (acc_ref[:, c] * factor_own + acc_mot * factor_mot) * scale
+        mixed = (acc_ref[:, c] * factor_own + both[:, :HD] * factor_mot) * scale
         o_ref[:, c] = jnp.where(row_live, mixed, 0.0).astype(o_ref.dtype)
 
 
@@ -171,36 +157,23 @@
             bytes_accessed=3 * span * local * 2 + span * local * 4,
         ),
     )
-    w_mot, mtop, mtot = call(
-        mscore_kernel,
+    (mixed,) = call(
+        finish_kernel,
         counts,
-        (q_heads, k_prior),
-        [rows_of(local), whole(tail, local)],
-        [(heads * tail, jnp.bfloat16), (COLS, f32), (COLS, f32)],
-        pl.CostEstimate(
-            flops=heads * 2 * span * tail * 2 * HD,
-            transcendentals=heads * span * tail,
-            bytes_accessed=span * local * 2 + tail * local * 2 + span * heads * tail * 2,
-        ),
-    )
-    (mixed,) = call(
-        merge_kernel,
-        counts,
-        (w_mot, v_prior, acc, top, tot, mtop, mtot),
+        (q_heads, k_prior, v_prior, acc, top, tot),
         [
-            rows_of(heads * tail),
+            rows_of(local),
+            whole(tail, local),
             whole(tail, local),
             rows_of(local),
-            rows_of(COLS),
-            rows_of(COLS),
             rows_of(COLS),
             rows_of(COLS),
         ],
         [(local, jnp.bfloat16)],
         pl.CostEstimate(
-            flops=heads * 2 * span * tail * HD,
-            transcendentals=2 * heads * span,
-            bytes_accessed=span * heads * tail * 2 + span * local * 6 + tail * local * 2,
+            flops=heads * 2 * span * tail * 3 * HD,
+            transcendentals=heads * span * tail,
+            bytes_accessed=span * local * 8 + 2 * tail * local * 2,
         ),
     )
     return lax.all_to_all(mixed, "head", split_axis=0, concat_axis=1, tiled=True)

time: 141 us -> 146 us (1.035)
  blocking collectives: 33.1 us -> 36.5 us
  Pallas kernels: 25.8 us -> 22.9 us
  waiting for transfers between devices: 38.7 us -> 41.2 us
    all_to_all x1, blocking collectives: 33.1 us -> 36.5 us  [body(): lax.all_to_all(mixed, 'head', split_axis=0, concat_axis=1, tiled=True)]
    pallas_call x3 -> x2, Pallas kernels: 25.8 us -> 22.9 us  [call(): pl.pallas_call(kernel, out_shape=tuple(shapes), grid_spec=pltpu.PrefetchS...]
    ppermute x2, waiting for transfers between devices: 2.32 us -> 4.44 us  [from_behind(): return lax.ppermute(shard, axis, pairs)]
  transfers between devices with their start and end apart: 8 -> 8, of which waited for: 4 -> 4; matrix products, arithmetic and copies ran while one was open for 5% -> 6% of each run, Pallas kernels for 13% -> 8%
where the time goes in v6:
time: 146 us
  waiting for transfers between devices  41.2 us (28%)
  blocking collectives  36.5 us (25%)
  starting transfers between devices  31 us (21%)
  Pallas kernels  22.9 us (16%)
  local copies, waits for them, and re-layouts  9.72 us (7%)
  other arithmetic  3.73 us (3%)
    all_to_all x1, blocking collectives, body(): lax.all_to_all(mixed, 'head', split_axis=0, concat_axis=1, tiled=True)  36.5 us
    pallas_call x2, Pallas kernels, call(): pl.pallas_call(kernel, out_shape=tuple(shapes), grid_spec=pltpu.PrefetchS...  22.9 us
    all_to_all x1, waiting for transfers between devices, body(): lax.all_to_all(keys, 'head', split_axis=1, concat_axis=0, tiled=True)  14.5 us
    all_to_all x1, waiting for transfers between devices, body(): lax.all_to_all(values, 'head', split_axis=1, concat_axis=0, tiled=True)  13.9 us
    ppermute x2, starting transfers between devices, from_behind(): return lax.ppermute(shard, axis, pairs)  8.54 us
    ppermute x1, waiting for transfers between devices, body(): lax.ppermute(lax.ppermute(v_far, 'stretch', first), 'stretch', second)  8.4 us
    all_to_all x1, starting transfers between devices, body(): lax.all_to_all(keys, 'head', split_axis=1, concat_axis=0, tiled=True)  5.89 us
    all_to_all x1, starting transfers between devices, body(): lax.all_to_all(values, 'head', split_axis=1, concat_axis=0, tiled=True)  4.81 us
  transfers between devices with their start and end apart: 8, of which 4 were waited for; matrix products, arithmetic and copies ran while one was open for 6% of the time, Pallas kernels for 8%

profile of v6, /device:TPU:56, one launch (start us, length us, event | category | flops | bytes accessed | tf_op | source)
XLA Modules:
  0.0 145.7 jit_solution(13331968653984711722)
XLA Ops:
  0.0 2.4 %copy.18 = bf16[14,8,8,640]{3,2,0,1:T(8,128)(2,1)} copy(bf16[14,8,8,640]{3,2,1,0:T(8,128)(2,1)} %bitcast.34) | data formatting | bytes 2293760 | tf_op jit(solution)/shard_map/all_to_all | solution.py:128
  2.4 5.9 %all-to-all-start.1 = ((bf16[112,8,640]{2,0,1:T(8,128)(2,1)}), bf16[112,8,640]{2,0,1:T(8,128)(2,1)S(1)}, u32[]{:S(2)}, u32[]{:S(2)}) async-start(bf16[112,8,640]{2,0,1:T(8,128)(2,1)} %bitcast.24), calls=%async_computation.1 | async-start | bytes 2293760 | tf_op jit(solution)/shard_map/all_to_all | solution.py:128
  8.3 1.1 copy.17
  9.4 14.5 %all-to-all-done.1 = bf16[112,8,640]{2,0,1:T(8,128)(2,1)S(1)} async-done(((bf16[112,8,640]{2,0,1:T(8,128)(2,1)}), bf16[112,8,640]{2,0,1:T(8,128)(2,1)S(1)}, u32[]{:S(2)}, u32[]{:S(2)}) %all-to-all-start.1) | async-done | bytes 1146912 | tf_op jit(solution)/shard_map/all_to_all | solution.py:128
  23.8 4.8 %all-to-all-start.2 = ((bf16[112,8,640]{2,0,1:T(8,128)(2,1)}), bf16[112,8,640]{2,0,1:T(8,128)(2,1)S(1)}, u32[]{:S(2)}, u32[]{:S(2)}) async-start(bf16[112,8,640]{2,0,1:T(8,128)(2,1)} %bitcast.23), calls=%async_computation.2 | async-start | bytes 2293760 | tf_op jit(solution)/shard_map/all_to_all | solution.py:129
  28.7 1.1 copy.19
  29.8 13.9 %all-to-all-done.2 = bf16[112,8,640]{2,0,1:T(8,128)(2,1)S(1)} async-done(((bf16[112,8,640]{2,0,1:T(8,128)(2,1)}), bf16[112,8,640]{2,0,1:T(8,128)(2,1)S(1)}, u32[]{:S(2)}, u32[]{:S(2)}) %all-to-all-start.2) | async-done | bytes 1146912 | tf_op jit(solution)/shard_map/all_to_all | solution.py:129
  43.7 4.8 %all-to-all-start = ((bf16[112,8,640]{2,0,1:T(8,128)(2,1)}), bf16[112,8,640]{2,0,1:T(8,128)(2,1)S(1)}, u32[]{:S(2)}, u32[]{:S(2)}) async-start(bf16[112,8,640]{2,0,1:T(8,128)(2,1)} %bitcast.25), calls=%async_computation | async-start | bytes 2293760 | tf_op jit(solution)/shard_map/all_to_all | solution.py:144
  49.6 0.9 constant_dynamic-slice_fusion
  50.5 1.4 collective-permute-start.3
  51.9 4.3 %collective-permute-start = (bf16[512,640]{1,0:T(8,128)(2,1)S(1)}, bf16[512,640]{1,0:T(8,128)(2,1)S(1)}, u32[]{:S(2)}, u32[]{:S(2)}) collective-permute-start(bf16[512,640]{1,0:T(8,128)(2,1)S(1)} %constant_dynamic-slice_fusion.2), channel_id=1, source_target_pairs={{0,16},{16,32},{32,48},{48,64},{64,80},{80,96},{96,112},{112,128},... | collective-permute-start | bytes 1966088 | tf_op jit(solution)/shard_map/ppermute | solution.py:23
  56.8 4.3 %collective-permute-start.2 = (bf16[256,640]{1,0:T(8,128)(2,1)}, bf16[256,640]{1,0:T(8,128)(2,1)S(1)}, u32[]{:S(2)}, u32[]{:S(2)}) collective-permute-start(bf16[256,640]{1,0:T(8,128)(2,1)} %get-tuple-element.12), channel_id=1, source_target_pairs={{0,16},{16,32},{32,48},{48,64},{64,80},{80,96},{96,112},{128,144},... | collective-permute-start | bytes 983048 | tf_op jit(solution)/shard_map/ppermute | solution.py:138
  61.1 4.3 %collective-permute-start.1 = (bf16[256,640]{1,0:T(8,128)(2,1)}, bf16[256,640]{1,0:T(8,128)(2,1)S(1)}, u32[]{:S(2)}, u32[]{:S(2)}) collective-permute-start(bf16[256,640]{1,0:T(8,128)(2,1)} %get-tuple-element.11), channel_id=1, source_target_pairs={{0,16},{16,32},{32,48},{48,64},{64,80},{80,96},{96,112},{112,128},... | collective-permute-start | bytes 983048 | tf_op jit(solution)/shard_map/ppermute | solution.py:23
  65.4 1.3 collective-permute-start.4
  66.7 1.8 %pad_add_fusion.counts = s32[2]{0:T(128)} fusion(s32[1]{0:T(128)} %dynamic_slice.13, s32[1]{0:T(128)} %dynamic_slice.12), kind=kLoop, calls=%fused_computation.7 | loop fusion | flops 2 | bytes 16 | tf_op jit(solution)/shard_map/stack | solution.py:126
  68.5 1.0 copy-done
  69.5 11.3 %shard_map.55 = (f32[896,640]{1,0:T(8,128)}, f32[896,8]{1,0:T(8,128)}, f32[896,8]{1,0:T(8,128)}) custom-call(s32[2]{0:T(128)} %pad_add_fusion.counts, bf16[896,640]{1,0:T(8,128)(2,1)} %bitcast.26, bf16[896,640]{1,0:T(8,128)(2,1)} %bitcast.31, bf16[896,640]{1,0:T(8,128)(2,1)} %bitcast.33), custom_call_target="tpu_custom_call" | custom-call | flops 3082813440 | bytes 5734400 | tf_op jit(solution)/shard_map/pallas_call | solution.py:94
  80.8 8.4 %collective-permute-done.4 = bf16[256,640]{1,0:T(8,128)(2,1)} collective-permute-done((bf16[256,640]{1,0:T(8,128)(2,1)}, bf16[256,640]{1,0:T(8,128)(2,1)}, u32[]{:S(2)}, u32[]{:S(2)}) %collective-permute-start.4) | collective-permute-done | bytes 327712 | tf_op jit(solution)/shard_map/ppermute | solution.py:138
  89.2 1.1 add.15
  90.2 4.4 %collective-permute-done.1 = bf16[256,640]{1,0:T(8,128)(2,1)S(1)} collective-permute-done((bf16[256,640]{1,0:T(8,128)(2,1)}, bf16[256,640]{1,0:T(8,128)(2,1)S(1)}, u32[]{:S(2)}, u32[]{:S(2)}) %collective-permute-start.1) | collective-permute-done | bytes 327712 | tf_op jit(solution)/shard_map/ppermute | solution.py:23
  94.7 0.9 pad_maximum_fusion.mv_ref
  96.4 11.6 %shard_map.56 = bf16[896,640]{1,0:T(8,128)(2,1)} custom-call(s32[2]{0:T(128)} %pad_add_fusion.counts, bf16[896,640]{1,0:T(8,128)(2,1)} %bitcast.27, bf16[512,640]{1,0:T(8,128)(2,1)} %copy-done.5, bf16[512,640]{1,0:T(8,128)(2,1)} %pad_maximum_fusion.mv_ref, f32[896,640]{1,0:T(8,128)} %get-tuple-element.8.acc_ref, f32[896,8]{1,0:T(8,128)} %get-tuple-element.9.top_ref, ...), custom_call_target="tpu_custom_call" | custom-call | flops 1761607680 | bytes 5898240 | tf_op jit(solution)/shard_map/pallas_call | solution.py:94
  108.1 36.5 %all_to_all.76 = bf16[8,112,640]{2,1,0:T(8,128)(2,1)S(1)} all-to-all(bf16[8,112,640]{2,1,0:T(8,128)(2,1)} %bitcast.28), channel_id=1, replica_groups=mesh['stretch'=32,'head'=8,'cfg'=2] {'head'}, dimensions={0} | all-to-all | bytes 2293760 | tf_op jit(solution)/shard_map/all_to_all | solution.py:179
  144.6 1.2 copy.13
  (22 shorter events, 2.1 us)
Async XLA Ops:
  2.4 5.9 %copy-start.3 = (bf16[112,5120]{1,0:T(8,128)(2,1)S(1)}, bf16[112,5120]{1,0:T(8,128)(2,1)}, u32[]{:S(2)}) copy-start(bf16[112,5120]{1,0:T(8,128)(2,1)} %param.7) | copy-start | bytes 3440644
  2.4 21.5 %all-to-all-start.1 = ((bf16[112,8,640]{2,0,1:T(8,128)(2,1)}), bf16[112,8,640]{2,0,1:T(8,128)(2,1)S(1)}, u32[]{:S(2)}, u32[]{:S(2)}) async-start(bf16[112,8,640]{2,0,1:T(8,128)(2,1)} %bitcast.24), calls=%async_computation.1 | async-start | bytes 2293760 | tf_op jit(solution)/shard_map/all_to_all | solution.py:128
  23.8 28.0 %copy-start.1 = (bf16[112,8,640]{2,0,1:T(8,128)(2,1)}, bf16[112,8,640]{2,0,1:T(8,128)(2,1)S(1)}, u32[]{:S(2)}) copy-start(bf16[112,8,640]{2,0,1:T(8,128)(2,1)S(1)} %all-to-all-done.1) | copy-start | bytes 3440644
  23.8 4.8 %copy-start.4 = (bf16[112,5120]{1,0:T(8,128)(2,1)S(1)}, bf16[112,5120]{1,0:T(8,128)(2,1)}, u32[]{:S(2)}) copy-start(bf16[112,5120]{1,0:T(8,128)(2,1)} %param.5) | copy-start | bytes 3440644
  23.8 19.8 %all-to-all-start.2 = ((bf16[112,8,640]{2,0,1:T(8,128)(2,1)}), bf16[112,8,640]{2,0,1:T(8,128)(2,1)S(1)}, u32[]{:S(2)}, u32[]{:S(2)}) async-start(bf16[112,8,640]{2,0,1:T(8,128)(2,1)} %bitcast.23), calls=%async_computation.2 | async-start | bytes 2293760 | tf_op jit(solution)/shard_map/all_to_all | solution.py:129
  43.6 5.9 %copy-start.2 = (bf16[112,8,640]{2,0,1:T(8,128)(2,1)}, bf16[112,8,640]{2,0,1:T(8,128)(2,1)S(1)}, u32[]{:S(2)}) copy-start(bf16[112,8,640]{2,0,1:T(8,128)(2,1)S(1)} %all-to-all-done.2) | copy-start | bytes 3440644
  43.6 4.8 %copy-start.6 = (s32[32]{0:T(128)S(1)}, s32[32]{0:T(128)}, u32[]{:S(2)}) copy-start(s32[32]{0:T(128)} %param.8) | copy-start | bytes 388
  43.7 24.8 %all-to-all-start = ((bf16[112,8,640]{2,0,1:T(8,128)(2,1)}), bf16[112,8,640]{2,0,1:T(8,128)(2,1)S(1)}, u32[]{:S(2)}, u32[]{:S(2)}) async-start(bf16[112,8,640]{2,0,1:T(8,128)(2,1)} %bitcast.25), calls=%async_computation | async-start | bytes 2293760 | tf_op jit(solution)/shard_map/all_to_all | solution.py:144
  49.5 6.7 %copy-start.7 = (s32[32]{0:T(128)S(1)}, s32[32]{0:T(128)}, u32[]{:S(2)}) copy-start(s32[32]{0:T(128)} %param.9) | copy-start | bytes 388
  50.5 14.9 %collective-permute-start.3 = (bf16[256,640]{1,0:T(8,128)(2,1)}, bf16[256,640]{1,0:T(8,128)(2,1)}, u32[]{:S(2)}, u32[]{:S(2)}) collective-permute-start(bf16[256,640]{1,0:T(8,128)(2,1)} %get-tuple-element.12), channel_id=1, source_target_pairs={{112,0},{240,128},{368,256},{113,1},{241,129},{369,257},{114,2},{2... | collective-permute-start | bytes 983048 | tf_op jit(solution)/shard_map/ppermute | solution.py:139
  51.9 43.7 %collective-permute-start = (bf16[512,640]{1,0:T(8,128)(2,1)S(1)}, bf16[512,640]{1,0:T(8,128)(2,1)S(1)}, u32[]{:S(2)}, u32[]{:S(2)}) collective-permute-start(bf16[512,640]{1,0:T(8,128)(2,1)S(1)} %constant_dynamic-slice_fusion.2), channel_id=1, source_target_pairs={{0,16},{16,32},{32,48},{48,64},{64,80},{80,96},{96,112},{112,128},... | collective-permute-start | bytes 1966088 | tf_op jit(solution)/shard_map/ppermute | solution.py:23
  56.8 24.0 %collective-permute-start.2 = (bf16[256,640]{1,0:T(8,128)(2,1)}, bf16[256,640]{1,0:T(8,128)(2,1)S(1)}, u32[]{:S(2)}, u32[]{:S(2)}) collective-permute-start(bf16[256,640]{1,0:T(8,128)(2,1)} %get-tuple-element.12), channel_id=1, source_target_pairs={{0,16},{16,32},{32,48},{48,64},{64,80},{80,96},{96,112},{128,144},... | collective-permute-start | bytes 983048 | tf_op jit(solution)/shard_map/ppermute | solution.py:138
  61.1 33.6 %collective-permute-start.1 = (bf16[256,640]{1,0:T(8,128)(2,1)}, bf16[256,640]{1,0:T(8,128)(2,1)S(1)}, u32[]{:S(2)}, u32[]{:S(2)}) collective-permute-start(bf16[256,640]{1,0:T(8,128)(2,1)} %get-tuple-element.11), channel_id=1, source_target_pairs={{0,16},{16,32},{32,48},{48,64},{64,80},{80,96},{96,112},{112,128},... | collective-permute-start | bytes 983048 | tf_op jit(solution)/shard_map/ppermute | solution.py:23
  65.4 23.8 %collective-permute-start.4 = (bf16[256,640]{1,0:T(8,128)(2,1)}, bf16[256,640]{1,0:T(8,128)(2,1)}, u32[]{:S(2)}, u32[]{:S(2)}) collective-permute-start(bf16[256,640]{1,0:T(8,128)(2,1)} %collective-permute-done.3), channel_id=1, source_target_pairs={{0,128},{128,256},{256,384},{1,129},{129,257},{257,385},{2,130},{1... | collective-permute-start | bytes 983048 | tf_op jit(solution)/shard_map/ppermute | solution.py:138
  68.5 1.0 copy-start
  95.6 0.9 copy-start.5

commit v7 on v5

--- a/solution.py
+++ b/solution.py
@@ -139,8 +139,17 @@
     count_own = frames[stretch_index]
     counts = jnp.stack([count_own, motion[stretch_index]]).astype(jnp.int32)
     tail_begin = (count_own - MOT_CAP) * FT
-    k_heads = lax.all_to_all(keys, "head", split_axis=1, concat_axis=0, tiled=True)
-    v_heads = lax.all_to_all(values, "head", split_axis=1, concat_axis=0, tiled=True)
+    groups = lax.axis_size("head")
+    rows, width = keys.shape
+    local = width // groups
+
+    def by_target(x):
+        return x.reshape(rows, groups, local).transpose(1, 0, 2)
+
+    kv_send = jnp.stack([by_target(keys), by_target(values)], axis=1)
+    kv_recv = lax.all_to_all(kv_send, "head", split_axis=0, concat_axis=0, tiled=True)
+    kv_rows = kv_recv.transpose(1, 0, 2, 3).reshape(2, groups * rows, local)
+    k_heads, v_heads = kv_rows[0], kv_rows[1]
     k_tail = lax.dynamic_slice_in_dim(k_heads, tail_begin, tail, 0)
     v_tail = lax.dynamic_slice_in_dim(v_heads, tail_begin, tail, 0)
     k_prior = from_behind(k_tail, "stretch", 1)

time: 141 us -> 136 us (0.965)
  starting transfers between devices: 30.4 us -> 26.2 us
  local copies, waits for them, and re-layouts: 9.06 us -> 7.2 us
    all_to_all x2 -> x1, starting transfers between devices: 10.7 us -> 5.89 us  [body(): lax.all_to_all(kv_send, 'head', split_axis=0, concat_axis=0, tiled=True)]
    ppermute x1, waiting for transfers between devices: 8.02 us -> 12 us  [body(): lax.ppermute(lax.ppermute(v_far, 'stretch', first), 'stretch', second)]
    all_to_all x2 -> x0, local copies, waits for them, and re-layouts: 3.47 us -> none  [the longest x1 2.36 us: body(): lax.all_to_all(keys, 'head', split_axis=1, concat_axis=0, tiled=True)]
    ppermute x2, waiting for transfers between devices: 2.32 us -> 0.01 us  [from_behind(): return lax.ppermute(shard, axis, pairs)]
    another operation x0 -> x1, local copies, waits for them, and re-layouts: none -> 1.7 us  [body(): kv_send = jnp.stack([by_target(keys), by_target(values)], axis=1)]
    all_to_all x2 -> x1, waiting for transfers between devices: 28.4 us -> 26.8 us  [body(): lax.all_to_all(kv_send, 'head', split_axis=0, concat_axis=0, tiled=True)]
  transfers between devices with their start and end apart: 8 -> 7, of which waited for: 4 -> 2; matrix products, arithmetic and copies ran while one was open for 5% -> 3% of each run, Pallas kernels for 13% -> 14%
where the time goes in v7:
time: 136 us
  waiting for transfers between devices  38.8 us (29%)
  blocking collectives  34 us (25%)
  starting transfers between devices  26.2 us (19%)
  Pallas kernels  25.8 us (19%)
  local copies, waits for them, and re-layouts  7.2 us (5%)
  other arithmetic  2.92 us (2%)
    all_to_all x1, blocking collectives, body(): lax.all_to_all(mixed, 'head', split_axis=0, concat_axis=1, tiled=True)  34 us
    all_to_all x1, waiting for transfers between devices, body(): lax.all_to_all(kv_send, 'head', split_axis=0, concat_axis=0, tiled=True)  26.8 us
    pallas_call x3, Pallas kernels, call(): pl.pallas_call(kernel, out_shape=tuple(shapes), grid_spec=pltpu.PrefetchS...  25.8 us
    ppermute x1, waiting for transfers between devices, body(): lax.ppermute(lax.ppermute(v_far, 'stretch', first), 'stretch', second)  12 us
    ppermute x2, starting transfers between devices, from_behind(): return lax.ppermute(shard, axis, pairs)  8.55 us
    all_to_all x1, starting transfers between devices, body(): lax.all_to_all(kv_send, 'head', split_axis=0, concat_axis=0, tiled=True)  5.89 us
    all_to_all x1, starting transfers between devices, body(): lax.all_to_all(queries, 'head', split_axis=1, concat_axis=0, tiled=True)  5.49 us
    ppermute x1, starting transfers between devices, body(): lax.ppermute(v_far, 'stretch', inner)  4.28 us
  transfers between devices with their start and end apart: 7, of which 2 were waited for; matrix products, arithmetic and copies ran while one was open for 3% of the time, Pallas kernels for 14%

profile of v7, /device:TPU:56, one launch (start us, length us, event | category | flops | bytes accessed | tf_op | source)
XLA Modules:
  0.0 135.6 jit_solution(6575972117172860309)
XLA Ops:
  0.0 1.5 %copy.17 = bf16[14,8,8,640]{3,2,1,0:T(8,128)(2,1)S(1)} copy(bf16[14,8,8,640]{3,1,2,0:T(8,128)(2,1)} %bitcast.36) | data formatting | bytes 2293760
  1.6 0.2 copy.18
  1.8 0.2 pad_maximum_fusion
  2.0 1.7 %copy.13 = bf16[8,2,112,640]{3,2,1,0:T(8,128)(2,1)} copy(bf16[8,2,112,640]{3,0,2,1:T(8,128)(2,1)S(1)} %pad_maximum_fusion) | data formatting | bytes 4587520 | tf_op jit(solution)/shard_map/stack | solution.py:149
  3.7 5.9 %all-to-all-start.1 = ((bf16[8,2,112,640]{3,2,1,0:T(8,128)(2,1)}), bf16[8,2,112,640]{3,2,1,0:T(8,128)(2,1)S(1)}, u32[]{:S(2)}, u32[]{:S(2)}) async-start(bf16[8,2,112,640]{3,2,1,0:T(8,128)(2,1)} %copy.13), calls=%async_computation.1 | async-start | bytes 4587520 | tf_op jit(solution)/shard_map/all_to_all | solution.py:150
  9.6 1.1 copy.20
  10.7 26.8 %all-to-all-done.1 = bf16[8,2,112,640]{3,2,1,0:T(8,128)(2,1)S(1)} async-done(((bf16[8,2,112,640]{3,2,1,0:T(8,128)(2,1)}), bf16[8,2,112,640]{3,2,1,0:T(8,128)(2,1)S(1)}, u32[]{:S(2)}, u32[]{:S(2)}) %all-to-all-start.1) | async-done | bytes 2293792 | tf_op jit(solution)/shard_map/all_to_all | solution.py:150
  37.5 5.5 %all-to-all-start = ((bf16[112,8,640]{2,0,1:T(8,128)(2,1)}), bf16[112,8,640]{2,0,1:T(8,128)(2,1)}, u32[]{:S(2)}, u32[]{:S(2)}) async-start(bf16[112,8,640]{2,0,1:T(8,128)(2,1)} %bitcast.26), calls=%async_computation | async-start | bytes 2293760 | tf_op jit(solution)/shard_map/all_to_all | solution.py:167
  43.0 0.6 dynamic_slice.12
  44.1 0.2 fusion
  44.4 4.3 %collective-permute-start = (bf16[512,640]{1,0:T(8,128)(2,1)S(1)}, bf16[512,640]{1,0:T(8,128)(2,1)}, u32[]{:S(2)}, u32[]{:S(2)}) collective-permute-start(bf16[512,640]{1,0:T(8,128)(2,1)S(1)} %constant_dynamic-slice_fusion.2), channel_id=1, source_target_pairs={{0,16},{16,32},{32,48},{48,64},{64,80},{80,96},{96,112},{112,128},... | collective-permute-start | bytes 1966088 | tf_op jit(solution)/shard_map/ppermute | solution.py:23
  48.8 0.7 collective-permute-start.3
  49.5 0.6 dynamic_slice.13
  50.1 1.7 %pad_add_fusion.counts = s32[2]{0:T(128)} fusion(s32[1]{0:T(128)} %dynamic_slice.13, s32[1]{0:T(128)} %dynamic_slice.12), kind=kLoop, calls=%fused_computation.6 | loop fusion | flops 2 | bytes 16 | tf_op jit(solution)/shard_map/stack | solution.py:140
  51.8 4.3 %collective-permute-start.2 = (bf16[256,640]{1,0:T(8,128)(2,1)S(1)}, bf16[256,640]{1,0:T(8,128)(2,1)S(1)}, u32[]{:S(2)}, u32[]{:S(2)}) collective-permute-start(bf16[256,640]{1,0:T(8,128)(2,1)S(1)} %get-tuple-element.20), channel_id=1, source_target_pairs={{0,16},{16,32},{32,48},{48,64},{64,80},{80,96},{96,112},{128,144},... | collective-permute-start | bytes 983048 | tf_op jit(solution)/shard_map/ppermute | solution.py:161
  56.1 4.3 %collective-permute-start.1 = (bf16[256,640]{1,0:T(8,128)(2,1)S(1)}, bf16[256,640]{1,0:T(8,128)(2,1)S(1)}, u32[]{:S(2)}, u32[]{:S(2)}) collective-permute-start(bf16[256,640]{1,0:T(8,128)(2,1)S(1)} %get-tuple-element.19), channel_id=1, source_target_pairs={{0,16},{16,32},{32,48},{48,64},{64,80},{80,96},{96,112},{112,128},... | collective-permute-start | bytes 983048 | tf_op jit(solution)/shard_map/ppermute | solution.py:23
  60.4 1.3 collective-permute-start.4
  61.7 11.3 %shard_map.56 = (f32[896,640]{1,0:T(8,128)}, f32[896,8]{1,0:T(8,128)}, f32[896,8]{1,0:T(8,128)}) custom-call(s32[2]{0:T(128)} %pad_add_fusion.counts, bf16[896,640]{1,0:T(8,128)(2,1)} %bitcast.1.q_ref, bf16[896,640]{1,0:T(8,128)(2,1)} %bitcast.33, bf16[896,640]{1,0:T(8,128)(2,1)} %bitcast.35), custom_call_target="tpu_custom_call" | custom-call | flops 3082813440 | bytes 5734400 | tf_op jit(solution)/shard_map/pallas_call | solution.py:108
  73.0 7.2 %shard_map.55 = (bf16[896,2560]{1,0:T(8,128)(2,1)}, f32[896,8]{1,0:T(8,128)}, f32[896,8]{1,0:T(8,128)}) custom-call(s32[2]{0:T(128)} %pad_add_fusion.counts, bf16[896,640]{1,0:T(8,128)(2,1)} %bitcast.1.q_ref, bf16[512,640]{1,0:T(8,128)(2,1)} %collective-permute-done.mk_ref), custom_call_target="tpu_custom_call" | custom-call | flops 1174405120 | bytes 6389760 | tf_op jit(solution)/shard_map/pallas_call | solution.py:108
  80.2 12.0 %collective-permute-done.4 = bf16[256,640]{1,0:T(8,128)(2,1)S(1)} collective-permute-done((bf16[256,640]{1,0:T(8,128)(2,1)S(1)}, bf16[256,640]{1,0:T(8,128)(2,1)S(1)}, u32[]{:S(2)}, u32[]{:S(2)}) %collective-permute-start.4) | collective-permute-done | bytes 327712 | tf_op jit(solution)/shard_map/ppermute | solution.py:161
  92.3 0.9 pad_maximum_fusion.1.mv_ref
  93.2 7.2 %shard_map.57 = bf16[896,640]{1,0:T(8,128)(2,1)} custom-call(s32[2]{0:T(128)} %pad_add_fusion.counts, bf16[896,2560]{1,0:T(8,128)(2,1)} %get-tuple-element.11.w_ref, bf16[512,640]{1,0:T(8,128)(2,1)} %pad_maximum_fusion.1.mv_ref, f32[896,640]{1,0:T(8,128)} %get-tuple-element.12.acc_ref, f32[896,8]{1,0:T(8,128)} %get-tuple-element.13.top_ref, ...), custom_call_target="tpu_custom_call" | custom-call | flops 587202560 | bytes 8683520 | tf_op jit(solution)/shard_map/pallas_call | solution.py:108
  100.4 34.0 %all_to_all.43 = bf16[8,112,640]{2,1,0:T(8,128)(2,1)S(1)} all-to-all(bf16[8,112,640]{2,1,0:T(8,128)(2,1)} %bitcast.31), channel_id=1, replica_groups=mesh['stretch'=32,'head'=8,'cfg'=2] {'head'}, dimensions={0} | all-to-all | bytes 2293760 | tf_op jit(solution)/shard_map/all_to_all | solution.py:215
  134.4 1.2 copy.16
  (20 shorter events, 0.3 us)
Async XLA Ops:
  0.0 1.6 %copy-start.2 = (bf16[112,5120]{1,0:T(8,128)(2,1)S(1)}, bf16[112,5120]{1,0:T(8,128)(2,1)}, u32[]{:S(2)}) copy-start(bf16[112,5120]{1,0:T(8,128)(2,1)} %param.7) | copy-start | bytes 3440644
  3.7 5.9 %copy-start.3 = (bf16[112,5120]{1,0:T(8,128)(2,1)S(1)}, bf16[112,5120]{1,0:T(8,128)(2,1)}, u32[]{:S(2)}) copy-start(bf16[112,5120]{1,0:T(8,128)(2,1)} %param.5) | copy-start | bytes 3440644
  3.7 33.8 %all-to-all-start.1 = ((bf16[8,2,112,640]{3,2,1,0:T(8,128)(2,1)}), bf16[8,2,112,640]{3,2,1,0:T(8,128)(2,1)S(1)}, u32[]{:S(2)}, u32[]{:S(2)}) async-start(bf16[8,2,112,640]{3,2,1,0:T(8,128)(2,1)} %copy.13), calls=%async_computation.1 | async-start | bytes 4587520 | tf_op jit(solution)/shard_map/all_to_all | solution.py:150
  37.5 5.5 %copy-start.4 = (s32[32]{0:T(128)S(1)}, s32[32]{0:T(128)}, u32[]{:S(2)}) copy-start(s32[32]{0:T(128)} %param.8) | copy-start | bytes 388
  37.5 24.2 %all-to-all-start = ((bf16[112,8,640]{2,0,1:T(8,128)(2,1)}), bf16[112,8,640]{2,0,1:T(8,128)(2,1)}, u32[]{:S(2)}, u32[]{:S(2)}) async-start(bf16[112,8,640]{2,0,1:T(8,128)(2,1)} %bitcast.26), calls=%async_computation | async-start | bytes 2293760 | tf_op jit(solution)/shard_map/all_to_all | solution.py:167
  44.3 4.5 %copy-start = (bf16[1,8,112,640]{3,2,0,1:T(8,128)(2,1)}, bf16[1,8,112,640]{3,2,0,1:T(8,128)(2,1)S(1)}, u32[]{:S(2)}) copy-start(bf16[1,8,112,640]{3,2,0,1:T(8,128)(2,1)S(1)} %get-tuple-element.18) | copy-start | bytes 3440644
  44.3 4.5 %copy-start.1 = (bf16[1,8,112,640]{3,2,0,1:T(8,128)(2,1)}, bf16[1,8,112,640]{3,2,0,1:T(8,128)(2,1)S(1)}, u32[]{:S(2)}) copy-start(bf16[1,8,112,640]{3,2,0,1:T(8,128)(2,1)S(1)} %get-tuple-element.17) | copy-start | bytes 3440644
  44.3 5.2 %copy-start.5 = (s32[32]{0:T(128)S(1)}, s32[32]{0:T(128)}, u32[]{:S(2)}) copy-start(s32[32]{0:T(128)} %param.9) | copy-start | bytes 388
  44.4 28.6 %collective-permute-start = (bf16[512,640]{1,0:T(8,128)(2,1)S(1)}, bf16[512,640]{1,0:T(8,128)(2,1)}, u32[]{:S(2)}, u32[]{:S(2)}) collective-permute-start(bf16[512,640]{1,0:T(8,128)(2,1)S(1)} %constant_dynamic-slice_fusion.2), channel_id=1, source_target_pairs={{0,16},{16,32},{32,48},{48,64},{64,80},{80,96},{96,112},{112,128},... | collective-permute-start | bytes 1966088 | tf_op jit(solution)/shard_map/ppermute | solution.py:23
  48.8 11.6 %collective-permute-start.3 = (bf16[256,640]{1,0:T(8,128)(2,1)S(1)}, bf16[256,640]{1,0:T(8,128)(2,1)S(1)}, u32[]{:S(2)}, u32[]{:S(2)}) collective-permute-start(bf16[256,640]{1,0:T(8,128)(2,1)S(1)} %get-tuple-element.20), channel_id=1, source_target_pairs={{112,0},{240,128},{368,256},{113,1},{241,129},{369,257},{114,2},{2... | collective-permute-start | bytes 983048 | tf_op jit(solution)/shard_map/ppermute | solution.py:162
  51.8 28.4 %collective-permute-start.2 = (bf16[256,640]{1,0:T(8,128)(2,1)S(1)}, bf16[256,640]{1,0:T(8,128)(2,1)S(1)}, u32[]{:S(2)}, u32[]{:S(2)}) collective-permute-start(bf16[256,640]{1,0:T(8,128)(2,1)S(1)} %get-tuple-element.20), channel_id=1, source_target_pairs={{0,16},{16,32},{32,48},{48,64},{64,80},{80,96},{96,112},{128,144},... | collective-permute-start | bytes 983048 | tf_op jit(solution)/shard_map/ppermute | solution.py:161
  56.1 36.2 %collective-permute-start.1 = (bf16[256,640]{1,0:T(8,128)(2,1)S(1)}, bf16[256,640]{1,0:T(8,128)(2,1)S(1)}, u32[]{:S(2)}, u32[]{:S(2)}) collective-permute-start(bf16[256,640]{1,0:T(8,128)(2,1)S(1)} %get-tuple-element.19), channel_id=1, source_target_pairs={{0,16},{16,32},{32,48},{48,64},{64,80},{80,96},{96,112},{112,128},... | collective-permute-start | bytes 983048 | tf_op jit(solution)/shard_map/ppermute | solution.py:23
  60.4 31.9 %collective-permute-start.4 = (bf16[256,640]{1,0:T(8,128)(2,1)S(1)}, bf16[256,640]{1,0:T(8,128)(2,1)S(1)}, u32[]{:S(2)}, u32[]{:S(2)}) collective-permute-start(bf16[256,640]{1,0:T(8,128)(2,1)S(1)} %collective-permute-done.3), channel_id=1, source_target_pairs={{0,128},{128,256},{256,384},{1,129},{129,257},{257,385},{2,130},{1... | collective-permute-start | bytes 983048 | tf_op jit(solution)/shard_map/ppermute | solution.py:161

commit v8 on v7

--- a/solution.py
+++ b/solution.py
@@ -154,16 +154,12 @@
     v_tail = lax.dynamic_slice_in_dim(v_heads, tail_begin, tail, 0)
     k_prior = from_behind(k_tail, "stretch", 1)
     inner, first, second = plan
-    half = tail // 2
-    v_near = from_behind(v_tail[:half], "stretch", 1)
-    v_far = v_tail[half:]
     if first:
-        v_far = lax.ppermute(v_far, "stretch", inner) + lax.ppermute(
-            lax.ppermute(v_far, "stretch", first), "stretch", second
+        v_prior = lax.ppermute(v_tail, "stretch", inner) + lax.ppermute(
+            lax.ppermute(v_tail, "stretch", first), "stretch", second
         )
     else:
-        v_far = from_behind(v_far, "stretch", 1)
-    v_prior = jnp.concatenate([v_near, v_far], axis=0)
+        v_prior = from_behind(v_tail, "stretch", 1)
     q_heads = lax.all_to_all(queries, "head", split_axis=1, concat_axis=0, tiled=True)
     span, local = q_heads.shape
     heads = local // HD

time: 136 us -> 146 us (1.074)
  the two profiles are of different devices: /device:TPU:56 before, /device:TPU:40 now
where the time goes in v8:
time: 146 us; the launch traced here: 145 us
  waiting for transfers between devices  63.7 us (44%)
  Pallas kernels  25.8 us (18%)
  starting transfers between devices  23.4 us (16%)
  blocking collectives  21.3 us (15%)
  local copies, waits for them, and re-layouts  7.28 us (5%)
  other arithmetic  3.09 us (2%)
    ppermute x1, waiting for transfers between devices, body(): lax.ppermute(v_tail, 'stretch', first)  27.5 us
    all_to_all x1, waiting for transfers between devices, body(): lax.all_to_all(kv_send, 'head', split_axis=0, concat_axis=0, tiled=True)  26.8 us
    pallas_call x3, Pallas kernels, call(): pl.pallas_call(kernel, out_shape=tuple(shapes), grid_spec=pltpu.PrefetchS...  25.8 us
    all_to_all x1, blocking collectives, body(): lax.all_to_all(mixed, 'head', split_axis=0, concat_axis=1, tiled=True)  21.3 us
    ppermute x1, waiting for transfers between devices, body(): lax.ppermute(lax.ppermute(v_tail, 'stretch', first), 'stretch', second)  9.41 us
    all_to_all x1, starting transfers between devices, body(): lax.all_to_all(kv_send, 'head', split_axis=0, concat_axis=0, tiled=True)  5.89 us
    all_to_all x1, starting transfers between devices, body(): lax.all_to_all(queries, 'head', split_axis=1, concat_axis=0, tiled=True)  5.47 us
    ppermute x1, starting transfers between devices, from_behind(): return lax.ppermute(shard, axis, pairs)  4.54 us
  transfers between devices with their start and end apart: 6, of which 3 were waited for; matrix products, arithmetic and copies ran while one was open for 3% of the time, Pallas kernels for 13%

profile of v8, /device:TPU:40, one launch (start us, length us, event | category | flops | bytes accessed | tf_op | source)
XLA Modules:
  0.0 145.3 jit_solution(5848996545927405617)
XLA Ops:
  0.0 1.5 %copy.17 = bf16[14,8,8,640]{3,2,1,0:T(8,128)(2,1)S(1)} copy(bf16[14,8,8,640]{3,1,2,0:T(8,128)(2,1)} %bitcast.36) | data formatting | bytes 2293760
  1.6 0.2 copy.18
  1.8 0.2 pad_maximum_fusion
  2.0 1.7 %copy.13 = bf16[8,2,112,640]{3,2,1,0:T(8,128)(2,1)} copy(bf16[8,2,112,640]{3,0,2,1:T(8,128)(2,1)S(1)} %pad_maximum_fusion) | data formatting | bytes 4587520 | tf_op jit(solution)/shard_map/stack | solution.py:149
  3.7 5.9 %all-to-all-start.1 = ((bf16[8,2,112,640]{3,2,1,0:T(8,128)(2,1)}), bf16[8,2,112,640]{3,2,1,0:T(8,128)(2,1)S(1)}, u32[]{:S(2)}, u32[]{:S(2)}) async-start(bf16[8,2,112,640]{3,2,1,0:T(8,128)(2,1)} %copy.13), calls=%async_computation.1 | async-start | bytes 4587520 | tf_op jit(solution)/shard_map/all_to_all | solution.py:150
  9.6 1.1 copy.20
  10.7 26.8 %all-to-all-done.1 = bf16[8,2,112,640]{3,2,1,0:T(8,128)(2,1)S(1)} async-done(((bf16[8,2,112,640]{3,2,1,0:T(8,128)(2,1)}), bf16[8,2,112,640]{3,2,1,0:T(8,128)(2,1)S(1)}, u32[]{:S(2)}, u32[]{:S(2)}) %all-to-all-start.1) | async-done | bytes 2293792 | tf_op jit(solution)/shard_map/all_to_all | solution.py:150
  37.5 5.5 %all-to-all-start = ((bf16[112,8,640]{2,0,1:T(8,128)(2,1)}), bf16[112,8,640]{2,0,1:T(8,128)(2,1)}, u32[]{:S(2)}, u32[]{:S(2)}) async-start(bf16[112,8,640]{2,0,1:T(8,128)(2,1)} %bitcast.26), calls=%async_computation | async-start | bytes 2293760 | tf_op jit(solution)/shard_map/all_to_all | solution.py:163
  43.0 0.6 dynamic_slice.12
  44.1 0.2 fusion
  44.4 1.3 collective-permute-start.2
  45.8 4.5 %collective-permute-start = (bf16[512,640]{1,0:T(8,128)(2,1)S(1)}, bf16[512,640]{1,0:T(8,128)(2,1)}, u32[]{:S(2)}, u32[]{:S(2)}) collective-permute-start(bf16[512,640]{1,0:T(8,128)(2,1)S(1)} %constant_dynamic-slice_fusion.1), channel_id=1, source_target_pairs={{0,16},{16,32},{32,48},{48,64},{64,80},{80,96},{96,112},{112,128},... | collective-permute-start | bytes 1966088 | tf_op jit(solution)/shard_map/ppermute | solution.py:23
  50.4 4.3 %collective-permute-start.1 = (bf16[512,640]{1,0:T(8,128)(2,1)S(1)}, bf16[512,640]{1,0:T(8,128)(2,1)S(1)}, u32[]{:S(2)}, u32[]{:S(2)}) collective-permute-start(bf16[512,640]{1,0:T(8,128)(2,1)S(1)} %constant_dynamic-slice_fusion), channel_id=1, source_target_pairs={{0,16},{16,32},{32,48},{48,64},{64,80},{80,96},{96,112},{128,144},... | collective-permute-start | bytes 1966088 | tf_op jit(solution)/shard_map/ppermute | solution.py:158
  54.7 27.5 %collective-permute-done.2 = bf16[512,640]{1,0:T(8,128)(2,1)} collective-permute-done((bf16[512,640]{1,0:T(8,128)(2,1)S(1)}, bf16[512,640]{1,0:T(8,128)(2,1)}, u32[]{:S(2)}, u32[]{:S(2)}) %collective-permute-start.2) | collective-permute-done | bytes 655392 | tf_op jit(solution)/shard_map/ppermute | solution.py:159
  82.2 1.9 %collective-permute-start.3 = (bf16[512,640]{1,0:T(8,128)(2,1)}, bf16[512,640]{1,0:T(8,128)(2,1)S(1)}, u32[]{:S(2)}, u32[]{:S(2)}) collective-permute-start(bf16[512,640]{1,0:T(8,128)(2,1)} %collective-permute-done.2), channel_id=1, source_target_pairs={{0,128},{128,256},{256,384},{1,129},{129,257},{257,385},{2,130},{1... | collective-permute-start | bytes 1966088 | tf_op jit(solution)/shard_map/ppermute | solution.py:158
  84.1 0.7 dynamic_slice.13
  84.8 1.9 %pad_add_fusion.counts = s32[2]{0:T(128)} fusion(s32[1]{0:T(128)} %dynamic_slice.13, s32[1]{0:T(128)} %dynamic_slice.12), kind=kLoop, calls=%fused_computation.2 | loop fusion | flops 2 | bytes 16 | tf_op jit(solution)/shard_map/stack | solution.py:140
  86.6 11.3 %shard_map.56 = (f32[896,640]{1,0:T(8,128)}, f32[896,8]{1,0:T(8,128)}, f32[896,8]{1,0:T(8,128)}) custom-call(s32[2]{0:T(128)} %pad_add_fusion.counts, bf16[896,640]{1,0:T(8,128)(2,1)} %bitcast.1.q_ref, bf16[896,640]{1,0:T(8,128)(2,1)} %bitcast.35, bf16[896,640]{1,0:T(8,128)(2,1)} %bitcast.33), custom_call_target="tpu_custom_call" | custom-call | flops 3082813440 | bytes 5734400 | tf_op jit(solution)/shard_map/pallas_call | solution.py:108
  98.0 7.2 %shard_map.55 = (bf16[896,2560]{1,0:T(8,128)(2,1)}, f32[896,8]{1,0:T(8,128)}, f32[896,8]{1,0:T(8,128)}) custom-call(s32[2]{0:T(128)} %pad_add_fusion.counts, bf16[896,640]{1,0:T(8,128)(2,1)} %bitcast.1.q_ref, bf16[512,640]{1,0:T(8,128)(2,1)} %collective-permute-done.mk_ref), custom_call_target="tpu_custom_call" | custom-call | flops 1174405120 | bytes 6389760 | tf_op jit(solution)/shard_map/pallas_call | solution.py:108
  105.2 9.4 %collective-permute-done.3 = bf16[512,640]{1,0:T(8,128)(2,1)S(1)} collective-permute-done((bf16[512,640]{1,0:T(8,128)(2,1)}, bf16[512,640]{1,0:T(8,128)(2,1)S(1)}, u32[]{:S(2)}, u32[]{:S(2)}) %collective-permute-start.3) | collective-permute-done | bytes 655392 | tf_op jit(solution)/shard_map/ppermute | solution.py:158
  114.6 1.0 add.15.mv_ref
  115.6 7.2 %shard_map.57 = bf16[896,640]{1,0:T(8,128)(2,1)} custom-call(s32[2]{0:T(128)} %pad_add_fusion.counts, bf16[896,2560]{1,0:T(8,128)(2,1)} %get-tuple-element.11.w_ref, bf16[512,640]{1,0:T(8,128)(2,1)} %add.15.mv_ref, f32[896,640]{1,0:T(8,128)} %get-tuple-element.12.acc_ref, f32[896,8]{1,0:T(8,128)} %get-tuple-element.13.top_ref, ...), custom_call_target="tpu_custom_call" | custom-call | flops 587202560 | bytes 8683520 | tf_op jit(solution)/shard_map/pallas_call | solution.py:108
  122.8 21.3 %all_to_all.43 = bf16[8,112,640]{2,1,0:T(8,128)(2,1)S(1)} all-to-all(bf16[8,112,640]{2,1,0:T(8,128)(2,1)} %bitcast.31), channel_id=1, replica_groups=mesh['stretch'=32,'head'=8,'cfg'=2] {'head'}, dimensions={0} | all-to-all | bytes 2293760 | tf_op jit(solution)/shard_map/all_to_all | solution.py:211
  144.2 1.2 copy.16
  (17 shorter events, 0.2 us)
Async XLA Ops:
  0.0 1.6 %copy-start.2 = (bf16[112,5120]{1,0:T(8,128)(2,1)S(1)}, bf16[112,5120]{1,0:T(8,128)(2,1)}, u32[]{:S(2)}) copy-start(bf16[112,5120]{1,0:T(8,128)(2,1)} %param.7) | copy-start | bytes 3440644
  3.7 5.9 %copy-start.3 = (bf16[112,5120]{1,0:T(8,128)(2,1)S(1)}, bf16[112,5120]{1,0:T(8,128)(2,1)}, u32[]{:S(2)}) copy-start(bf16[112,5120]{1,0:T(8,128)(2,1)} %param.5) | copy-start | bytes 3440644
  3.7 33.8 %all-to-all-start.1 = ((bf16[8,2,112,640]{3,2,1,0:T(8,128)(2,1)}), bf16[8,2,112,640]{3,2,1,0:T(8,128)(2,1)S(1)}, u32[]{:S(2)}, u32[]{:S(2)}) async-start(bf16[8,2,112,640]{3,2,1,0:T(8,128)(2,1)} %copy.13), calls=%async_computation.1 | async-start | bytes 4587520 | tf_op jit(solution)/shard_map/all_to_all | solution.py:150
  37.5 5.5 %copy-start.4 = (s32[32]{0:T(128)S(1)}, s32[32]{0:T(128)}, u32[]{:S(2)}) copy-start(s32[32]{0:T(128)} %param.8) | copy-start | bytes 388
  37.5 49.2 %all-to-all-start = ((bf16[112,8,640]{2,0,1:T(8,128)(2,1)}), bf16[112,8,640]{2,0,1:T(8,128)(2,1)}, u32[]{:S(2)}, u32[]{:S(2)}) async-start(bf16[112,8,640]{2,0,1:T(8,128)(2,1)} %bitcast.26), calls=%async_computation | async-start | bytes 2293760 | tf_op jit(solution)/shard_map/all_to_all | solution.py:163
  44.3 1.5 %copy-start = (bf16[1,8,112,640]{3,2,0,1:T(8,128)(2,1)}, bf16[1,8,112,640]{3,2,0,1:T(8,128)(2,1)S(1)}, u32[]{:S(2)}) copy-start(bf16[1,8,112,640]{3,2,0,1:T(8,128)(2,1)S(1)} %get-tuple-element.17) | copy-start | bytes 3440644
  44.3 1.5 %copy-start.1 = (bf16[1,8,112,640]{3,2,0,1:T(8,128)(2,1)}, bf16[1,8,112,640]{3,2,0,1:T(8,128)(2,1)S(1)}, u32[]{:S(2)}) copy-start(bf16[1,8,112,640]{3,2,0,1:T(8,128)(2,1)S(1)} %get-tuple-element.18) | copy-start | bytes 3440644
  44.3 39.8 %copy-start.5 = (s32[32]{0:T(128)S(1)}, s32[32]{0:T(128)}, u32[]{:S(2)}) copy-start(s32[32]{0:T(128)} %param.9) | copy-start | bytes 388
  44.4 37.8 %collective-permute-start.2 = (bf16[512,640]{1,0:T(8,128)(2,1)S(1)}, bf16[512,640]{1,0:T(8,128)(2,1)}, u32[]{:S(2)}, u32[]{:S(2)}) collective-permute-start(bf16[512,640]{1,0:T(8,128)(2,1)S(1)} %constant_dynamic-slice_fusion), channel_id=1, source_target_pairs={{112,0},{240,128},{368,256},{113,1},{241,129},{369,257},{114,2},{2... | collective-permute-start | bytes 1966088 | tf_op jit(solution)/shard_map/ppermute | solution.py:159
  45.8 52.2 %collective-permute-start = (bf16[512,640]{1,0:T(8,128)(2,1)S(1)}, bf16[512,640]{1,0:T(8,128)(2,1)}, u32[]{:S(2)}, u32[]{:S(2)}) collective-permute-start(bf16[512,640]{1,0:T(8,128)(2,1)S(1)} %constant_dynamic-slice_fusion.1), channel_id=1, source_target_pairs={{0,16},{16,32},{32,48},{48,64},{64,80},{80,96},{96,112},{112,128},... | collective-permute-start | bytes 1966088 | tf_op jit(solution)/shard_map/ppermute | solution.py:23
  50.4 54.8 %collective-permute-start.1 = (bf16[512,640]{1,0:T(8,128)(2,1)S(1)}, bf16[512,640]{1,0:T(8,128)(2,1)S(1)}, u32[]{:S(2)}, u32[]{:S(2)}) collective-permute-start(bf16[512,640]{1,0:T(8,128)(2,1)S(1)} %constant_dynamic-slice_fusion), channel_id=1, source_target_pairs={{0,16},{16,32},{32,48},{48,64},{64,80},{80,96},{96,112},{128,144},... | collective-permute-start | bytes 1966088 | tf_op jit(solution)/shard_map/ppermute | solution.py:158
  82.2 32.4 %collective-permute-start.3 = (bf16[512,640]{1,0:T(8,128)(2,1)}, bf16[512,640]{1,0:T(8,128)(2,1)S(1)}, u32[]{:S(2)}, u32[]{:S(2)}) collective-permute-start(bf16[512,640]{1,0:T(8,128)(2,1)} %collective-permute-done.2), channel_id=1, source_target_pairs={{0,128},{128,256},{256,384},{1,129},{129,257},{257,385},{2,130},{1... | collective-permute-start | bytes 1966088 | tf_op jit(solution)/shard_map/ppermute | solution.py:158

commit v9 on v7

--- a/solution.py
+++ b/solution.py
@@ -14,6 +14,7 @@
 
 NEG = -1e30
 TQ = 448
+MT = 224
 COLS = 8
 
 
@@ -73,7 +74,8 @@
 ):
     own_live = counts[0] * FT
     tail = mv_ref.shape[0]
-    rows = pl.program_id(0) * TQ + lax.broadcasted_iota(jnp.int32, (TQ, 1), 0)
+    tq = o_ref.shape[0]
+    rows = pl.program_id(0) * tq + lax.broadcasted_iota(jnp.int32, (tq, 1), 0)
     row_live = rows < own_live
     for h in range(o_ref.shape[1] // HD):
         c = head_cols(h)
@@ -94,15 +96,15 @@
         o_ref[:, c] = jnp.where(row_live, mixed, 0.0).astype(o_ref.dtype)
 
 
-def rows_of(width):
-    return pl.BlockSpec((TQ, width), lambda i, c: (i, 0))
+def rows_of(width, tq=TQ):
+    return pl.BlockSpec((tq, width), lambda i, c: (i, 0))
 
 
 def whole(rows, width):
     return pl.BlockSpec((rows, width), lambda i, c: (0, 0))
 
 
-def call(kernel, counts, operands, in_specs, outs, cost):
+def call(kernel, counts, operands, in_specs, outs, cost, tq=TQ):
     span = operands[0].shape[0]
     shapes = [jax.ShapeDtypeStruct((span, w), t) for w, t in outs]
     return pl.pallas_call(
@@ -110,9 +112,9 @@
         out_shape=tuple(shapes),
         grid_spec=pltpu.PrefetchScalarGridSpec(
             num_scalar_prefetch=1,
-            grid=(span // TQ,),
+            grid=(span // tq,),
             in_specs=in_specs,
-            out_specs=[rows_of(w) for w, _ in outs],
+            out_specs=[rows_of(w, tq) for w, _ in outs],
         ),
         compiler_params=pltpu.CompilerParams(dimension_semantics=("arbitrary",)),
         cost_estimate=cost,
@@ -150,20 +152,19 @@
     kv_recv = lax.all_to_all(kv_send, "head", split_axis=0, concat_axis=0, tiled=True)
     kv_rows = kv_recv.transpose(1, 0, 2, 3).reshape(2, groups * rows, local)
     k_heads, v_heads = kv_rows[0], kv_rows[1]
-    k_tail = lax.dynamic_slice_in_dim(k_heads, tail_begin, tail, 0)
-    v_tail = lax.dynamic_slice_in_dim(v_heads, tail_begin, tail, 0)
-    k_prior = from_behind(k_tail, "stretch", 1)
+    kv_tail = lax.dynamic_slice_in_dim(kv_rows, tail_begin, tail, 1)
     inner, first, second = plan
     half = tail // 2
-    v_near = from_behind(v_tail[:half], "stretch", 1)
-    v_far = v_tail[half:]
+    direct = jnp.concatenate([kv_tail[0], kv_tail[1, :half]], axis=0)
+    direct_prior = from_behind(direct, "stretch", 1)
+    v_far = kv_tail[1, half:]
     if first:
         v_far = lax.ppermute(v_far, "stretch", inner) + lax.ppermute(
             lax.ppermute(v_far, "stretch", first), "stretch", second
         )
     else:
         v_far = from_behind(v_far, "stretch", 1)
-    v_prior = jnp.concatenate([v_near, v_far], axis=0)
+    v_prior = jnp.concatenate([direct_prior[tail:], v_far], axis=0)
     q_heads = lax.all_to_all(queries, "head", split_axis=1, concat_axis=0, tiled=True)
     span, local = q_heads.shape
     heads = local // HD
@@ -183,27 +184,28 @@
     w_mot, mtop, mtot = call(
         mscore_kernel,
         counts,
-        (q_heads, k_prior),
-        [rows_of(local), whole(tail, local)],
+        (q_heads, direct_prior),
+        [rows_of(local, MT), whole(tail, local)],
         [(heads * tail, jnp.bfloat16), (COLS, f32), (COLS, f32)],
         pl.CostEstimate(
             flops=heads * 2 * span * tail * 2 * HD,
             transcendentals=heads * span * tail,
             bytes_accessed=span * local * 2 + tail * local * 2 + span * heads * tail * 2,
         ),
+        tq=MT,
     )
     (mixed,) = call(
         merge_kernel,
         counts,
         (w_mot, v_prior, acc, top, tot, mtop, mtot),
         [
-            rows_of(heads * tail),
+            rows_of(heads * tail, MT),
             whole(tail, local),
-            rows_of(local),
-            rows_of(COLS),
-            rows_of(COLS),
-            rows_of(COLS),
-            rows_of(COLS),
+            rows_of(local, MT),
+            rows_of(COLS, MT),
+            rows_of(COLS, MT),
+            rows_of(COLS, MT),
+            rows_of(COLS, MT),
         ],
         [(local, jnp.bfloat16)],
         pl.CostEstimate(
@@ -211,6 +213,7 @@
             transcendentals=2 * heads * span,
             bytes_accessed=span * heads * tail * 2 + span * local * 6 + tail * local * 2,
         ),
+        tq=MT,
     )
     return lax.all_to_all(mixed, "head", split_axis=0, concat_axis=1, tiled=True)
 

time: 136 us -> 146 us (1.074)
  local copies, waits for them, and re-layouts: 7.2 us -> 11.6 us
  waiting for transfers between devices: 38.8 us -> 42.8 us
  starting transfers between devices: 26.2 us -> 22.6 us
  Pallas kernels: 25.8 us -> 28.1 us
  other arithmetic: 2.92 us -> 5.17 us
    ppermute x2 -> x1, starting transfers between devices: 8.55 us -> 4.27 us  [from_behind(): return lax.ppermute(shard, axis, pairs)]
    ppermute x1, waiting for transfers between devices: 0.01 us -> 3.09 us  [body(): lax.ppermute(v_far, 'stretch', inner)]
    pallas_call x3, Pallas kernels: 25.8 us -> 28.1 us  [call(): pl.pallas_call(kernel, out_shape=tuple(shapes), grid_spec=pltpu.PrefetchS...]
  transfers between devices with their start and end apart: 7 -> 6, of which waited for: 2 -> 3; matrix products, arithmetic and copies ran while one was open for 3% -> 6% of each run, Pallas kernels for 14% -> 8%
where the time goes in v9:
time: 146 us
  waiting for transfers between devices  42.8 us (29%)
  blocking collectives  34.6 us (24%)
  Pallas kernels  28.1 us (19%)
  starting transfers between devices  22.6 us (15%)
  local copies, waits for them, and re-layouts  11.6 us (8%)
  other arithmetic  5.17 us (4%)
    all_to_all x1, blocking collectives, body(): lax.all_to_all(mixed, 'head', split_axis=0, concat_axis=1, tiled=True)  34.6 us
    pallas_call x3, Pallas kernels, call(): pl.pallas_call(kernel, out_shape=tuple(shapes), grid_spec=pltpu.PrefetchS...  28.1 us
    all_to_all x1, waiting for transfers between devices, body(): lax.all_to_all(kv_send, 'head', split_axis=0, concat_axis=0, tiled=True)  26.8 us
    ppermute x1, waiting for transfers between devices, body(): lax.ppermute(lax.ppermute(v_far, 'stretch', first), 'stretch', second)  13 us
    all_to_all x1, starting transfers between devices, body(): lax.all_to_all(kv_send, 'head', split_axis=0, concat_axis=0, tiled=True)  5.89 us
    ppermute x1, starting transfers between devices, body(): lax.ppermute(v_far, 'stretch', inner)  5.01 us
    all_to_all x1, starting transfers between devices, body(): lax.all_to_all(queries, 'head', split_axis=1, concat_axis=0, tiled=True)  4.68 us
    ppermute x1, starting transfers between devices, from_behind(): return lax.ppermute(shard, axis, pairs)  4.27 us
  transfers between devices with their start and end apart: 6, of which 3 were waited for; matrix products, arithmetic and copies ran while one was open for 6% of the time, Pallas kernels for 8%

profile of v9, /device:TPU:56, one launch (start us, length us, event | category | flops | bytes accessed | tf_op | source)
XLA Modules:
  0.0 145.6 jit_solution(3372916376822070670)
XLA Ops:
  0.0 1.5 %copy.19 = bf16[14,8,8,640]{3,2,1,0:T(8,128)(2,1)S(1)} copy(bf16[14,8,8,640]{3,1,2,0:T(8,128)(2,1)} %bitcast.44) | data formatting | bytes 2293760
  2.0 1.7 %copy.14 = bf16[8,2,112,640]{3,2,1,0:T(8,128)(2,1)} copy(bf16[8,2,112,640]{3,0,2,1:T(8,128)(2,1)S(1)} %pad_maximum_fusion) | data formatting | bytes 4587520 | tf_op jit(solution)/shard_map/stack | solution.py:151
  3.7 5.9 %all-to-all-start.1 = ((bf16[8,2,112,640]{3,2,1,0:T(8,128)(2,1)}), bf16[8,2,112,640]{3,2,1,0:T(8,128)(2,1)S(1)}, u32[]{:S(2)}, u32[]{:S(2)}) async-start(bf16[8,2,112,640]{3,2,1,0:T(8,128)(2,1)} %copy.14), calls=%async_computation.1 | async-start | bytes 4587520 | tf_op jit(solution)/shard_map/all_to_all | solution.py:152
  9.6 1.1 copy.22
  10.7 26.8 %all-to-all-done.1 = bf16[8,2,112,640]{3,2,1,0:T(8,128)(2,1)S(1)} async-done(((bf16[8,2,112,640]{3,2,1,0:T(8,128)(2,1)}), bf16[8,2,112,640]{3,2,1,0:T(8,128)(2,1)S(1)}, u32[]{:S(2)}, u32[]{:S(2)}) %all-to-all-start.1) | async-done | bytes 2293792 | tf_op jit(solution)/shard_map/all_to_all | solution.py:152
  37.5 4.7 %all-to-all-start = ((bf16[112,8,640]{2,0,1:T(8,128)(2,1)}), bf16[112,8,640]{2,0,1:T(8,128)(2,1)S(1)}, u32[]{:S(2)}, u32[]{:S(2)}) async-start(bf16[112,8,640]{2,0,1:T(8,128)(2,1)} %bitcast.33), calls=%async_computation | async-start | bytes 2293760 | tf_op jit(solution)/shard_map/all_to_all | solution.py:168
  44.4 1.1 pad_maximum_fusion.1
  45.5 4.3 %collective-permute-start = (bf16[768,640]{1,0:T(8,128)(2,1)}, bf16[768,640]{1,0:T(8,128)(2,1)}, u32[]{:S(2)}, u32[]{:S(2)}) collective-permute-start(bf16[768,640]{1,0:T(8,128)(2,1)} %pad_maximum_fusion.1), channel_id=1, source_target_pairs={{0,16},{16,32},{32,48},{48,64},{64,80},{80,96},{96,112},{112,128},... | collective-permute-start | bytes 2949128 | tf_op jit(solution)/shard_map/ppermute | solution.py:24
  49.8 1.4 collective-permute-start.2
  51.8 1.8 %pad_add_fusion.counts = s32[2]{0:T(128)} fusion(s32[1]{0:T(128)} %dynamic_slice.10, s32[1]{0:T(128)} %dynamic_slice.9), kind=kLoop, calls=%fused_computation.7 | loop fusion | flops 2 | bytes 16 | tf_op jit(solution)/shard_map/stack | solution.py:142
  53.6 5.0 %collective-permute-start.1 = (bf16[256,640]{1,0:T(8,128)(2,1)}, bf16[256,640]{1,0:T(8,128)(2,1)}, u32[]{:S(2)}, u32[]{:S(2)}) collective-permute-start(bf16[256,640]{1,0:T(8,128)(2,1)} %get-tuple-element.19), channel_id=1, source_target_pairs={{0,16},{16,32},{32,48},{48,64},{64,80},{80,96},{96,112},{128,144},... | collective-permute-start | bytes 983048 | tf_op jit(solution)/shard_map/ppermute | solution.py:162
  58.6 1.3 collective-permute-start.3
  59.9 1.6 %fusion = (bf16[1,8,112,640]{3,2,0,1:T(8,128)(2,1)}, bf16[1,8,112,640]{3,2,0,1:T(8,128)(2,1)}) fusion(bf16[2,8,112,640]{3,2,0,1:T(8,128)(2,1)S(1)} %bitcast.35), kind=kLoop, calls=%fused_computation.8 | loop fusion | bytes 4587520 | tf_op jit(solution)/shard_map/slice | solution.py:154
  61.5 1.0 copy-done.2
  62.5 11.3 %shard_map.56 = (f32[896,640]{1,0:T(8,128)}, f32[896,8]{1,0:T(8,128)}, f32[896,8]{1,0:T(8,128)}) custom-call(s32[2]{0:T(128)} %pad_add_fusion.counts, bf16[896,640]{1,0:T(8,128)(2,1)} %bitcast.47, bf16[896,640]{1,0:T(8,128)(2,1)} %bitcast.43, bf16[896,640]{1,0:T(8,128)(2,1)} %bitcast.42), custom_call_target="tpu_custom_call" | custom-call | flops 3082813440 | bytes 5734400 | tf_op jit(solution)/shard_map/pallas_call | solution.py:110
  73.8 3.1 %collective-permute-done.1 = bf16[256,640]{1,0:T(8,128)(2,1)} collective-permute-done((bf16[256,640]{1,0:T(8,128)(2,1)}, bf16[256,640]{1,0:T(8,128)(2,1)}, u32[]{:S(2)}, u32[]{:S(2)}) %collective-permute-start.1) | collective-permute-done | bytes 327712 | tf_op jit(solution)/shard_map/ppermute | solution.py:162
  76.9 13.0 %collective-permute-done.3 = bf16[256,640]{1,0:T(8,128)(2,1)} collective-permute-done((bf16[256,640]{1,0:T(8,128)(2,1)}, bf16[256,640]{1,0:T(8,128)(2,1)}, u32[]{:S(2)}, u32[]{:S(2)}) %collective-permute-start.3) | collective-permute-done | bytes 327712 | tf_op jit(solution)/shard_map/ppermute | solution.py:162
  89.9 1.2 add.14
  91.1 1.0 slice.26
  92.1 1.0 pad_maximum_fusion.2.mv_ref
  93.0 9.6 %shard_map.55 = (bf16[896,2560]{1,0:T(8,128)(2,1)}, f32[896,8]{1,0:T(8,128)}, f32[896,8]{1,0:T(8,128)}) custom-call(s32[2]{0:T(128)} %pad_add_fusion.counts, bf16[896,640]{1,0:T(8,128)(2,1)} %bitcast.48, bf16[768,640]{1,0:T(8,128)(2,1)} %collective-permute-done.mk_ref), custom_call_target="tpu_custom_call" | custom-call | flops 1174405120 | bytes 6389760 | tf_op jit(solution)/shard_map/pallas_call | solution.py:110
  102.6 7.2 %shard_map.57 = bf16[896,640]{1,0:T(8,128)(2,1)} custom-call(s32[2]{0:T(128)} %pad_add_fusion.counts, bf16[896,2560]{1,0:T(8,128)(2,1)} %get-tuple-element.11.w_ref, bf16[512,640]{1,0:T(8,128)(2,1)} %pad_maximum_fusion.2.mv_ref, f32[896,640]{1,0:T(8,128)} %get-tuple-element.12.acc_ref, f32[896,8]{1,0:T(8,128)} %get-tuple-element.13.top_ref, ...), custom_call_target="tpu_custom_call" | custom-call | flops 587202560 | bytes 8683520 | tf_op jit(solution)/shard_map/pallas_call | solution.py:110
  109.8 34.6 %all_to_all.43 = bf16[8,112,640]{2,1,0:T(8,128)(2,1)S(1)} all-to-all(bf16[8,112,640]{2,1,0:T(8,128)(2,1)} %bitcast.41), channel_id=1, replica_groups=mesh['stretch'=32,'head'=8,'cfg'=2] {'head'}, dimensions={0} | all-to-all | bytes 2293760 | tf_op jit(solution)/shard_map/all_to_all | solution.py:218
  144.4 1.2 copy.18
  (19 shorter events, 2.8 us)
Async XLA Ops:
  0.0 1.6 %copy-start = (bf16[112,5120]{1,0:T(8,128)(2,1)S(1)}, bf16[112,5120]{1,0:T(8,128)(2,1)}, u32[]{:S(2)}) copy-start(bf16[112,5120]{1,0:T(8,128)(2,1)} %param.7) | copy-start | bytes 3440644
  3.7 5.9 %copy-start.1 = (bf16[112,5120]{1,0:T(8,128)(2,1)S(1)}, bf16[112,5120]{1,0:T(8,128)(2,1)}, u32[]{:S(2)}) copy-start(bf16[112,5120]{1,0:T(8,128)(2,1)} %param.5) | copy-start | bytes 3440644
  3.7 33.8 %all-to-all-start.1 = ((bf16[8,2,112,640]{3,2,1,0:T(8,128)(2,1)}), bf16[8,2,112,640]{3,2,1,0:T(8,128)(2,1)S(1)}, u32[]{:S(2)}, u32[]{:S(2)}) async-start(bf16[8,2,112,640]{3,2,1,0:T(8,128)(2,1)} %copy.14), calls=%async_computation.1 | async-start | bytes 4587520 | tf_op jit(solution)/shard_map/all_to_all | solution.py:152
  10.7 31.5 %copy-start.3 = (s32[32]{0:T(128)S(1)}, s32[32]{0:T(128)}, u32[]{:S(2)}) copy-start(s32[32]{0:T(128)} %param.8) | copy-start | bytes 388
  37.5 24.0 %all-to-all-start = ((bf16[112,8,640]{2,0,1:T(8,128)(2,1)}), bf16[112,8,640]{2,0,1:T(8,128)(2,1)S(1)}, u32[]{:S(2)}, u32[]{:S(2)}) async-start(bf16[112,8,640]{2,0,1:T(8,128)(2,1)} %bitcast.33), calls=%async_computation | async-start | bytes 2293760 | tf_op jit(solution)/shard_map/all_to_all | solution.py:168
  44.4 6.8 %copy-start.4 = (s32[32]{0:T(128)S(1)}, s32[32]{0:T(128)}, u32[]{:S(2)}) copy-start(s32[32]{0:T(128)} %param.9) | copy-start | bytes 388
  45.5 45.6 %collective-permute-start = (bf16[768,640]{1,0:T(8,128)(2,1)}, bf16[768,640]{1,0:T(8,128)(2,1)}, u32[]{:S(2)}, u32[]{:S(2)}) collective-permute-start(bf16[768,640]{1,0:T(8,128)(2,1)} %pad_maximum_fusion.1), channel_id=1, source_target_pairs={{0,16},{16,32},{32,48},{48,64},{64,80},{80,96},{96,112},{112,128},... | collective-permute-start | bytes 2949128 | tf_op jit(solution)/shard_map/ppermute | solution.py:24
  49.8 8.9 %collective-permute-start.2 = (bf16[256,640]{1,0:T(8,128)(2,1)}, bf16[256,640]{1,0:T(8,128)(2,1)}, u32[]{:S(2)}, u32[]{:S(2)}) collective-permute-start(bf16[256,640]{1,0:T(8,128)(2,1)} %get-tuple-element.19), channel_id=1, source_target_pairs={{112,0},{240,128},{368,256},{113,1},{241,129},{369,257},{114,2},{2... | collective-permute-start | bytes 983048 | tf_op jit(solution)/shard_map/ppermute | solution.py:163
  53.6 23.3 %collective-permute-start.1 = (bf16[256,640]{1,0:T(8,128)(2,1)}, bf16[256,640]{1,0:T(8,128)(2,1)}, u32[]{:S(2)}, u32[]{:S(2)}) collective-permute-start(bf16[256,640]{1,0:T(8,128)(2,1)} %get-tuple-element.19), channel_id=1, source_target_pairs={{0,16},{16,32},{32,48},{48,64},{64,80},{80,96},{96,112},{128,144},... | collective-permute-start | bytes 983048 | tf_op jit(solution)/shard_map/ppermute | solution.py:162
  58.6 31.3 %collective-permute-start.3 = (bf16[256,640]{1,0:T(8,128)(2,1)}, bf16[256,640]{1,0:T(8,128)(2,1)}, u32[]{:S(2)}, u32[]{:S(2)}) collective-permute-start(bf16[256,640]{1,0:T(8,128)(2,1)} %collective-permute-done.2), channel_id=1, source_target_pairs={{0,128},{128,256},{256,384},{1,129},{129,257},{257,385},{2,130},{1... | collective-permute-start | bytes 983048 | tf_op jit(solution)/shard_map/ppermute | solution.py:162
  61.5 1.0 copy-start.2

commit v10 on v7

--- a/solution.py
+++ b/solution.py
@@ -35,7 +35,7 @@
     return slice(h * HD, (h + 1) * HD)
 
 
-def own_kernel(counts, q_ref, k_ref, v_ref, acc_ref, top_ref, tot_ref):
+def own_kernel(counts, q_ref, k_ref, v_ref, order_ref, acc_ref, top_ref, tot_ref):
     own_live = counts[0] * FT
     span = k_ref.shape[0]
     key_live = lax.broadcasted_iota(jnp.int32, (1, span), 1) < own_live
@@ -155,7 +155,8 @@
     k_prior = from_behind(k_tail, "stretch", 1)
     inner, first, second = plan
     half = tail // 2
-    v_near = from_behind(v_tail[:half], "stretch", 1)
+    v_near, k_prior = lax.optimization_barrier((v_tail[:half], k_prior))
+    v_near = from_behind(v_near, "stretch", 1)
     v_far = v_tail[half:]
     if first:
         v_far = lax.ppermute(v_far, "stretch", inner) + lax.ppermute(
@@ -171,8 +172,13 @@
     acc, top, tot = call(
         own_kernel,
         counts,
-        (q_heads, k_heads, v_heads),
-        [rows_of(local), whole(span, local), whole(span, local)],
+        (q_heads, k_heads, v_heads, k_prior),
+        [
+            rows_of(local),
+            whole(span, local),
+            whole(span, local),
+            pl.BlockSpec(memory_space=pl.ANY),
+        ],
         [(local, f32), (COLS, f32), (COLS, f32)],
         pl.CostEstimate(
             flops=heads * 2 * span * span * 3 * HD,

time: 136 us -> 142 us (1.044)
  waiting for transfers between devices: 38.8 us -> 46.8 us
  starting transfers between devices: 26.2 us -> 23.9 us
  local copies, waits for them, and re-layouts: 7.2 us -> 9.14 us
  blocking collectives: 34 us -> 32.3 us
    ppermute x2, waiting for transfers between devices: 0.01 us -> 20 us  [from_behind(): return lax.ppermute(shard, axis, pairs)]
    ppermute x1, waiting for transfers between devices: 12 us -> 0.01 us  [body(): lax.ppermute(lax.ppermute(v_far, 'stretch', first), 'stretch', second)]
    ppermute x2, starting transfers between devices: 8.55 us -> 6.32 us  [from_behind(): return lax.ppermute(shard, axis, pairs)]
    all_to_all x1, blocking collectives: 34 us -> 32.3 us  [body(): lax.all_to_all(mixed, 'head', split_axis=0, concat_axis=1, tiled=True)]
  transfers between devices with their start and end apart: 7 -> 7, of which waited for: 2 -> 3; matrix products, arithmetic and copies ran while one was open for 3% -> 5% of each run, Pallas kernels for 14% -> 13%
where the time goes in v10:
time: 142 us
  waiting for transfers between devices  46.8 us (33%)
  blocking collectives  32.3 us (23%)
  Pallas kernels  25.7 us (18%)
  starting transfers between devices  23.9 us (17%)
  local copies, waits for them, and re-layouts  9.14 us (6%)
  other arithmetic  3.16 us (2%)
    all_to_all x1, blocking collectives, body(): lax.all_to_all(mixed, 'head', split_axis=0, concat_axis=1, tiled=True)  32.3 us
    all_to_all x1, waiting for transfers between devices, body(): lax.all_to_all(kv_send, 'head', split_axis=0, concat_axis=0, tiled=True)  26.8 us
    pallas_call x3, Pallas kernels, call(): pl.pallas_call(kernel, out_shape=tuple(shapes), grid_spec=pltpu.PrefetchS...  25.7 us
    ppermute x2, waiting for transfers between devices, from_behind(): return lax.ppermute(shard, axis, pairs)  20 us
    ppermute x2, starting transfers between devices, from_behind(): return lax.ppermute(shard, axis, pairs)  6.32 us
    all_to_all x1, starting transfers between devices, body(): lax.all_to_all(kv_send, 'head', split_axis=0, concat_axis=0, tiled=True)  5.89 us
    all_to_all x1, starting transfers between devices, body(): lax.all_to_all(queries, 'head', split_axis=1, concat_axis=0, tiled=True)  5.49 us
    ppermute x1, starting transfers between devices, body(): lax.ppermute(v_far, 'stretch', inner)  4.28 us
  transfers between devices with their start and end apart: 7, of which 3 were waited for; matrix products, arithmetic and copies ran while one was open for 5% of the time, Pallas kernels for 13%

profile of v10, /device:TPU:56, one launch (start us, length us, event | category | flops | bytes accessed | tf_op | source)
XLA Modules:
  0.0 141.9 jit_solution(15042117015585711835)
XLA Ops:
  0.0 1.5 %copy.17 = bf16[14,8,8,640]{3,2,1,0:T(8,128)(2,1)S(1)} copy(bf16[14,8,8,640]{3,1,2,0:T(8,128)(2,1)} %bitcast.36) | data formatting | bytes 2293760
  2.0 1.7 %copy.13 = bf16[8,2,112,640]{3,2,1,0:T(8,128)(2,1)} copy(bf16[8,2,112,640]{3,0,2,1:T(8,128)(2,1)S(1)} %pad_maximum_fusion) | data formatting | bytes 4587520 | tf_op jit(solution)/shard_map/stack | solution.py:149
  3.7 5.9 %all-to-all-start.1 = ((bf16[8,2,112,640]{3,2,1,0:T(8,128)(2,1)}), bf16[8,2,112,640]{3,2,1,0:T(8,128)(2,1)S(1)}, u32[]{:S(2)}, u32[]{:S(2)}) async-start(bf16[8,2,112,640]{3,2,1,0:T(8,128)(2,1)} %copy.13), calls=%async_computation.1 | async-start | bytes 4587520 | tf_op jit(solution)/shard_map/all_to_all | solution.py:150
  9.6 1.1 copy.20
  10.7 26.8 %all-to-all-done.1 = bf16[8,2,112,640]{3,2,1,0:T(8,128)(2,1)S(1)} async-done(((bf16[8,2,112,640]{3,2,1,0:T(8,128)(2,1)}), bf16[8,2,112,640]{3,2,1,0:T(8,128)(2,1)S(1)}, u32[]{:S(2)}, u32[]{:S(2)}) %all-to-all-start.1) | async-done | bytes 2293792 | tf_op jit(solution)/shard_map/all_to_all | solution.py:150
  37.5 5.5 %all-to-all-start = ((bf16[112,8,640]{2,0,1:T(8,128)(2,1)}), bf16[112,8,640]{2,0,1:T(8,128)(2,1)}, u32[]{:S(2)}, u32[]{:S(2)}) async-start(bf16[112,8,640]{2,0,1:T(8,128)(2,1)} %bitcast.26), calls=%async_computation | async-start | bytes 2293760 | tf_op jit(solution)/shard_map/all_to_all | solution.py:168
  43.0 0.7 dynamic_slice.12
  44.3 1.3 fusion
  45.7 4.4 %collective-permute-start = (bf16[512,640]{1,0:T(8,128)(2,1)S(1)}, bf16[512,640]{1,0:T(8,128)(2,1)}, u32[]{:S(2)}, u32[]{:S(2)}) collective-permute-start(bf16[512,640]{1,0:T(8,128)(2,1)S(1)} %constant_dynamic-slice_fusion.1), channel_id=1, source_target_pairs={{0,16},{16,32},{32,48},{48,64},{64,80},{80,96},{96,112},{112,128},... | collective-permute-start | bytes 1966088 | tf_op jit(solution)/shard_map/ppermute | solution.py:23
  50.1 0.8 constant_dynamic-slice_fusion.2
  50.9 0.7 collective-permute-start.3
  51.6 0.6 dynamic_slice.13
  52.2 2.0 %pad_add_fusion.counts = s32[2]{0:T(128)} fusion(s32[1]{0:T(128)} %dynamic_slice.13, s32[1]{0:T(128)} %dynamic_slice.12), kind=kLoop, calls=%fused_computation.6 | loop fusion | flops 2 | bytes 16 | tf_op jit(solution)/shard_map/stack | solution.py:140
  54.2 4.3 %collective-permute-start.2 = (bf16[256,640]{1,0:T(8,128)(2,1)}, bf16[256,640]{1,0:T(8,128)(2,1)S(1)}, u32[]{:S(2)}, u32[]{:S(2)}) collective-permute-start(bf16[256,640]{1,0:T(8,128)(2,1)} %get-tuple-element.23), channel_id=1, source_target_pairs={{0,16},{16,32},{32,48},{48,64},{64,80},{80,96},{96,112},{128,144},... | collective-permute-start | bytes 983048 | tf_op jit(solution)/shard_map/ppermute | solution.py:162
  58.5 1.3 collective-permute-start.4
  59.8 12.1 %collective-permute-done.mk_ref.order_ref = bf16[512,640]{1,0:T(8,128)(2,1)} collective-permute-done((bf16[512,640]{1,0:T(8,128)(2,1)S(1)}, bf16[512,640]{1,0:T(8,128)(2,1)}, u32[]{:S(2)}, u32[]{:S(2)}) %collective-permute-start) | collective-permute-done | bytes 655392 | tf_op jit(solution)/shard_map/ppermute | solution.py:23
  71.9 1.9 %collective-permute-start.1 = (bf16[256,640]{1,0:T(8,128)(2,1)S(1)}, bf16[256,640]{1,0:T(8,128)(2,1)S(1)}, u32[]{:S(2)}, u32[]{:S(2)}) collective-permute-start(bf16[256,640]{1,0:T(8,128)(2,1)S(1)} %get-tuple-element.15), channel_id=1, source_target_pairs={{0,16},{16,32},{32,48},{48,64},{64,80},{80,96},{96,112},{112,128},... | collective-permute-start | bytes 983048 | tf_op jit(solution)/shard_map/ppermute | solution.py:23
  73.8 7.1 %shard_map.55 = (bf16[896,2560]{1,0:T(8,128)(2,1)}, f32[896,8]{1,0:T(8,128)}, f32[896,8]{1,0:T(8,128)}) custom-call(s32[2]{0:T(128)} %pad_add_fusion.counts, bf16[896,640]{1,0:T(8,128)(2,1)} %bitcast.1.q_ref, bf16[512,640]{1,0:T(8,128)(2,1)} %collective-permute-done.mk_ref.order_ref), custom_call_target="tpu_custom_call" | custom-call | flops 1174405120 | bytes 6389760 | tf_op jit(solution)/shard_map/pallas_call | solution.py:108
  80.9 11.4 %shard_map.56 = (f32[896,640]{1,0:T(8,128)}, f32[896,8]{1,0:T(8,128)}, f32[896,8]{1,0:T(8,128)}) custom-call(s32[2]{0:T(128)} %pad_add_fusion.counts, bf16[896,640]{1,0:T(8,128)(2,1)} %bitcast.1.q_ref, bf16[896,640]{1,0:T(8,128)(2,1)} %bitcast.33, bf16[896,640]{1,0:T(8,128)(2,1)} %bitcast.34, bf16[512,640]{1,0:T(8,128)(2,1)} %collective-permute-done.mk_ref.order_ref), custom_call_target="tpu_custom_call" | custom-call | flops 3082813440 | bytes 5734400 | tf_op jit(solution)/shard_map/pallas_call | solution.py:108
  92.4 7.9 %collective-permute-done.1 = bf16[256,640]{1,0:T(8,128)(2,1)S(1)} collective-permute-done((bf16[256,640]{1,0:T(8,128)(2,1)S(1)}, bf16[256,640]{1,0:T(8,128)(2,1)S(1)}, u32[]{:S(2)}, u32[]{:S(2)}) %collective-permute-start.1) | collective-permute-done | bytes 327712 | tf_op jit(solution)/shard_map/ppermute | solution.py:23
  100.3 0.9 pad_maximum_fusion.1.mv_ref
  101.2 7.2 %shard_map.57 = bf16[896,640]{1,0:T(8,128)(2,1)} custom-call(s32[2]{0:T(128)} %pad_add_fusion.counts, bf16[896,2560]{1,0:T(8,128)(2,1)} %get-tuple-element.14.w_ref, bf16[512,640]{1,0:T(8,128)(2,1)} %pad_maximum_fusion.1.mv_ref, f32[896,640]{1,0:T(8,128)} %get-tuple-element.16.acc_ref, f32[896,8]{1,0:T(8,128)} %get-tuple-element.17.top_ref, ...), custom_call_target="tpu_custom_call" | custom-call | flops 587202560 | bytes 8683520 | tf_op jit(solution)/shard_map/pallas_call | solution.py:108
  108.5 32.3 %all_to_all.43 = bf16[8,112,640]{2,1,0:T(8,128)(2,1)S(1)} all-to-all(bf16[8,112,640]{2,1,0:T(8,128)(2,1)} %bitcast.31), channel_id=1, replica_groups=mesh['stretch'=32,'head'=8,'cfg'=2] {'head'}, dimensions={0} | all-to-all | bytes 2293760 | tf_op jit(solution)/shard_map/all_to_all | solution.py:221
  140.8 1.2 copy.16
  (20 shorter events, 0.6 us)
Async XLA Ops:
  0.0 1.6 %copy-start.2 = (bf16[112,5120]{1,0:T(8,128)(2,1)S(1)}, bf16[112,5120]{1,0:T(8,128)(2,1)}, u32[]{:S(2)}) copy-start(bf16[112,5120]{1,0:T(8,128)(2,1)} %param.7) | copy-start | bytes 3440644
  3.7 5.9 %copy-start.3 = (bf16[112,5120]{1,0:T(8,128)(2,1)S(1)}, bf16[112,5120]{1,0:T(8,128)(2,1)}, u32[]{:S(2)}) copy-start(bf16[112,5120]{1,0:T(8,128)(2,1)} %param.5) | copy-start | bytes 3440644
  3.7 33.8 %all-to-all-start.1 = ((bf16[8,2,112,640]{3,2,1,0:T(8,128)(2,1)}), bf16[8,2,112,640]{3,2,1,0:T(8,128)(2,1)S(1)}, u32[]{:S(2)}, u32[]{:S(2)}) async-start(bf16[8,2,112,640]{3,2,1,0:T(8,128)(2,1)} %copy.13), calls=%async_computation.1 | async-start | bytes 4587520 | tf_op jit(solution)/shard_map/all_to_all | solution.py:150
  37.5 5.5 %copy-start.4 = (s32[32]{0:T(128)S(1)}, s32[32]{0:T(128)}, u32[]{:S(2)}) copy-start(s32[32]{0:T(128)} %param.8) | copy-start | bytes 388
  37.5 36.3 %all-to-all-start = ((bf16[112,8,640]{2,0,1:T(8,128)(2,1)}), bf16[112,8,640]{2,0,1:T(8,128)(2,1)}, u32[]{:S(2)}, u32[]{:S(2)}) async-start(bf16[112,8,640]{2,0,1:T(8,128)(2,1)} %bitcast.26), calls=%async_computation | async-start | bytes 2293760 | tf_op jit(solution)/shard_map/all_to_all | solution.py:168
  45.6 5.3 %copy-start = (bf16[1,8,112,640]{3,2,0,1:T(8,128)(2,1)}, bf16[1,8,112,640]{3,2,0,1:T(8,128)(2,1)S(1)}, u32[]{:S(2)}) copy-start(bf16[1,8,112,640]{3,2,0,1:T(8,128)(2,1)S(1)} %get-tuple-element.21) | copy-start | bytes 3440644
  45.6 4.5 %copy-start.1 = (bf16[1,8,112,640]{3,2,0,1:T(8,128)(2,1)S(1)}, bf16[1,8,112,640]{3,2,0,1:T(8,128)(2,1)}, u32[]{:S(2)}) copy-start(bf16[1,8,112,640]{3,2,0,1:T(8,128)(2,1)} %get-tuple-element.22) | copy-start | bytes 3440644
  45.6 6.0 %copy-start.5 = (s32[32]{0:T(128)S(1)}, s32[32]{0:T(128)}, u32[]{:S(2)}) copy-start(s32[32]{0:T(128)} %param.9) | copy-start | bytes 388
  45.7 26.2 %collective-permute-start = (bf16[512,640]{1,0:T(8,128)(2,1)S(1)}, bf16[512,640]{1,0:T(8,128)(2,1)}, u32[]{:S(2)}, u32[]{:S(2)}) collective-permute-start(bf16[512,640]{1,0:T(8,128)(2,1)S(1)} %constant_dynamic-slice_fusion.1), channel_id=1, source_target_pairs={{0,16},{16,32},{32,48},{48,64},{64,80},{80,96},{96,112},{112,128},... | collective-permute-start | bytes 1966088 | tf_op jit(solution)/shard_map/ppermute | solution.py:23
  50.9 7.5 %collective-permute-start.3 = (bf16[256,640]{1,0:T(8,128)(2,1)}, bf16[256,640]{1,0:T(8,128)(2,1)S(1)}, u32[]{:S(2)}, u32[]{:S(2)}) collective-permute-start(bf16[256,640]{1,0:T(8,128)(2,1)} %get-tuple-element.23), channel_id=1, source_target_pairs={{112,0},{240,128},{368,256},{113,1},{241,129},{369,257},{114,2},{2... | collective-permute-start | bytes 983048 | tf_op jit(solution)/shard_map/ppermute | solution.py:163
  54.2 38.1 %collective-permute-start.2 = (bf16[256,640]{1,0:T(8,128)(2,1)}, bf16[256,640]{1,0:T(8,128)(2,1)S(1)}, u32[]{:S(2)}, u32[]{:S(2)}) collective-permute-start(bf16[256,640]{1,0:T(8,128)(2,1)} %get-tuple-element.23), channel_id=1, source_target_pairs={{0,16},{16,32},{32,48},{48,64},{64,80},{80,96},{96,112},{128,144},... | collective-permute-start | bytes 983048 | tf_op jit(solution)/shard_map/ppermute | solution.py:162
  58.5 33.8 %collective-permute-start.4 = (bf16[256,640]{1,0:T(8,128)(2,1)S(1)}, bf16[256,640]{1,0:T(8,128)(2,1)S(1)}, u32[]{:S(2)}, u32[]{:S(2)}) collective-permute-start(bf16[256,640]{1,0:T(8,128)(2,1)S(1)} %collective-permute-done.3), channel_id=1, source_target_pairs={{0,128},{128,256},{256,384},{1,129},{129,257},{257,385},{2,130},{1... | collective-permute-start | bytes 983048 | tf_op jit(solution)/shard_map/ppermute | solution.py:162
  71.9 28.5 %collective-permute-start.1 = (bf16[256,640]{1,0:T(8,128)(2,1)S(1)}, bf16[256,640]{1,0:T(8,128)(2,1)S(1)}, u32[]{:S(2)}, u32[]{:S(2)}) collective-permute-start(bf16[256,640]{1,0:T(8,128)(2,1)S(1)} %get-tuple-element.15), channel_id=1, source_target_pairs={{0,16},{16,32},{32,48},{48,64},{64,80},{80,96},{96,112},{112,128},... | collective-permute-start | bytes 983048 | tf_op jit(solution)/shard_map/ppermute | solution.py:23

commit v11 on v7

--- a/solution.py
+++ b/solution.py
@@ -150,20 +150,19 @@
     kv_recv = lax.all_to_all(kv_send, "head", split_axis=0, concat_axis=0, tiled=True)
     kv_rows = kv_recv.transpose(1, 0, 2, 3).reshape(2, groups * rows, local)
     k_heads, v_heads = kv_rows[0], kv_rows[1]
-    k_tail = lax.dynamic_slice_in_dim(k_heads, tail_begin, tail, 0)
-    v_tail = lax.dynamic_slice_in_dim(v_heads, tail_begin, tail, 0)
-    k_prior = from_behind(k_tail, "stretch", 1)
+    kv_tail = lax.dynamic_slice_in_dim(kv_rows, tail_begin, tail, 1)
     inner, first, second = plan
     half = tail // 2
-    v_near = from_behind(v_tail[:half], "stretch", 1)
-    v_far = v_tail[half:]
+    direct = jnp.concatenate([kv_tail[0], kv_tail[1, :half]], axis=0)
+    direct_prior = from_behind(direct, "stretch", 1)
+    v_far = kv_tail[1, half:]
     if first:
         v_far = lax.ppermute(v_far, "stretch", inner) + lax.ppermute(
             lax.ppermute(v_far, "stretch", first), "stretch", second
         )
     else:
         v_far = from_behind(v_far, "stretch", 1)
-    v_prior = jnp.concatenate([v_near, v_far], axis=0)
+    v_prior = jnp.concatenate([direct_prior[tail:], v_far], axis=0)
     q_heads = lax.all_to_all(queries, "head", split_axis=1, concat_axis=0, tiled=True)
     span, local = q_heads.shape
     heads = local // HD
@@ -183,7 +182,7 @@
     w_mot, mtop, mtot = call(
         mscore_kernel,
         counts,
-        (q_heads, k_prior),
+        (q_heads, direct_prior),
         [rows_of(local), whole(tail, local)],
         [(heads * tail, jnp.bfloat16), (COLS, f32), (COLS, f32)],
         pl.CostEstimate(

time: 136 us -> 144 us (1.059)
  local copies, waits for them, and re-layouts: 7.2 us -> 11.6 us
  waiting for transfers between devices: 38.8 us -> 42.8 us
  starting transfers between devices: 26.2 us -> 22.6 us
  other arithmetic: 2.92 us -> 5.17 us
    ppermute x2 -> x1, starting transfers between devices: 8.55 us -> 4.27 us  [from_behind(): return lax.ppermute(shard, axis, pairs)]
    ppermute x1, waiting for transfers between devices: 0.01 us -> 3.09 us  [body(): lax.ppermute(v_far, 'stretch', inner)]
  transfers between devices with their start and end apart: 7 -> 6, of which waited for: 2 -> 3; matrix products, arithmetic and copies ran while one was open for 3% -> 6% of each run, Pallas kernels for 14% -> 8%
where the time goes in v11:
time: 144 us; the launch traced here: 143 us
  waiting for transfers between devices  42.8 us (30%)
  blocking collectives  34.6 us (24%)
  Pallas kernels  25.8 us (18%)
  starting transfers between devices  22.6 us (16%)
  local copies, waits for them, and re-layouts  11.6 us (8%)
  other arithmetic  5.17 us (4%)
    all_to_all x1, blocking collectives, body(): lax.all_to_all(mixed, 'head', split_axis=0, concat_axis=1, tiled=True)  34.6 us
    all_to_all x1, waiting for transfers between devices, body(): lax.all_to_all(kv_send, 'head', split_axis=0, concat_axis=0, tiled=True)  26.8 us
    pallas_call x3, Pallas kernels, call(): pl.pallas_call(kernel, out_shape=tuple(shapes), grid_spec=pltpu.PrefetchS...  25.8 us
    ppermute x1, waiting for transfers between devices, body(): lax.ppermute(lax.ppermute(v_far, 'stretch', first), 'stretch', second)  13 us
    all_to_all x1, starting transfers between devices, body(): lax.all_to_all(kv_send, 'head', split_axis=0, concat_axis=0, tiled=True)  5.89 us
    ppermute x1, starting transfers between devices, body(): lax.ppermute(v_far, 'stretch', inner)  5.01 us
    all_to_all x1, starting transfers between devices, body(): lax.all_to_all(queries, 'head', split_axis=1, concat_axis=0, tiled=True)  4.68 us
    ppermute x1, starting transfers between devices, from_behind(): return lax.ppermute(shard, axis, pairs)  4.27 us
  transfers between devices with their start and end apart: 6, of which 3 were waited for; matrix products, arithmetic and copies ran while one was open for 6% of the time, Pallas kernels for 8%

profile of v11, /device:TPU:56, one launch (start us, length us, event | category | flops | bytes accessed | tf_op | source)
XLA Modules:
  0.0 143.2 jit_solution(9944888989695085154)
XLA Ops:
  0.0 1.5 %copy.19 = bf16[14,8,8,640]{3,2,1,0:T(8,128)(2,1)S(1)} copy(bf16[14,8,8,640]{3,1,2,0:T(8,128)(2,1)} %bitcast.44) | data formatting | bytes 2293760
  2.0 1.7 %copy.14 = bf16[8,2,112,640]{3,2,1,0:T(8,128)(2,1)} copy(bf16[8,2,112,640]{3,0,2,1:T(8,128)(2,1)S(1)} %pad_maximum_fusion) | data formatting | bytes 4587520 | tf_op jit(solution)/shard_map/stack | solution.py:149
  3.7 5.9 %all-to-all-start.1 = ((bf16[8,2,112,640]{3,2,1,0:T(8,128)(2,1)}), bf16[8,2,112,640]{3,2,1,0:T(8,128)(2,1)S(1)}, u32[]{:S(2)}, u32[]{:S(2)}) async-start(bf16[8,2,112,640]{3,2,1,0:T(8,128)(2,1)} %copy.14), calls=%async_computation.1 | async-start | bytes 4587520 | tf_op jit(solution)/shard_map/all_to_all | solution.py:150
  9.6 1.1 copy.22
  10.7 26.8 %all-to-all-done.1 = bf16[8,2,112,640]{3,2,1,0:T(8,128)(2,1)S(1)} async-done(((bf16[8,2,112,640]{3,2,1,0:T(8,128)(2,1)}), bf16[8,2,112,640]{3,2,1,0:T(8,128)(2,1)S(1)}, u32[]{:S(2)}, u32[]{:S(2)}) %all-to-all-start.1) | async-done | bytes 2293792 | tf_op jit(solution)/shard_map/all_to_all | solution.py:150
  37.5 4.7 %all-to-all-start = ((bf16[112,8,640]{2,0,1:T(8,128)(2,1)}), bf16[112,8,640]{2,0,1:T(8,128)(2,1)S(1)}, u32[]{:S(2)}, u32[]{:S(2)}) async-start(bf16[112,8,640]{2,0,1:T(8,128)(2,1)} %bitcast.33), calls=%async_computation | async-start | bytes 2293760 | tf_op jit(solution)/shard_map/all_to_all | solution.py:166
  44.4 1.1 pad_maximum_fusion.1
  45.5 4.3 %collective-permute-start = (bf16[768,640]{1,0:T(8,128)(2,1)}, bf16[768,640]{1,0:T(8,128)(2,1)}, u32[]{:S(2)}, u32[]{:S(2)}) collective-permute-start(bf16[768,640]{1,0:T(8,128)(2,1)} %pad_maximum_fusion.1), channel_id=1, source_target_pairs={{0,16},{16,32},{32,48},{48,64},{64,80},{80,96},{96,112},{112,128},... | collective-permute-start | bytes 2949128 | tf_op jit(solution)/shard_map/ppermute | solution.py:23
  49.8 1.4 collective-permute-start.2
  51.8 1.8 %pad_add_fusion.counts = s32[2]{0:T(128)} fusion(s32[1]{0:T(128)} %dynamic_slice.10, s32[1]{0:T(128)} %dynamic_slice.9), kind=kLoop, calls=%fused_computation.7 | loop fusion | flops 2 | bytes 16 | tf_op jit(solution)/shard_map/stack | solution.py:140
  53.6 5.0 %collective-permute-start.1 = (bf16[256,640]{1,0:T(8,128)(2,1)}, bf16[256,640]{1,0:T(8,128)(2,1)}, u32[]{:S(2)}, u32[]{:S(2)}) collective-permute-start(bf16[256,640]{1,0:T(8,128)(2,1)} %get-tuple-element.19), channel_id=1, source_target_pairs={{0,16},{16,32},{32,48},{48,64},{64,80},{80,96},{96,112},{128,144},... | collective-permute-start | bytes 983048 | tf_op jit(solution)/shard_map/ppermute | solution.py:160
  58.6 1.3 collective-permute-start.3
  59.9 1.6 %fusion = (bf16[1,8,112,640]{3,2,0,1:T(8,128)(2,1)}, bf16[1,8,112,640]{3,2,0,1:T(8,128)(2,1)}) fusion(bf16[2,8,112,640]{3,2,0,1:T(8,128)(2,1)S(1)} %bitcast.35), kind=kLoop, calls=%fused_computation.8 | loop fusion | bytes 4587520 | tf_op jit(solution)/shard_map/slice | solution.py:152
  61.5 1.0 copy-done.2
  62.5 11.3 %shard_map.56 = (f32[896,640]{1,0:T(8,128)}, f32[896,8]{1,0:T(8,128)}, f32[896,8]{1,0:T(8,128)}) custom-call(s32[2]{0:T(128)} %pad_add_fusion.counts, bf16[896,640]{1,0:T(8,128)(2,1)} %bitcast.47, bf16[896,640]{1,0:T(8,128)(2,1)} %bitcast.43, bf16[896,640]{1,0:T(8,128)(2,1)} %bitcast.42), custom_call_target="tpu_custom_call" | custom-call | flops 3082813440 | bytes 5734400 | tf_op jit(solution)/shard_map/pallas_call | solution.py:108
  73.8 3.1 %collective-permute-done.1 = bf16[256,640]{1,0:T(8,128)(2,1)} collective-permute-done((bf16[256,640]{1,0:T(8,128)(2,1)}, bf16[256,640]{1,0:T(8,128)(2,1)}, u32[]{:S(2)}, u32[]{:S(2)}) %collective-permute-start.1) | collective-permute-done | bytes 327712 | tf_op jit(solution)/shard_map/ppermute | solution.py:160
  76.9 13.0 %collective-permute-done.3 = bf16[256,640]{1,0:T(8,128)(2,1)} collective-permute-done((bf16[256,640]{1,0:T(8,128)(2,1)}, bf16[256,640]{1,0:T(8,128)(2,1)}, u32[]{:S(2)}, u32[]{:S(2)}) %collective-permute-start.3) | collective-permute-done | bytes 327712 | tf_op jit(solution)/shard_map/ppermute | solution.py:160
  89.9 1.2 add.14
  91.1 1.0 slice.26
  92.1 1.0 pad_maximum_fusion.2.mv_ref
  93.0 7.2 %shard_map.55 = (bf16[896,2560]{1,0:T(8,128)(2,1)}, f32[896,8]{1,0:T(8,128)}, f32[896,8]{1,0:T(8,128)}) custom-call(s32[2]{0:T(128)} %pad_add_fusion.counts, bf16[896,640]{1,0:T(8,128)(2,1)} %bitcast.48, bf16[768,640]{1,0:T(8,128)(2,1)} %collective-permute-done.mk_ref), custom_call_target="tpu_custom_call" | custom-call | flops 1174405120 | bytes 6389760 | tf_op jit(solution)/shard_map/pallas_call | solution.py:108
  100.2 7.2 %shard_map.57 = bf16[896,640]{1,0:T(8,128)(2,1)} custom-call(s32[2]{0:T(128)} %pad_add_fusion.counts, bf16[896,2560]{1,0:T(8,128)(2,1)} %get-tuple-element.11.w_ref, bf16[512,640]{1,0:T(8,128)(2,1)} %pad_maximum_fusion.2.mv_ref, f32[896,640]{1,0:T(8,128)} %get-tuple-element.12.acc_ref, f32[896,8]{1,0:T(8,128)} %get-tuple-element.13.top_ref, ...), custom_call_target="tpu_custom_call" | custom-call | flops 587202560 | bytes 8683520 | tf_op jit(solution)/shard_map/pallas_call | solution.py:108
  107.4 34.6 %all_to_all.43 = bf16[8,112,640]{2,1,0:T(8,128)(2,1)S(1)} all-to-all(bf16[8,112,640]{2,1,0:T(8,128)(2,1)} %bitcast.41), channel_id=1, replica_groups=mesh['stretch'=32,'head'=8,'cfg'=2] {'head'}, dimensions={0} | all-to-all | bytes 2293760 | tf_op jit(solution)/shard_map/all_to_all | solution.py:214
  142.1 1.2 copy.18
  (19 shorter events, 2.8 us)
Async XLA Ops:
  0.0 1.6 %copy-start = (bf16[112,5120]{1,0:T(8,128)(2,1)S(1)}, bf16[112,5120]{1,0:T(8,128)(2,1)}, u32[]{:S(2)}) copy-start(bf16[112,5120]{1,0:T(8,128)(2,1)} %param.7) | copy-start | bytes 3440644
  3.7 5.9 %copy-start.1 = (bf16[112,5120]{1,0:T(8,128)(2,1)S(1)}, bf16[112,5120]{1,0:T(8,128)(2,1)}, u32[]{:S(2)}) copy-start(bf16[112,5120]{1,0:T(8,128)(2,1)} %param.5) | copy-start | bytes 3440644
  3.7 33.8 %all-to-all-start.1 = ((bf16[8,2,112,640]{3,2,1,0:T(8,128)(2,1)}), bf16[8,2,112,640]{3,2,1,0:T(8,128)(2,1)S(1)}, u32[]{:S(2)}, u32[]{:S(2)}) async-start(bf16[8,2,112,640]{3,2,1,0:T(8,128)(2,1)} %copy.14), calls=%async_computation.1 | async-start | bytes 4587520 | tf_op jit(solution)/shard_map/all_to_all | solution.py:150
  10.7 31.5 %copy-start.3 = (s32[32]{0:T(128)S(1)}, s32[32]{0:T(128)}, u32[]{:S(2)}) copy-start(s32[32]{0:T(128)} %param.8) | copy-start | bytes 388
  37.5 24.0 %all-to-all-start = ((bf16[112,8,640]{2,0,1:T(8,128)(2,1)}), bf16[112,8,640]{2,0,1:T(8,128)(2,1)S(1)}, u32[]{:S(2)}, u32[]{:S(2)}) async-start(bf16[112,8,640]{2,0,1:T(8,128)(2,1)} %bitcast.33), calls=%async_computation | async-start | bytes 2293760 | tf_op jit(solution)/shard_map/all_to_all | solution.py:166
  44.4 6.8 %copy-start.4 = (s32[32]{0:T(128)S(1)}, s32[32]{0:T(128)}, u32[]{:S(2)}) copy-start(s32[32]{0:T(128)} %param.9) | copy-start | bytes 388
  45.5 45.6 %collective-permute-start = (bf16[768,640]{1,0:T(8,128)(2,1)}, bf16[768,640]{1,0:T(8,128)(2,1)}, u32[]{:S(2)}, u32[]{:S(2)}) collective-permute-start(bf16[768,640]{1,0:T(8,128)(2,1)} %pad_maximum_fusion.1), channel_id=1, source_target_pairs={{0,16},{16,32},{32,48},{48,64},{64,80},{80,96},{96,112},{112,128},... | collective-permute-start | bytes 2949128 | tf_op jit(solution)/shard_map/ppermute | solution.py:23
  49.8 8.9 %collective-permute-start.2 = (bf16[256,640]{1,0:T(8,128)(2,1)}, bf16[256,640]{1,0:T(8,128)(2,1)}, u32[]{:S(2)}, u32[]{:S(2)}) collective-permute-start(bf16[256,640]{1,0:T(8,128)(2,1)} %get-tuple-element.19), channel_id=1, source_target_pairs={{112,0},{240,128},{368,256},{113,1},{241,129},{369,257},{114,2},{2... | collective-permute-start | bytes 983048 | tf_op jit(solution)/shard_map/ppermute | solution.py:161
  53.6 23.3 %collective-permute-start.1 = (bf16[256,640]{1,0:T(8,128)(2,1)}, bf16[256,640]{1,0:T(8,128)(2,1)}, u32[]{:S(2)}, u32[]{:S(2)}) collective-permute-start(bf16[256,640]{1,0:T(8,128)(2,1)} %get-tuple-element.19), channel_id=1, source_target_pairs={{0,16},{16,32},{32,48},{48,64},{64,80},{80,96},{96,112},{128,144},... | collective-permute-start | bytes 983048 | tf_op jit(solution)/shard_map/ppermute | solution.py:160
  58.6 31.3 %collective-permute-start.3 = (bf16[256,640]{1,0:T(8,128)(2,1)}, bf16[256,640]{1,0:T(8,128)(2,1)}, u32[]{:S(2)}, u32[]{:S(2)}) collective-permute-start(bf16[256,640]{1,0:T(8,128)(2,1)} %collective-permute-done.2), channel_id=1, source_target_pairs={{0,128},{128,256},{256,384},{1,129},{129,257},{257,385},{2,130},{1... | collective-permute-start | bytes 983048 | tf_op jit(solution)/shard_map/ppermute | solution.py:160
  61.5 1.0 copy-start.2

commit v12 on v7

--- a/solution.py
+++ b/solution.py
@@ -155,7 +155,7 @@
     k_prior = from_behind(k_tail, "stretch", 1)
     inner, first, second = plan
     half = tail // 2
-    v_near = from_behind(v_tail[:half], "stretch", 1)
+    v_near = v_tail[:half]
     v_far = v_tail[half:]
     if first:
         v_far = lax.ppermute(v_far, "stretch", inner) + lax.ppermute(
@@ -163,7 +163,6 @@
         )
     else:
         v_far = from_behind(v_far, "stretch", 1)
-    v_prior = jnp.concatenate([v_near, v_far], axis=0)
     q_heads = lax.all_to_all(queries, "head", split_axis=1, concat_axis=0, tiled=True)
     span, local = q_heads.shape
     heads = local // HD
@@ -180,6 +179,9 @@
             bytes_accessed=3 * span * local * 2 + span * local * 4,
         ),
     )
+    v_near, k_prior, acc = lax.optimization_barrier((v_near, k_prior, acc))
+    v_near = from_behind(v_near, "stretch", 1)
+    v_prior = jnp.concatenate([v_near, v_far], axis=0)
     w_mot, mtop, mtot = call(
         mscore_kernel,
         counts,

time: 136 us -> 138 us (1.015)
  waiting for transfers between devices: 38.8 us -> 47.2 us
  blocking collectives: 34 us -> 26.4 us
  local copies, waits for them, and re-layouts: 7.2 us -> 8.93 us
  starting transfers between devices: 26.2 us -> 24.7 us
    ppermute x2, waiting for transfers between devices: 0.01 us -> 12.3 us  [from_behind(): return lax.ppermute(shard, axis, pairs)]
    all_to_all x1, blocking collectives: 34 us -> 26.4 us  [body(): lax.all_to_all(mixed, 'head', split_axis=0, concat_axis=1, tiled=True)]
    ppermute x1, waiting for transfers between devices: 12 us -> 8.04 us  [body(): lax.ppermute(lax.ppermute(v_far, 'stretch', first), 'stretch', second)]
    ppermute x2, starting transfers between devices: 8.55 us -> 7.1 us  [from_behind(): return lax.ppermute(shard, axis, pairs)]
  transfers between devices with their start and end apart: 7 -> 7, of which waited for: 2 -> 4; matrix products, arithmetic and copies ran while one was open for 3% -> 4% of each run, Pallas kernels for 14% -> 14%
where the time goes in v12:
time: 138 us; the launch traced here: 137 us
  waiting for transfers between devices  47.2 us (34%)
  blocking collectives  26.4 us (19%)
  Pallas kernels  25.8 us (19%)
  starting transfers between devices  24.7 us (18%)
  local copies, waits for them, and re-layouts  8.93 us (6%)
  other arithmetic  2.96 us (2%)
    all_to_all x1, waiting for transfers between devices, body(): lax.all_to_all(kv_send, 'head', split_axis=0, concat_axis=0, tiled=True)  26.8 us
    all_to_all x1, blocking collectives, body(): lax.all_to_all(mixed, 'head', split_axis=0, concat_axis=1, tiled=True)  26.4 us
    pallas_call x3, Pallas kernels, call(): pl.pallas_call(kernel, out_shape=tuple(shapes), grid_spec=pltpu.PrefetchS...  25.8 us
    ppermute x2, waiting for transfers between devices, from_behind(): return lax.ppermute(shard, axis, pairs)  12.3 us
    ppermute x1, waiting for transfers between devices, body(): lax.ppermute(lax.ppermute(v_far, 'stretch', first), 'stretch', second)  8.04 us
    ppermute x2, starting transfers between devices, from_behind(): return lax.ppermute(shard, axis, pairs)  7.1 us
    all_to_all x1, starting transfers between devices, body(): lax.all_to_all(kv_send, 'head', split_axis=0, concat_axis=0, tiled=True)  5.89 us
    all_to_all x1, starting transfers between devices, body(): lax.all_to_all(queries, 'head', split_axis=1, concat_axis=0, tiled=True)  5.49 us
  transfers between devices with their start and end apart: 7, of which 4 were waited for; matrix products, arithmetic and copies ran while one was open for 4% of the time, Pallas kernels for 14%

profile of v12, /device:TPU:56, one launch (start us, length us, event | category | flops | bytes accessed | tf_op | source)
XLA Modules:
  0.0 136.6 jit_solution(6773016397074114556)
XLA Ops:
  0.0 1.5 %copy.17 = bf16[14,8,8,640]{3,2,1,0:T(8,128)(2,1)S(1)} copy(bf16[14,8,8,640]{3,1,2,0:T(8,128)(2,1)} %bitcast.36) | data formatting | bytes 2293760
  2.0 1.7 %copy.13 = bf16[8,2,112,640]{3,2,1,0:T(8,128)(2,1)} copy(bf16[8,2,112,640]{3,0,2,1:T(8,128)(2,1)S(1)} %pad_maximum_fusion) | data formatting | bytes 4587520 | tf_op jit(solution)/shard_map/stack | solution.py:149
  3.7 5.9 %all-to-all-start.1 = ((bf16[8,2,112,640]{3,2,1,0:T(8,128)(2,1)}), bf16[8,2,112,640]{3,2,1,0:T(8,128)(2,1)S(1)}, u32[]{:S(2)}, u32[]{:S(2)}) async-start(bf16[8,2,112,640]{3,2,1,0:T(8,128)(2,1)} %copy.13), calls=%async_computation.1 | async-start | bytes 4587520 | tf_op jit(solution)/shard_map/all_to_all | solution.py:150
  9.6 1.1 copy.20
  10.7 26.8 %all-to-all-done.1 = bf16[8,2,112,640]{3,2,1,0:T(8,128)(2,1)S(1)} async-done(((bf16[8,2,112,640]{3,2,1,0:T(8,128)(2,1)}), bf16[8,2,112,640]{3,2,1,0:T(8,128)(2,1)S(1)}, u32[]{:S(2)}, u32[]{:S(2)}) %all-to-all-start.1) | async-done | bytes 2293792 | tf_op jit(solution)/shard_map/all_to_all | solution.py:150
  37.5 5.5 %all-to-all-start = ((bf16[112,8,640]{2,0,1:T(8,128)(2,1)}), bf16[112,8,640]{2,0,1:T(8,128)(2,1)}, u32[]{:S(2)}, u32[]{:S(2)}) async-start(bf16[112,8,640]{2,0,1:T(8,128)(2,1)} %bitcast.26), calls=%async_computation | async-start | bytes 2293760 | tf_op jit(solution)/shard_map/all_to_all | solution.py:166
  44.1 1.2 fusion
  45.4 4.4 %collective-permute-start = (bf16[512,640]{1,0:T(8,128)(2,1)S(1)}, bf16[512,640]{1,0:T(8,128)(2,1)}, u32[]{:S(2)}, u32[]{:S(2)}) collective-permute-start(bf16[512,640]{1,0:T(8,128)(2,1)S(1)} %constant_dynamic-slice_fusion.1), channel_id=1, source_target_pairs={{0,16},{16,32},{32,48},{48,64},{64,80},{80,96},{96,112},{112,128},... | collective-permute-start | bytes 1966088 | tf_op jit(solution)/shard_map/ppermute | solution.py:23
  49.8 0.6 dynamic_slice.13
  50.4 0.8 constant_dynamic-slice_fusion.2
  51.2 0.7 collective-permute-start.3
  51.9 1.8 %pad_add_fusion.counts = s32[2]{0:T(128)} fusion(s32[1]{0:T(128)} %dynamic_slice.13, s32[1]{0:T(128)} %dynamic_slice.12), kind=kLoop, calls=%fused_computation.6 | loop fusion | flops 2 | bytes 16 | tf_op jit(solution)/shard_map/stack | solution.py:140
  53.6 4.3 %collective-permute-start.2 = (bf16[256,640]{1,0:T(8,128)(2,1)}, bf16[256,640]{1,0:T(8,128)(2,1)S(1)}, u32[]{:S(2)}, u32[]{:S(2)}) collective-permute-start(bf16[256,640]{1,0:T(8,128)(2,1)} %get-tuple-element.25), channel_id=1, source_target_pairs={{0,16},{16,32},{32,48},{48,64},{64,80},{80,96},{96,112},{128,144},... | collective-permute-start | bytes 983048 | tf_op jit(solution)/shard_map/ppermute | solution.py:161
  57.9 11.3 %shard_map.55 = (f32[896,640]{1,0:T(8,128)}, f32[896,8]{1,0:T(8,128)}, f32[896,8]{1,0:T(8,128)}) custom-call(s32[2]{0:T(128)} %pad_add_fusion.counts, bf16[896,640]{1,0:T(8,128)(2,1)} %bitcast.1.q_ref, bf16[896,640]{1,0:T(8,128)(2,1)} %bitcast.33, bf16[896,640]{1,0:T(8,128)(2,1)} %bitcast.34), custom_call_target="tpu_custom_call" | custom-call | flops 3082813440 | bytes 5734400 | tf_op jit(solution)/shard_map/pallas_call | solution.py:108
  69.3 1.3 collective-permute-start.4
  70.6 1.0 collective-permute-done.mk_ref
  71.5 2.7 %collective-permute-start.1 = (bf16[256,640]{1,0:T(8,128)(2,1)S(1)}, bf16[256,640]{1,0:T(8,128)(2,1)S(1)}, u32[]{:S(2)}, u32[]{:S(2)}) collective-permute-start(bf16[256,640]{1,0:T(8,128)(2,1)S(1)} %get-tuple-element.17), channel_id=1, source_target_pairs={{0,16},{16,32},{32,48},{48,64},{64,80},{80,96},{96,112},{112,128},... | collective-permute-start | bytes 983048 | tf_op jit(solution)/shard_map/ppermute | solution.py:23
  74.2 7.2 %shard_map.56 = (bf16[896,2560]{1,0:T(8,128)(2,1)}, f32[896,8]{1,0:T(8,128)}, f32[896,8]{1,0:T(8,128)}) custom-call(s32[2]{0:T(128)} %pad_add_fusion.counts, bf16[896,640]{1,0:T(8,128)(2,1)} %bitcast.1.q_ref, bf16[512,640]{1,0:T(8,128)(2,1)} %collective-permute-done.mk_ref), custom_call_target="tpu_custom_call" | custom-call | flops 1174405120 | bytes 6389760 | tf_op jit(solution)/shard_map/pallas_call | solution.py:108
  81.4 8.0 %collective-permute-done.4 = bf16[256,640]{1,0:T(8,128)(2,1)S(1)} collective-permute-done((bf16[256,640]{1,0:T(8,128)(2,1)S(1)}, bf16[256,640]{1,0:T(8,128)(2,1)S(1)}, u32[]{:S(2)}, u32[]{:S(2)}) %collective-permute-start.4) | collective-permute-done | bytes 327712 | tf_op jit(solution)/shard_map/ppermute | solution.py:161
  89.6 11.4 %collective-permute-done.1 = bf16[256,640]{1,0:T(8,128)(2,1)S(1)} collective-permute-done((bf16[256,640]{1,0:T(8,128)(2,1)S(1)}, bf16[256,640]{1,0:T(8,128)(2,1)S(1)}, u32[]{:S(2)}, u32[]{:S(2)}) %collective-permute-start.1) | collective-permute-done | bytes 327712 | tf_op jit(solution)/shard_map/ppermute | solution.py:23
  100.9 0.9 pad_maximum_fusion.1.mv_ref
  101.8 7.2 %shard_map.57 = bf16[896,640]{1,0:T(8,128)(2,1)} custom-call(s32[2]{0:T(128)} %pad_add_fusion.counts, bf16[896,2560]{1,0:T(8,128)(2,1)} %get-tuple-element.16.w_ref, bf16[512,640]{1,0:T(8,128)(2,1)} %pad_maximum_fusion.1.mv_ref, f32[896,640]{1,0:T(8,128)} %get-tuple-element.18.acc_ref, f32[896,8]{1,0:T(8,128)} %get-tuple-element.19.top_ref, ...), custom_call_target="tpu_custom_call" | custom-call | flops 587202560 | bytes 8683520 | tf_op jit(solution)/shard_map/pallas_call | solution.py:108
  109.0 26.4 %all_to_all.43 = bf16[8,112,640]{2,1,0:T(8,128)(2,1)S(1)} all-to-all(bf16[8,112,640]{2,1,0:T(8,128)(2,1)} %bitcast.31), channel_id=1, replica_groups=mesh['stretch'=32,'head'=8,'cfg'=2] {'head'}, dimensions={0} | all-to-all | bytes 2293760 | tf_op jit(solution)/shard_map/all_to_all | solution.py:217
  135.5 1.2 copy.16
  (20 shorter events, 1.2 us)
Async XLA Ops:
  0.0 1.6 %copy-start.2 = (bf16[112,5120]{1,0:T(8,128)(2,1)S(1)}, bf16[112,5120]{1,0:T(8,128)(2,1)}, u32[]{:S(2)}) copy-start(bf16[112,5120]{1,0:T(8,128)(2,1)} %param.7) | copy-start | bytes 3440644
  3.7 5.9 %copy-start.3 = (bf16[112,5120]{1,0:T(8,128)(2,1)S(1)}, bf16[112,5120]{1,0:T(8,128)(2,1)}, u32[]{:S(2)}) copy-start(bf16[112,5120]{1,0:T(8,128)(2,1)} %param.5) | copy-start | bytes 3440644
  3.7 33.8 %all-to-all-start.1 = ((bf16[8,2,112,640]{3,2,1,0:T(8,128)(2,1)}), bf16[8,2,112,640]{3,2,1,0:T(8,128)(2,1)S(1)}, u32[]{:S(2)}, u32[]{:S(2)}) async-start(bf16[8,2,112,640]{3,2,1,0:T(8,128)(2,1)} %copy.13), calls=%async_computation.1 | async-start | bytes 4587520 | tf_op jit(solution)/shard_map/all_to_all | solution.py:150
  37.5 5.5 %copy-start.4 = (s32[32]{0:T(128)S(1)}, s32[32]{0:T(128)}, u32[]{:S(2)}) copy-start(s32[32]{0:T(128)} %param.8) | copy-start | bytes 388
  37.5 20.4 %all-to-all-start = ((bf16[112,8,640]{2,0,1:T(8,128)(2,1)}), bf16[112,8,640]{2,0,1:T(8,128)(2,1)}, u32[]{:S(2)}, u32[]{:S(2)}) async-start(bf16[112,8,640]{2,0,1:T(8,128)(2,1)} %bitcast.26), calls=%async_computation | async-start | bytes 2293760 | tf_op jit(solution)/shard_map/all_to_all | solution.py:166
  45.3 5.9 %copy-start = (bf16[1,8,112,640]{3,2,0,1:T(8,128)(2,1)}, bf16[1,8,112,640]{3,2,0,1:T(8,128)(2,1)S(1)}, u32[]{:S(2)}) copy-start(bf16[1,8,112,640]{3,2,0,1:T(8,128)(2,1)S(1)} %get-tuple-element.23) | copy-start | bytes 3440644
  45.3 4.5 %copy-start.5 = (s32[32]{0:T(128)S(1)}, s32[32]{0:T(128)}, u32[]{:S(2)}) copy-start(s32[32]{0:T(128)} %param.9) | copy-start | bytes 388
  45.3 5.1 %copy-start.1 = (bf16[1,8,112,640]{3,2,0,1:T(8,128)(2,1)S(1)}, bf16[1,8,112,640]{3,2,0,1:T(8,128)(2,1)}, u32[]{:S(2)}) copy-start(bf16[1,8,112,640]{3,2,0,1:T(8,128)(2,1)} %get-tuple-element.24) | copy-start | bytes 3440644
  45.4 26.2 %collective-permute-start = (bf16[512,640]{1,0:T(8,128)(2,1)S(1)}, bf16[512,640]{1,0:T(8,128)(2,1)}, u32[]{:S(2)}, u32[]{:S(2)}) collective-permute-start(bf16[512,640]{1,0:T(8,128)(2,1)S(1)} %constant_dynamic-slice_fusion.1), channel_id=1, source_target_pairs={{0,16},{16,32},{32,48},{48,64},{64,80},{80,96},{96,112},{112,128},... | collective-permute-start | bytes 1966088 | tf_op jit(solution)/shard_map/ppermute | solution.py:23
  51.2 18.1 %collective-permute-start.3 = (bf16[256,640]{1,0:T(8,128)(2,1)}, bf16[256,640]{1,0:T(8,128)(2,1)S(1)}, u32[]{:S(2)}, u32[]{:S(2)}) collective-permute-start(bf16[256,640]{1,0:T(8,128)(2,1)} %get-tuple-element.25), channel_id=1, source_target_pairs={{112,0},{240,128},{368,256},{113,1},{241,129},{369,257},{114,2},{2... | collective-permute-start | bytes 983048 | tf_op jit(solution)/shard_map/ppermute | solution.py:162
  53.6 27.8 %collective-permute-start.2 = (bf16[256,640]{1,0:T(8,128)(2,1)}, bf16[256,640]{1,0:T(8,128)(2,1)S(1)}, u32[]{:S(2)}, u32[]{:S(2)}) collective-permute-start(bf16[256,640]{1,0:T(8,128)(2,1)} %get-tuple-element.25), channel_id=1, source_target_pairs={{0,16},{16,32},{32,48},{48,64},{64,80},{80,96},{96,112},{128,144},... | collective-permute-start | bytes 983048 | tf_op jit(solution)/shard_map/ppermute | solution.py:161
  69.3 20.2 %collective-permute-start.4 = (bf16[256,640]{1,0:T(8,128)(2,1)S(1)}, bf16[256,640]{1,0:T(8,128)(2,1)S(1)}, u32[]{:S(2)}, u32[]{:S(2)}) collective-permute-start(bf16[256,640]{1,0:T(8,128)(2,1)S(1)} %collective-permute-done.3), channel_id=1, source_target_pairs={{0,128},{128,256},{256,384},{1,129},{129,257},{257,385},{2,130},{1... | collective-permute-start | bytes 983048 | tf_op jit(solution)/shard_map/ppermute | solution.py:161
  71.5 29.4 %collective-permute-start.1 = (bf16[256,640]{1,0:T(8,128)(2,1)S(1)}, bf16[256,640]{1,0:T(8,128)(2,1)S(1)}, u32[]{:S(2)}, u32[]{:S(2)}) collective-permute-start(bf16[256,640]{1,0:T(8,128)(2,1)S(1)} %get-tuple-element.17), channel_id=1, source_target_pairs={{0,16},{16,32},{32,48},{48,64},{64,80},{80,96},{96,112},{112,128},... | collective-permute-start | bytes 983048 | tf_op jit(solution)/shard_map/ppermute | solution.py:23

commit v13 on v7

--- a/solution.py
+++ b/solution.py
@@ -154,7 +154,7 @@
     v_tail = lax.dynamic_slice_in_dim(v_heads, tail_begin, tail, 0)
     k_prior = from_behind(k_tail, "stretch", 1)
     inner, first, second = plan
-    half = tail // 2
+    half = tail // 4
     v_near = from_behind(v_tail[:half], "stretch", 1)
     v_far = v_tail[half:]
     if first:

time: 136 us -> 134 us (0.985)
  the two profiles are of different devices: /device:TPU:56 before, /device:TPU:16 now
where the time goes in v13:
time: 134 us
  waiting for transfers between devices  51.5 us (38%)
  Pallas kernels  25.8 us (19%)
  starting transfers between devices  23.7 us (18%)
  blocking collectives  20.7 us (15%)
  local copies, waits for them, and re-layouts  8.04 us (6%)
  other arithmetic  3.21 us (2%)
    all_to_all x1, waiting for transfers between devices, body(): lax.all_to_all(kv_send, 'head', split_axis=0, concat_axis=0, tiled=True)  28 us
    pallas_call x3, Pallas kernels, call(): pl.pallas_call(kernel, out_shape=tuple(shapes), grid_spec=pltpu.PrefetchS...  25.8 us
    ppermute x1, waiting for transfers between devices, body(): lax.ppermute(v_far, 'stretch', first)  23.5 us
    all_to_all x1, blocking collectives, body(): lax.all_to_all(mixed, 'head', split_axis=0, concat_axis=1, tiled=True)  20.7 us
    ppermute x2, starting transfers between devices, from_behind(): return lax.ppermute(shard, axis, pairs)  6.37 us
    all_to_all x1, starting transfers between devices, body(): lax.all_to_all(kv_send, 'head', split_axis=0, concat_axis=0, tiled=True)  5.44 us
    all_to_all x1, starting transfers between devices, body(): lax.all_to_all(queries, 'head', split_axis=1, concat_axis=0, tiled=True)  4.4 us
    ppermute x1, starting transfers between devices, body(): lax.ppermute(v_far, 'stretch', inner)  4.29 us
  transfers between devices with their start and end apart: 7, of which 2 were waited for; matrix products, arithmetic and copies ran while one was open for 4% of the time, Pallas kernels for 14%

profile of v13, /device:TPU:16, one launch (start us, length us, event | category | flops | bytes accessed | tf_op | source)
XLA Modules:
  0.0 133.8 jit_solution(4485088096460829818)
XLA Ops:
  0.0 1.5 %copy.17 = bf16[14,8,8,640]{3,2,1,0:T(8,128)(2,1)S(1)} copy(bf16[14,8,8,640]{3,1,2,0:T(8,128)(2,1)} %bitcast.37) | data formatting | bytes 2293760
  1.8 0.2 pad_maximum_fusion
  2.0 1.7 %copy.13 = bf16[8,2,112,640]{3,2,1,0:T(8,128)(2,1)} copy(bf16[8,2,112,640]{3,0,2,1:T(8,128)(2,1)S(1)} %pad_maximum_fusion) | data formatting | bytes 4587520 | tf_op jit(solution)/shard_map/stack | solution.py:149
  3.7 5.4 %all-to-all-start.1 = ((bf16[8,2,112,640]{3,2,1,0:T(8,128)(2,1)}), bf16[8,2,112,640]{3,2,1,0:T(8,128)(2,1)S(1)}, u32[]{:S(2)}, u32[]{:S(2)}) async-start(bf16[8,2,112,640]{3,2,1,0:T(8,128)(2,1)} %copy.13), calls=%async_computation.1 | async-start | bytes 4587520 | tf_op jit(solution)/shard_map/all_to_all | solution.py:150
  9.2 1.1 copy.20
  10.3 28.0 %all-to-all-done.1 = bf16[8,2,112,640]{3,2,1,0:T(8,128)(2,1)S(1)} async-done(((bf16[8,2,112,640]{3,2,1,0:T(8,128)(2,1)}), bf16[8,2,112,640]{3,2,1,0:T(8,128)(2,1)S(1)}, u32[]{:S(2)}, u32[]{:S(2)}) %all-to-all-start.1) | async-done | bytes 2293792 | tf_op jit(solution)/shard_map/all_to_all | solution.py:150
  38.2 4.4 %all-to-all-start = ((bf16[112,8,640]{2,0,1:T(8,128)(2,1)}), bf16[112,8,640]{2,0,1:T(8,128)(2,1)}, u32[]{:S(2)}, u32[]{:S(2)}) async-start(bf16[112,8,640]{2,0,1:T(8,128)(2,1)} %bitcast.26), calls=%async_computation | async-start | bytes 2293760 | tf_op jit(solution)/shard_map/all_to_all | solution.py:167
  42.7 0.7 dynamic_slice.12
  44.0 0.2 fusion
  44.3 1.3 collective-permute-start.3
  45.6 4.5 %collective-permute-start = (bf16[512,640]{1,0:T(8,128)(2,1)S(1)}, bf16[512,640]{1,0:T(8,128)(2,1)}, u32[]{:S(2)}, u32[]{:S(2)}) collective-permute-start(bf16[512,640]{1,0:T(8,128)(2,1)S(1)} %constant_dynamic-slice_fusion.2), channel_id=1, source_target_pairs={{0,16},{16,32},{32,48},{48,64},{64,80},{80,96},{96,112},{112,128},... | collective-permute-start | bytes 1966088 | tf_op jit(solution)/shard_map/ppermute | solution.py:23
  50.1 0.7 dynamic_slice.13
  50.8 2.0 %pad_add_fusion.counts = s32[2]{0:T(128)} fusion(s32[1]{0:T(128)} %dynamic_slice.13, s32[1]{0:T(128)} %dynamic_slice.12), kind=kLoop, calls=%fused_computation.6 | loop fusion | flops 2 | bytes 16 | tf_op jit(solution)/shard_map/stack | solution.py:140
  52.7 4.3 %collective-permute-start.2 = (bf16[384,640]{1,0:T(8,128)(2,1)S(1)}, bf16[384,640]{1,0:T(8,128)(2,1)S(1)}, u32[]{:S(2)}, u32[]{:S(2)}) collective-permute-start(bf16[384,640]{1,0:T(8,128)(2,1)S(1)} %constant_dynamic-slice_fusion.1), channel_id=1, source_target_pairs={{0,16},{16,32},{32,48},{48,64},{64,80},{80,96},{96,112},{128,144},... | collective-permute-start | bytes 1474568 | tf_op jit(solution)/shard_map/ppermute | solution.py:161
  57.1 23.5 %collective-permute-done.3 = bf16[384,640]{1,0:T(8,128)(2,1)} collective-permute-done((bf16[384,640]{1,0:T(8,128)(2,1)S(1)}, bf16[384,640]{1,0:T(8,128)(2,1)}, u32[]{:S(2)}, u32[]{:S(2)}) %collective-permute-start.3) | collective-permute-done | bytes 491552 | tf_op jit(solution)/shard_map/ppermute | solution.py:162
  80.6 1.9 %collective-permute-start.4 = (bf16[384,640]{1,0:T(8,128)(2,1)}, bf16[384,640]{1,0:T(8,128)(2,1)S(1)}, u32[]{:S(2)}, u32[]{:S(2)}) collective-permute-start(bf16[384,640]{1,0:T(8,128)(2,1)} %collective-permute-done.3), channel_id=1, source_target_pairs={{0,128},{128,256},{256,384},{1,129},{129,257},{257,385},{2,130},{1... | collective-permute-start | bytes 1474568 | tf_op jit(solution)/shard_map/ppermute | solution.py:161
  82.5 0.7 constant_dynamic-slice_fusion
  83.2 1.9 %collective-permute-start.1 = (bf16[128,640]{1,0:T(8,128)(2,1)}, bf16[128,640]{1,0:T(8,128)(2,1)S(1)}, u32[]{:S(2)}, u32[]{:S(2)}) collective-permute-start(bf16[128,640]{1,0:T(8,128)(2,1)} %constant_dynamic-slice_fusion), channel_id=1, source_target_pairs={{0,16},{16,32},{32,48},{48,64},{64,80},{80,96},{96,112},{112,128},... | collective-permute-start | bytes 491528 | tf_op jit(solution)/shard_map/ppermute | solution.py:23
  85.1 11.3 %shard_map.56 = (f32[896,640]{1,0:T(8,128)}, f32[896,8]{1,0:T(8,128)}, f32[896,8]{1,0:T(8,128)}) custom-call(s32[2]{0:T(128)} %pad_add_fusion.counts, bf16[896,640]{1,0:T(8,128)(2,1)} %bitcast.1.q_ref, bf16[896,640]{1,0:T(8,128)(2,1)} %bitcast.36, bf16[896,640]{1,0:T(8,128)(2,1)} %bitcast.34), custom_call_target="tpu_custom_call" | custom-call | flops 3082813440 | bytes 5734400 | tf_op jit(solution)/shard_map/pallas_call | solution.py:108
  96.4 7.2 %shard_map.55 = (bf16[896,2560]{1,0:T(8,128)(2,1)}, f32[896,8]{1,0:T(8,128)}, f32[896,8]{1,0:T(8,128)}) custom-call(s32[2]{0:T(128)} %pad_add_fusion.counts, bf16[896,640]{1,0:T(8,128)(2,1)} %bitcast.1.q_ref, bf16[512,640]{1,0:T(8,128)(2,1)} %collective-permute-done.mk_ref), custom_call_target="tpu_custom_call" | custom-call | flops 1174405120 | bytes 6389760 | tf_op jit(solution)/shard_map/pallas_call | solution.py:108
  103.8 0.9 pad_maximum_fusion.1.mv_ref
  104.7 7.2 %shard_map.57 = bf16[896,640]{1,0:T(8,128)(2,1)} custom-call(s32[2]{0:T(128)} %pad_add_fusion.counts, bf16[896,2560]{1,0:T(8,128)(2,1)} %get-tuple-element.11.w_ref, bf16[512,640]{1,0:T(8,128)(2,1)} %pad_maximum_fusion.1.mv_ref, f32[896,640]{1,0:T(8,128)} %get-tuple-element.12.acc_ref, f32[896,8]{1,0:T(8,128)} %get-tuple-element.13.top_ref, ...), custom_call_target="tpu_custom_call" | custom-call | flops 587202560 | bytes 8683520 | tf_op jit(solution)/shard_map/pallas_call | solution.py:108
  111.9 20.7 %all_to_all.43 = bf16[8,112,640]{2,1,0:T(8,128)(2,1)S(1)} all-to-all(bf16[8,112,640]{2,1,0:T(8,128)(2,1)} %bitcast.31), channel_id=1, replica_groups=mesh['stretch'=32,'head'=8,'cfg'=2] {'head'}, dimensions={0} | all-to-all | bytes 2293760 | tf_op jit(solution)/shard_map/all_to_all | solution.py:215
  132.6 1.2 copy.16
  (21 shorter events, 0.5 us)
Async XLA Ops:
  0.0 1.6 %copy-start.2 = (bf16[112,5120]{1,0:T(8,128)(2,1)S(1)}, bf16[112,5120]{1,0:T(8,128)(2,1)}, u32[]{:S(2)}) copy-start(bf16[112,5120]{1,0:T(8,128)(2,1)} %param.7) | copy-start | bytes 3440644
  3.7 5.4 %copy-start.3 = (bf16[112,5120]{1,0:T(8,128)(2,1)S(1)}, bf16[112,5120]{1,0:T(8,128)(2,1)}, u32[]{:S(2)}) copy-start(bf16[112,5120]{1,0:T(8,128)(2,1)} %param.5) | copy-start | bytes 3440644
  3.7 34.5 %all-to-all-start.1 = ((bf16[8,2,112,640]{3,2,1,0:T(8,128)(2,1)}), bf16[8,2,112,640]{3,2,1,0:T(8,128)(2,1)S(1)}, u32[]{:S(2)}, u32[]{:S(2)}) async-start(bf16[8,2,112,640]{3,2,1,0:T(8,128)(2,1)} %copy.13), calls=%async_computation.1 | async-start | bytes 4587520 | tf_op jit(solution)/shard_map/all_to_all | solution.py:150
  38.2 4.4 %copy-start.4 = (s32[32]{0:T(128)S(1)}, s32[32]{0:T(128)}, u32[]{:S(2)}) copy-start(s32[32]{0:T(128)} %param.8) | copy-start | bytes 388
  38.2 46.9 %all-to-all-start = ((bf16[112,8,640]{2,0,1:T(8,128)(2,1)}), bf16[112,8,640]{2,0,1:T(8,128)(2,1)}, u32[]{:S(2)}, u32[]{:S(2)}) async-start(bf16[112,8,640]{2,0,1:T(8,128)(2,1)} %bitcast.26), calls=%async_computation | async-start | bytes 2293760 | tf_op jit(solution)/shard_map/all_to_all | solution.py:167
  44.2 1.5 %copy-start.1 = (bf16[1,8,112,640]{3,2,0,1:T(8,128)(2,1)}, bf16[1,8,112,640]{3,2,0,1:T(8,128)(2,1)S(1)}, u32[]{:S(2)}) copy-start(bf16[1,8,112,640]{3,2,0,1:T(8,128)(2,1)S(1)} %get-tuple-element.18) | copy-start | bytes 3440644
  44.2 38.3 %copy-start = (bf16[1,8,112,640]{3,2,0,1:T(8,128)(2,1)}, bf16[1,8,112,640]{3,2,0,1:T(8,128)(2,1)S(1)}, u32[]{:S(2)}) copy-start(bf16[1,8,112,640]{3,2,0,1:T(8,128)(2,1)S(1)} %get-tuple-element.17) | copy-start | bytes 3440644
  44.2 5.9 %copy-start.5 = (s32[32]{0:T(128)S(1)}, s32[32]{0:T(128)}, u32[]{:S(2)}) copy-start(s32[32]{0:T(128)} %param.9) | copy-start | bytes 388
  44.3 36.3 %collective-permute-start.3 = (bf16[384,640]{1,0:T(8,128)(2,1)S(1)}, bf16[384,640]{1,0:T(8,128)(2,1)}, u32[]{:S(2)}, u32[]{:S(2)}) collective-permute-start(bf16[384,640]{1,0:T(8,128)(2,1)S(1)} %constant_dynamic-slice_fusion.1), channel_id=1, source_target_pairs={{112,0},{240,128},{368,256},{113,1},{241,129},{369,257},{114,2},{2... | collective-permute-start | bytes 1474568 | tf_op jit(solution)/shard_map/ppermute | solution.py:162
  45.6 50.8 %collective-permute-start = (bf16[512,640]{1,0:T(8,128)(2,1)S(1)}, bf16[512,640]{1,0:T(8,128)(2,1)}, u32[]{:S(2)}, u32[]{:S(2)}) collective-permute-start(bf16[512,640]{1,0:T(8,128)(2,1)S(1)} %constant_dynamic-slice_fusion.2), channel_id=1, source_target_pairs={{0,16},{16,32},{32,48},{48,64},{64,80},{80,96},{96,112},{112,128},... | collective-permute-start | bytes 1966088 | tf_op jit(solution)/shard_map/ppermute | solution.py:23
  52.7 50.9 %collective-permute-start.2 = (bf16[384,640]{1,0:T(8,128)(2,1)S(1)}, bf16[384,640]{1,0:T(8,128)(2,1)S(1)}, u32[]{:S(2)}, u32[]{:S(2)}) collective-permute-start(bf16[384,640]{1,0:T(8,128)(2,1)S(1)} %constant_dynamic-slice_fusion.1), channel_id=1, source_target_pairs={{0,16},{16,32},{32,48},{48,64},{64,80},{80,96},{96,112},{128,144},... | collective-permute-start | bytes 1474568 | tf_op jit(solution)/shard_map/ppermute | solution.py:161
  80.6 23.1 %collective-permute-start.4 = (bf16[384,640]{1,0:T(8,128)(2,1)}, bf16[384,640]{1,0:T(8,128)(2,1)S(1)}, u32[]{:S(2)}, u32[]{:S(2)}) collective-permute-start(bf16[384,640]{1,0:T(8,128)(2,1)} %collective-permute-done.3), channel_id=1, source_target_pairs={{0,128},{128,256},{256,384},{1,129},{129,257},{257,385},{2,130},{1... | collective-permute-start | bytes 1474568 | tf_op jit(solution)/shard_map/ppermute | solution.py:161
  83.2 20.6 %collective-permute-start.1 = (bf16[128,640]{1,0:T(8,128)(2,1)}, bf16[128,640]{1,0:T(8,128)(2,1)S(1)}, u32[]{:S(2)}, u32[]{:S(2)}) collective-permute-start(bf16[128,640]{1,0:T(8,128)(2,1)} %constant_dynamic-slice_fusion), channel_id=1, source_target_pairs={{0,16},{16,32},{32,48},{48,64},{64,80},{80,96},{96,112},{112,128},... | collective-permute-start | bytes 491528 | tf_op jit(solution)/shard_map/ppermute | solution.py:23

commit v14 on v13

--- a/solution.py
+++ b/solution.py
@@ -154,7 +154,7 @@
     v_tail = lax.dynamic_slice_in_dim(v_heads, tail_begin, tail, 0)
     k_prior = from_behind(k_tail, "stretch", 1)
     inner, first, second = plan
-    half = tail // 4
+    half = tail // 8
     v_near = from_behind(v_tail[:half], "stretch", 1)
     v_far = v_tail[half:]
     if first:

time: 134 us -> 142 us (1.060)
  the two profiles are of different devices: /device:TPU:16 before, /device:TPU:40 now
where the time goes in v14:
time: 142 us; the launch traced here: 141 us
  waiting for transfers between devices  56.1 us (40%)
  Pallas kernels  25.8 us (18%)
  starting transfers between devices  25.3 us (18%)
  blocking collectives  21.9 us (15%)
  local copies, waits for them, and re-layouts  7.27 us (5%)
  other arithmetic  4.18 us (3%)
    all_to_all x1, waiting for transfers between devices, body(): lax.all_to_all(kv_send, 'head', split_axis=0, concat_axis=0, tiled=True)  26.8 us
    pallas_call x3, Pallas kernels, call(): pl.pallas_call(kernel, out_shape=tuple(shapes), grid_spec=pltpu.PrefetchS...  25.8 us
    ppermute x1, waiting for transfers between devices, body(): lax.ppermute(v_far, 'stretch', first)  25.2 us
    all_to_all x1, blocking collectives, body(): lax.all_to_all(mixed, 'head', split_axis=0, concat_axis=1, tiled=True)  21.9 us
    ppermute x2, starting transfers between devices, from_behind(): return lax.ppermute(shard, axis, pairs)  6.42 us
    all_to_all x1, starting transfers between devices, body(): lax.all_to_all(kv_send, 'head', split_axis=0, concat_axis=0, tiled=True)  5.89 us
    all_to_all x1, starting transfers between devices, body(): lax.all_to_all(queries, 'head', split_axis=1, concat_axis=0, tiled=True)  5.49 us
    ppermute x1, starting transfers between devices, body(): lax.ppermute(v_far, 'stretch', inner)  4.3 us
  transfers between devices with their start and end apart: 7, of which 3 were waited for; matrix products, arithmetic and copies ran while one was open for 4% of the time, Pallas kernels for 13%

profile of v14, /device:TPU:40, one launch (start us, length us, event | category | flops | bytes accessed | tf_op | source)
XLA Modules:
  0.0 141.4 jit_solution(4973140728274347065)
XLA Ops:
  0.0 1.5 %copy.17 = bf16[14,8,8,640]{3,2,1,0:T(8,128)(2,1)S(1)} copy(bf16[14,8,8,640]{3,1,2,0:T(8,128)(2,1)} %bitcast.37) | data formatting | bytes 2293760
  1.8 0.2 pad_maximum_fusion
  2.0 1.7 %copy.13 = bf16[8,2,112,640]{3,2,1,0:T(8,128)(2,1)} copy(bf16[8,2,112,640]{3,0,2,1:T(8,128)(2,1)S(1)} %pad_maximum_fusion) | data formatting | bytes 4587520 | tf_op jit(solution)/shard_map/stack | solution.py:149
  3.7 5.9 %all-to-all-start.1 = ((bf16[8,2,112,640]{3,2,1,0:T(8,128)(2,1)}), bf16[8,2,112,640]{3,2,1,0:T(8,128)(2,1)S(1)}, u32[]{:S(2)}, u32[]{:S(2)}) async-start(bf16[8,2,112,640]{3,2,1,0:T(8,128)(2,1)} %copy.13), calls=%async_computation.1 | async-start | bytes 4587520 | tf_op jit(solution)/shard_map/all_to_all | solution.py:150
  9.6 1.1 copy.20
  10.7 26.8 %all-to-all-done.1 = bf16[8,2,112,640]{3,2,1,0:T(8,128)(2,1)S(1)} async-done(((bf16[8,2,112,640]{3,2,1,0:T(8,128)(2,1)}), bf16[8,2,112,640]{3,2,1,0:T(8,128)(2,1)S(1)}, u32[]{:S(2)}, u32[]{:S(2)}) %all-to-all-start.1) | async-done | bytes 2293792 | tf_op jit(solution)/shard_map/all_to_all | solution.py:150
  37.5 5.5 %all-to-all-start = ((bf16[112,8,640]{2,0,1:T(8,128)(2,1)}), bf16[112,8,640]{2,0,1:T(8,128)(2,1)}, u32[]{:S(2)}, u32[]{:S(2)}) async-start(bf16[112,8,640]{2,0,1:T(8,128)(2,1)} %bitcast.26), calls=%async_computation | async-start | bytes 2293760 | tf_op jit(solution)/shard_map/all_to_all | solution.py:167
  43.0 0.6 dynamic_slice.12
  44.5 1.3 collective-permute-start.3
  45.9 4.5 %collective-permute-start = (bf16[512,640]{1,0:T(8,128)(2,1)S(1)}, bf16[512,640]{1,0:T(8,128)(2,1)}, u32[]{:S(2)}, u32[]{:S(2)}) collective-permute-start(bf16[512,640]{1,0:T(8,128)(2,1)S(1)} %constant_dynamic-slice_fusion.2), channel_id=1, source_target_pairs={{0,16},{16,32},{32,48},{48,64},{64,80},{80,96},{96,112},{112,128},... | collective-permute-start | bytes 1966088 | tf_op jit(solution)/shard_map/ppermute | solution.py:23
  50.4 0.6 dynamic_slice.13
  51.1 4.3 %collective-permute-start.2 = (bf16[448,640]{1,0:T(8,128)(2,1)S(1)}, bf16[448,640]{1,0:T(8,128)(2,1)S(1)}, u32[]{:S(2)}, u32[]{:S(2)}) collective-permute-start(bf16[448,640]{1,0:T(8,128)(2,1)S(1)} %constant_dynamic-slice_fusion.1), channel_id=1, source_target_pairs={{0,16},{16,32},{32,48},{48,64},{64,80},{80,96},{96,112},{128,144},... | collective-permute-start | bytes 1720328 | tf_op jit(solution)/shard_map/ppermute | solution.py:161
  55.4 25.2 %collective-permute-done.3 = bf16[448,640]{1,0:T(8,128)(2,1)} collective-permute-done((bf16[448,640]{1,0:T(8,128)(2,1)S(1)}, bf16[448,640]{1,0:T(8,128)(2,1)}, u32[]{:S(2)}, u32[]{:S(2)}) %collective-permute-start.3) | collective-permute-done | bytes 573472 | tf_op jit(solution)/shard_map/ppermute | solution.py:162
  80.6 1.9 %collective-permute-start.4 = (bf16[448,640]{1,0:T(8,128)(2,1)}, bf16[448,640]{1,0:T(8,128)(2,1)}, u32[]{:S(2)}, u32[]{:S(2)}) collective-permute-start(bf16[448,640]{1,0:T(8,128)(2,1)} %collective-permute-done.3), channel_id=1, source_target_pairs={{0,128},{128,256},{256,384},{1,129},{129,257},{257,385},{2,130},{1... | collective-permute-start | bytes 1720328 | tf_op jit(solution)/shard_map/ppermute | solution.py:161
  82.5 1.9 %pad_add_fusion.counts = s32[2]{0:T(128)} fusion(s32[1]{0:T(128)} %dynamic_slice.13, s32[1]{0:T(128)} %dynamic_slice.12), kind=kLoop, calls=%fused_computation.6 | loop fusion | flops 2 | bytes 16 | tf_op jit(solution)/shard_map/stack | solution.py:140
  84.3 1.9 %collective-permute-start.1 = (bf16[64,640]{1,0:T(8,128)(2,1)S(1)}, bf16[64,640]{1,0:T(8,128)(2,1)S(1)}, u32[]{:S(2)}, u32[]{:S(2)}) collective-permute-start(bf16[64,640]{1,0:T(8,128)(2,1)S(1)} %constant_dynamic-slice_fusion), channel_id=1, source_target_pairs={{0,16},{16,32},{32,48},{48,64},{64,80},{80,96},{96,112},{112,128},... | collective-permute-start | bytes 245768 | tf_op jit(solution)/shard_map/ppermute | solution.py:23
  86.3 11.4 %shard_map.56 = (f32[896,640]{1,0:T(8,128)}, f32[896,8]{1,0:T(8,128)}, f32[896,8]{1,0:T(8,128)}) custom-call(s32[2]{0:T(128)} %pad_add_fusion.counts, bf16[896,640]{1,0:T(8,128)(2,1)} %bitcast.1.q_ref, bf16[896,640]{1,0:T(8,128)(2,1)} %bitcast.36, bf16[896,640]{1,0:T(8,128)(2,1)} %bitcast.34), custom_call_target="tpu_custom_call" | custom-call | flops 3082813440 | bytes 5734400 | tf_op jit(solution)/shard_map/pallas_call | solution.py:108
  97.6 7.2 %shard_map.55 = (bf16[896,2560]{1,0:T(8,128)(2,1)}, f32[896,8]{1,0:T(8,128)}, f32[896,8]{1,0:T(8,128)}) custom-call(s32[2]{0:T(128)} %pad_add_fusion.counts, bf16[896,640]{1,0:T(8,128)(2,1)} %bitcast.1.q_ref, bf16[512,640]{1,0:T(8,128)(2,1)} %collective-permute-done.mk_ref), custom_call_target="tpu_custom_call" | custom-call | flops 1174405120 | bytes 6389760 | tf_op jit(solution)/shard_map/pallas_call | solution.py:108
  104.8 4.2 %collective-permute-done.4 = bf16[448,640]{1,0:T(8,128)(2,1)} collective-permute-done((bf16[448,640]{1,0:T(8,128)(2,1)}, bf16[448,640]{1,0:T(8,128)(2,1)}, u32[]{:S(2)}, u32[]{:S(2)}) %collective-permute-start.4) | collective-permute-done | bytes 573472 | tf_op jit(solution)/shard_map/ppermute | solution.py:161
  109.0 1.2 add.15
  110.2 0.9 pad_maximum_fusion.1.mv_ref
  111.1 7.2 %shard_map.57 = bf16[896,640]{1,0:T(8,128)(2,1)} custom-call(s32[2]{0:T(128)} %pad_add_fusion.counts, bf16[896,2560]{1,0:T(8,128)(2,1)} %get-tuple-element.11.w_ref, bf16[512,640]{1,0:T(8,128)(2,1)} %pad_maximum_fusion.1.mv_ref, f32[896,640]{1,0:T(8,128)} %get-tuple-element.12.acc_ref, f32[896,8]{1,0:T(8,128)} %get-tuple-element.13.top_ref, ...), custom_call_target="tpu_custom_call" | custom-call | flops 587202560 | bytes 8683520 | tf_op jit(solution)/shard_map/pallas_call | solution.py:108
  118.3 21.9 %all_to_all.43 = bf16[8,112,640]{2,1,0:T(8,128)(2,1)S(1)} all-to-all(bf16[8,112,640]{2,1,0:T(8,128)(2,1)} %bitcast.31), channel_id=1, replica_groups=mesh['stretch'=32,'head'=8,'cfg'=2] {'head'}, dimensions={0} | all-to-all | bytes 2293760 | tf_op jit(solution)/shard_map/all_to_all | solution.py:215
  140.2 1.2 copy.16
  (21 shorter events, 0.6 us)
Async XLA Ops:
  0.0 1.6 %copy-start.2 = (bf16[112,5120]{1,0:T(8,128)(2,1)S(1)}, bf16[112,5120]{1,0:T(8,128)(2,1)}, u32[]{:S(2)}) copy-start(bf16[112,5120]{1,0:T(8,128)(2,1)} %param.7) | copy-start | bytes 3440644
  3.7 5.9 %copy-start.3 = (bf16[112,5120]{1,0:T(8,128)(2,1)S(1)}, bf16[112,5120]{1,0:T(8,128)(2,1)}, u32[]{:S(2)}) copy-start(bf16[112,5120]{1,0:T(8,128)(2,1)} %param.5) | copy-start | bytes 3440644
  3.7 33.8 %all-to-all-start.1 = ((bf16[8,2,112,640]{3,2,1,0:T(8,128)(2,1)}), bf16[8,2,112,640]{3,2,1,0:T(8,128)(2,1)S(1)}, u32[]{:S(2)}, u32[]{:S(2)}) async-start(bf16[8,2,112,640]{3,2,1,0:T(8,128)(2,1)} %copy.13), calls=%async_computation.1 | async-start | bytes 4587520 | tf_op jit(solution)/shard_map/all_to_all | solution.py:150
  37.5 5.5 %copy-start.4 = (s32[32]{0:T(128)S(1)}, s32[32]{0:T(128)}, u32[]{:S(2)}) copy-start(s32[32]{0:T(128)} %param.8) | copy-start | bytes 388
  37.5 48.8 %all-to-all-start = ((bf16[112,8,640]{2,0,1:T(8,128)(2,1)}), bf16[112,8,640]{2,0,1:T(8,128)(2,1)}, u32[]{:S(2)}, u32[]{:S(2)}) async-start(bf16[112,8,640]{2,0,1:T(8,128)(2,1)} %bitcast.26), calls=%async_computation | async-start | bytes 2293760 | tf_op jit(solution)/shard_map/all_to_all | solution.py:167
  44.4 1.5 %copy-start.1 = (bf16[1,8,112,640]{3,2,0,1:T(8,128)(2,1)}, bf16[1,8,112,640]{3,2,0,1:T(8,128)(2,1)S(1)}, u32[]{:S(2)}) copy-start(bf16[1,8,112,640]{3,2,0,1:T(8,128)(2,1)S(1)} %get-tuple-element.18) | copy-start | bytes 3440644
  44.4 39.9 %copy-start = (bf16[1,8,112,640]{3,2,0,1:T(8,128)(2,1)}, bf16[1,8,112,640]{3,2,0,1:T(8,128)(2,1)S(1)}, u32[]{:S(2)}) copy-start(bf16[1,8,112,640]{3,2,0,1:T(8,128)(2,1)S(1)} %get-tuple-element.17) | copy-start | bytes 3440644
  44.5 6.0 %copy-start.5 = (s32[32]{0:T(128)S(1)}, s32[32]{0:T(128)}, u32[]{:S(2)}) copy-start(s32[32]{0:T(128)} %param.9) | copy-start | bytes 388
  44.5 36.0 %collective-permute-start.3 = (bf16[448,640]{1,0:T(8,128)(2,1)S(1)}, bf16[448,640]{1,0:T(8,128)(2,1)}, u32[]{:S(2)}, u32[]{:S(2)}) collective-permute-start(bf16[448,640]{1,0:T(8,128)(2,1)S(1)} %constant_dynamic-slice_fusion.1), channel_id=1, source_target_pairs={{112,0},{240,128},{368,256},{113,1},{241,129},{369,257},{114,2},{2... | collective-permute-start | bytes 1720328 | tf_op jit(solution)/shard_map/ppermute | solution.py:162
  45.9 51.7 %collective-permute-start = (bf16[512,640]{1,0:T(8,128)(2,1)S(1)}, bf16[512,640]{1,0:T(8,128)(2,1)}, u32[]{:S(2)}, u32[]{:S(2)}) collective-permute-start(bf16[512,640]{1,0:T(8,128)(2,1)S(1)} %constant_dynamic-slice_fusion.2), channel_id=1, source_target_pairs={{0,16},{16,32},{32,48},{48,64},{64,80},{80,96},{96,112},{112,128},... | collective-permute-start | bytes 1966088 | tf_op jit(solution)/shard_map/ppermute | solution.py:23
  51.1 53.8 %collective-permute-start.2 = (bf16[448,640]{1,0:T(8,128)(2,1)S(1)}, bf16[448,640]{1,0:T(8,128)(2,1)S(1)}, u32[]{:S(2)}, u32[]{:S(2)}) collective-permute-start(bf16[448,640]{1,0:T(8,128)(2,1)S(1)} %constant_dynamic-slice_fusion.1), channel_id=1, source_target_pairs={{0,16},{16,32},{32,48},{48,64},{64,80},{80,96},{96,112},{128,144},... | collective-permute-start | bytes 1720328 | tf_op jit(solution)/shard_map/ppermute | solution.py:161
  80.6 28.4 %collective-permute-start.4 = (bf16[448,640]{1,0:T(8,128)(2,1)}, bf16[448,640]{1,0:T(8,128)(2,1)}, u32[]{:S(2)}, u32[]{:S(2)}) collective-permute-start(bf16[448,640]{1,0:T(8,128)(2,1)} %collective-permute-done.3), channel_id=1, source_target_pairs={{0,128},{128,256},{256,384},{1,129},{129,257},{257,385},{2,130},{1... | collective-permute-start | bytes 1720328 | tf_op jit(solution)/shard_map/ppermute | solution.py:161
  84.3 25.8 %collective-permute-start.1 = (bf16[64,640]{1,0:T(8,128)(2,1)S(1)}, bf16[64,640]{1,0:T(8,128)(2,1)S(1)}, u32[]{:S(2)}, u32[]{:S(2)}) collective-permute-start(bf16[64,640]{1,0:T(8,128)(2,1)S(1)} %constant_dynamic-slice_fusion), channel_id=1, source_target_pairs={{0,16},{16,32},{32,48},{48,64},{64,80},{80,96},{96,112},{112,128},... | collective-permute-start | bytes 245768 | tf_op jit(solution)/shard_map/ppermute | solution.py:23

commit v15 on v14

--- a/solution.py
+++ b/solution.py
@@ -154,7 +154,7 @@
     v_tail = lax.dynamic_slice_in_dim(v_heads, tail_begin, tail, 0)
     k_prior = from_behind(k_tail, "stretch", 1)
     inner, first, second = plan
-    half = tail // 8
+    half = 3 * tail // 8
     v_near = from_behind(v_tail[:half], "stretch", 1)
     v_far = v_tail[half:]
     if first:

time: 142 us -> 134 us (0.944)
  the two profiles are of different devices: /device:TPU:40 before, /device:TPU:56 now
where the time goes in v15:
time: 134 us
  waiting for transfers between devices  37.6 us (28%)
  blocking collectives  32.4 us (24%)
  starting transfers between devices  26.3 us (20%)
  Pallas kernels  25.8 us (19%)
  local copies, waits for them, and re-layouts  7.97 us (6%)
  other arithmetic  3.11 us (2%)
    all_to_all x1, blocking collectives, body(): lax.all_to_all(mixed, 'head', split_axis=0, concat_axis=1, tiled=True)  32.4 us
    all_to_all x1, waiting for transfers between devices, body(): lax.all_to_all(kv_send, 'head', split_axis=0, concat_axis=0, tiled=True)  26.8 us
    pallas_call x3, Pallas kernels, call(): pl.pallas_call(kernel, out_shape=tuple(shapes), grid_spec=pltpu.PrefetchS...  25.8 us
    ppermute x2, starting transfers between devices, from_behind(): return lax.ppermute(shard, axis, pairs)  7.92 us
    ppermute x1, waiting for transfers between devices, body(): lax.ppermute(lax.ppermute(v_far, 'stretch', first), 'stretch', second)  6.92 us
    all_to_all x1, starting transfers between devices, body(): lax.all_to_all(kv_send, 'head', split_axis=0, concat_axis=0, tiled=True)  5.89 us
    all_to_all x1, starting transfers between devices, body(): lax.all_to_all(queries, 'head', split_axis=1, concat_axis=0, tiled=True)  5.49 us
    ppermute x1, starting transfers between devices, body(): lax.ppermute(v_far, 'stretch', inner)  4.29 us
  transfers between devices with their start and end apart: 7, of which 3 were waited for; matrix products, arithmetic and copies ran while one was open for 4% of the time, Pallas kernels for 14%

profile of v15, /device:TPU:56, one launch (start us, length us, event | category | flops | bytes accessed | tf_op | source)
XLA Modules:
  0.0 133.9 jit_solution(4572427102921211059)
XLA Ops:
  0.0 1.5 %copy.17 = bf16[14,8,8,640]{3,2,1,0:T(8,128)(2,1)S(1)} copy(bf16[14,8,8,640]{3,1,2,0:T(8,128)(2,1)} %bitcast.37) | data formatting | bytes 2293760
  1.8 0.2 pad_maximum_fusion
  2.0 1.7 %copy.13 = bf16[8,2,112,640]{3,2,1,0:T(8,128)(2,1)} copy(bf16[8,2,112,640]{3,0,2,1:T(8,128)(2,1)S(1)} %pad_maximum_fusion) | data formatting | bytes 4587520 | tf_op jit(solution)/shard_map/stack | solution.py:149
  3.7 5.9 %all-to-all-start.1 = ((bf16[8,2,112,640]{3,2,1,0:T(8,128)(2,1)}), bf16[8,2,112,640]{3,2,1,0:T(8,128)(2,1)S(1)}, u32[]{:S(2)}, u32[]{:S(2)}) async-start(bf16[8,2,112,640]{3,2,1,0:T(8,128)(2,1)} %copy.13), calls=%async_computation.1 | async-start | bytes 4587520 | tf_op jit(solution)/shard_map/all_to_all | solution.py:150
  9.6 1.1 copy.20
  10.7 26.8 %all-to-all-done.1 = bf16[8,2,112,640]{3,2,1,0:T(8,128)(2,1)S(1)} async-done(((bf16[8,2,112,640]{3,2,1,0:T(8,128)(2,1)}), bf16[8,2,112,640]{3,2,1,0:T(8,128)(2,1)S(1)}, u32[]{:S(2)}, u32[]{:S(2)}) %all-to-all-start.1) | async-done | bytes 2293792 | tf_op jit(solution)/shard_map/all_to_all | solution.py:150
  37.5 5.5 %all-to-all-start = ((bf16[112,8,640]{2,0,1:T(8,128)(2,1)}), bf16[112,8,640]{2,0,1:T(8,128)(2,1)}, u32[]{:S(2)}, u32[]{:S(2)}) async-start(bf16[112,8,640]{2,0,1:T(8,128)(2,1)} %bitcast.26), calls=%async_computation | async-start | bytes 2293760 | tf_op jit(solution)/shard_map/all_to_all | solution.py:167
  43.0 0.6 dynamic_slice.12
  44.5 1.4 %collective-permute-start.3 = (bf16[320,640]{1,0:T(8,128)(2,1)S(1)}, bf16[320,640]{1,0:T(8,128)(2,1)}, u32[]{:S(2)}, u32[]{:S(2)}) collective-permute-start(bf16[320,640]{1,0:T(8,128)(2,1)S(1)} %constant_dynamic-slice_fusion.1), channel_id=1, source_target_pairs={{112,0},{240,128},{368,256},{113,1},{241,129},{369,257},{114,2},{2... | collective-permute-start | bytes 1228808 | tf_op jit(solution)/shard_map/ppermute | solution.py:162
  46.0 4.3 %collective-permute-start = (bf16[512,640]{1,0:T(8,128)(2,1)S(1)}, bf16[512,640]{1,0:T(8,128)(2,1)}, u32[]{:S(2)}, u32[]{:S(2)}) collective-permute-start(bf16[512,640]{1,0:T(8,128)(2,1)S(1)} %constant_dynamic-slice_fusion.2), channel_id=1, source_target_pairs={{0,16},{16,32},{32,48},{48,64},{64,80},{80,96},{96,112},{112,128},... | collective-permute-start | bytes 1966088 | tf_op jit(solution)/shard_map/ppermute | solution.py:23
  50.3 0.6 dynamic_slice.13
  50.9 1.9 %pad_add_fusion.counts = s32[2]{0:T(128)} fusion(s32[1]{0:T(128)} %dynamic_slice.13, s32[1]{0:T(128)} %dynamic_slice.12), kind=kLoop, calls=%fused_computation.6 | loop fusion | flops 2 | bytes 16 | tf_op jit(solution)/shard_map/stack | solution.py:140
  52.8 4.3 %collective-permute-start.2 = (bf16[320,640]{1,0:T(8,128)(2,1)S(1)}, bf16[320,640]{1,0:T(8,128)(2,1)S(1)}, u32[]{:S(2)}, u32[]{:S(2)}) collective-permute-start(bf16[320,640]{1,0:T(8,128)(2,1)S(1)} %constant_dynamic-slice_fusion.1), channel_id=1, source_target_pairs={{0,16},{16,32},{32,48},{48,64},{64,80},{80,96},{96,112},{128,144},... | collective-permute-start | bytes 1228808 | tf_op jit(solution)/shard_map/ppermute | solution.py:161
  57.1 1.3 collective-permute-start.4
  58.4 0.7 constant_dynamic-slice_fusion
  59.1 3.6 %collective-permute-start.1 = (bf16[192,640]{1,0:T(8,128)(2,1)}, bf16[192,640]{1,0:T(8,128)(2,1)S(1)}, u32[]{:S(2)}, u32[]{:S(2)}) collective-permute-start(bf16[192,640]{1,0:T(8,128)(2,1)} %constant_dynamic-slice_fusion), channel_id=1, source_target_pairs={{0,16},{16,32},{32,48},{48,64},{64,80},{80,96},{96,112},{112,128},... | collective-permute-start | bytes 737288 | tf_op jit(solution)/shard_map/ppermute | solution.py:23
  62.8 11.3 %shard_map.56 = (f32[896,640]{1,0:T(8,128)}, f32[896,8]{1,0:T(8,128)}, f32[896,8]{1,0:T(8,128)}) custom-call(s32[2]{0:T(128)} %pad_add_fusion.counts, bf16[896,640]{1,0:T(8,128)(2,1)} %bitcast.1.q_ref, bf16[896,640]{1,0:T(8,128)(2,1)} %bitcast.33, bf16[896,640]{1,0:T(8,128)(2,1)} %bitcast.36), custom_call_target="tpu_custom_call" | custom-call | flops 3082813440 | bytes 5734400 | tf_op jit(solution)/shard_map/pallas_call | solution.py:108
  74.1 7.2 %shard_map.55 = (bf16[896,2560]{1,0:T(8,128)(2,1)}, f32[896,8]{1,0:T(8,128)}, f32[896,8]{1,0:T(8,128)}) custom-call(s32[2]{0:T(128)} %pad_add_fusion.counts, bf16[896,640]{1,0:T(8,128)(2,1)} %bitcast.1.q_ref, bf16[512,640]{1,0:T(8,128)(2,1)} %collective-permute-done.mk_ref), custom_call_target="tpu_custom_call" | custom-call | flops 1174405120 | bytes 6389760 | tf_op jit(solution)/shard_map/pallas_call | solution.py:108
  81.3 6.9 %collective-permute-done.4 = bf16[320,640]{1,0:T(8,128)(2,1)S(1)} collective-permute-done((bf16[320,640]{1,0:T(8,128)(2,1)}, bf16[320,640]{1,0:T(8,128)(2,1)S(1)}, u32[]{:S(2)}, u32[]{:S(2)}) %collective-permute-start.4) | collective-permute-done | bytes 409632 | tf_op jit(solution)/shard_map/ppermute | solution.py:161
  88.3 3.9 %collective-permute-done.1 = bf16[192,640]{1,0:T(8,128)(2,1)S(1)} collective-permute-done((bf16[192,640]{1,0:T(8,128)(2,1)}, bf16[192,640]{1,0:T(8,128)(2,1)S(1)}, u32[]{:S(2)}, u32[]{:S(2)}) %collective-permute-start.1) | collective-permute-done | bytes 245792 | tf_op jit(solution)/shard_map/ppermute | solution.py:23
  92.2 0.9 pad_maximum_fusion.1.mv_ref
  93.1 7.2 %shard_map.57 = bf16[896,640]{1,0:T(8,128)(2,1)} custom-call(s32[2]{0:T(128)} %pad_add_fusion.counts, bf16[896,2560]{1,0:T(8,128)(2,1)} %get-tuple-element.11.w_ref, bf16[512,640]{1,0:T(8,128)(2,1)} %pad_maximum_fusion.1.mv_ref, f32[896,640]{1,0:T(8,128)} %get-tuple-element.12.acc_ref, f32[896,8]{1,0:T(8,128)} %get-tuple-element.13.top_ref, ...), custom_call_target="tpu_custom_call" | custom-call | flops 587202560 | bytes 8683520 | tf_op jit(solution)/shard_map/pallas_call | solution.py:108
  100.3 32.4 %all_to_all.43 = bf16[8,112,640]{2,1,0:T(8,128)(2,1)S(1)} all-to-all(bf16[8,112,640]{2,1,0:T(8,128)(2,1)} %bitcast.31), channel_id=1, replica_groups=mesh['stretch'=32,'head'=8,'cfg'=2] {'head'}, dimensions={0} | all-to-all | bytes 2293760 | tf_op jit(solution)/shard_map/all_to_all | solution.py:215
  132.7 1.2 copy.16
  (21 shorter events, 0.7 us)
Async XLA Ops:
  0.0 1.6 %copy-start.2 = (bf16[112,5120]{1,0:T(8,128)(2,1)S(1)}, bf16[112,5120]{1,0:T(8,128)(2,1)}, u32[]{:S(2)}) copy-start(bf16[112,5120]{1,0:T(8,128)(2,1)} %param.7) | copy-start | bytes 3440644
  3.7 5.9 %copy-start.3 = (bf16[112,5120]{1,0:T(8,128)(2,1)S(1)}, bf16[112,5120]{1,0:T(8,128)(2,1)}, u32[]{:S(2)}) copy-start(bf16[112,5120]{1,0:T(8,128)(2,1)} %param.5) | copy-start | bytes 3440644
  3.7 33.8 %all-to-all-start.1 = ((bf16[8,2,112,640]{3,2,1,0:T(8,128)(2,1)}), bf16[8,2,112,640]{3,2,1,0:T(8,128)(2,1)S(1)}, u32[]{:S(2)}, u32[]{:S(2)}) async-start(bf16[8,2,112,640]{3,2,1,0:T(8,128)(2,1)} %copy.13), calls=%async_computation.1 | async-start | bytes 4587520 | tf_op jit(solution)/shard_map/all_to_all | solution.py:150
  37.5 5.5 %copy-start.4 = (s32[32]{0:T(128)S(1)}, s32[32]{0:T(128)}, u32[]{:S(2)}) copy-start(s32[32]{0:T(128)} %param.8) | copy-start | bytes 388
  37.5 25.3 %all-to-all-start = ((bf16[112,8,640]{2,0,1:T(8,128)(2,1)}), bf16[112,8,640]{2,0,1:T(8,128)(2,1)}, u32[]{:S(2)}, u32[]{:S(2)}) async-start(bf16[112,8,640]{2,0,1:T(8,128)(2,1)} %bitcast.26), calls=%async_computation | async-start | bytes 2293760 | tf_op jit(solution)/shard_map/all_to_all | solution.py:167
  44.4 14.7 %copy-start = (bf16[1,8,112,640]{3,2,0,1:T(8,128)(2,1)}, bf16[1,8,112,640]{3,2,0,1:T(8,128)(2,1)S(1)}, u32[]{:S(2)}) copy-start(bf16[1,8,112,640]{3,2,0,1:T(8,128)(2,1)S(1)} %get-tuple-element.18) | copy-start | bytes 3440644
  44.4 14.7 %copy-start.1 = (bf16[1,8,112,640]{3,2,0,1:T(8,128)(2,1)}, bf16[1,8,112,640]{3,2,0,1:T(8,128)(2,1)S(1)}, u32[]{:S(2)}) copy-start(bf16[1,8,112,640]{3,2,0,1:T(8,128)(2,1)S(1)} %get-tuple-element.17) | copy-start | bytes 3440644
  44.4 5.8 %copy-start.5 = (s32[32]{0:T(128)S(1)}, s32[32]{0:T(128)}, u32[]{:S(2)}) copy-start(s32[32]{0:T(128)} %param.9) | copy-start | bytes 388
  44.5 12.6 %collective-permute-start.3 = (bf16[320,640]{1,0:T(8,128)(2,1)S(1)}, bf16[320,640]{1,0:T(8,128)(2,1)}, u32[]{:S(2)}, u32[]{:S(2)}) collective-permute-start(bf16[320,640]{1,0:T(8,128)(2,1)S(1)} %constant_dynamic-slice_fusion.1), channel_id=1, source_target_pairs={{112,0},{240,128},{368,256},{113,1},{241,129},{369,257},{114,2},{2... | collective-permute-start | bytes 1228808 | tf_op jit(solution)/shard_map/ppermute | solution.py:162
  46.0 28.1 %collective-permute-start = (bf16[512,640]{1,0:T(8,128)(2,1)S(1)}, bf16[512,640]{1,0:T(8,128)(2,1)}, u32[]{:S(2)}, u32[]{:S(2)}) collective-permute-start(bf16[512,640]{1,0:T(8,128)(2,1)S(1)} %constant_dynamic-slice_fusion.2), channel_id=1, source_target_pairs={{0,16},{16,32},{32,48},{48,64},{64,80},{80,96},{96,112},{112,128},... | collective-permute-start | bytes 1966088 | tf_op jit(solution)/shard_map/ppermute | solution.py:23
  52.8 28.5 %collective-permute-start.2 = (bf16[320,640]{1,0:T(8,128)(2,1)S(1)}, bf16[320,640]{1,0:T(8,128)(2,1)S(1)}, u32[]{:S(2)}, u32[]{:S(2)}) collective-permute-start(bf16[320,640]{1,0:T(8,128)(2,1)S(1)} %constant_dynamic-slice_fusion.1), channel_id=1, source_target_pairs={{0,16},{16,32},{32,48},{48,64},{64,80},{80,96},{96,112},{128,144},... | collective-permute-start | bytes 1228808 | tf_op jit(solution)/shard_map/ppermute | solution.py:161
  57.1 31.1 %collective-permute-start.4 = (bf16[320,640]{1,0:T(8,128)(2,1)}, bf16[320,640]{1,0:T(8,128)(2,1)S(1)}, u32[]{:S(2)}, u32[]{:S(2)}) collective-permute-start(bf16[320,640]{1,0:T(8,128)(2,1)} %collective-permute-done.3), channel_id=1, source_target_pairs={{0,128},{128,256},{256,384},{1,129},{129,257},{257,385},{2,130},{1... | collective-permute-start | bytes 1228808 | tf_op jit(solution)/shard_map/ppermute | solution.py:161
  59.1 33.1 %collective-permute-start.1 = (bf16[192,640]{1,0:T(8,128)(2,1)}, bf16[192,640]{1,0:T(8,128)(2,1)S(1)}, u32[]{:S(2)}, u32[]{:S(2)}) collective-permute-start(bf16[192,640]{1,0:T(8,128)(2,1)} %constant_dynamic-slice_fusion), channel_id=1, source_target_pairs={{0,16},{16,32},{32,48},{48,64},{64,80},{80,96},{96,112},{112,128},... | collective-permute-start | bytes 737288 | tf_op jit(solution)/shard_map/ppermute | solution.py:23

commit v16 on v13

--- a/solution.py
+++ b/solution.py
@@ -15,6 +15,7 @@
 NEG = -1e30
 TQ = 448
 COLS = 8
+PAIR = 2 * COLS
 
 
 def from_behind(shard, axis, by):
@@ -35,7 +36,7 @@
     return slice(h * HD, (h + 1) * HD)
 
 
-def own_kernel(counts, q_ref, k_ref, v_ref, acc_ref, top_ref, tot_ref):
+def own_kernel(counts, q_ref, k_ref, v_ref, acc_ref, stat_ref):
     own_live = counts[0] * FT
     span = k_ref.shape[0]
     key_live = lax.broadcasted_iota(jnp.int32, (1, span), 1) < own_live
@@ -48,11 +49,11 @@
         v_ext = jnp.concatenate([v, jnp.ones_like(v)], axis=1)
         both = jnp.dot(weights, v_ext, preferred_element_type=jnp.float32)
         acc_ref[:, c] = both[:, :HD]
-        top_ref[:, h : h + 1] = top
-        tot_ref[:, h : h + 1] = both[:, HD : HD + 1]
-
-
-def mscore_kernel(counts, q_ref, mk_ref, w_ref, top_ref, tot_ref):
+        stat_ref[:, h : h + 1] = top
+        stat_ref[:, COLS + h : COLS + h + 1] = both[:, HD : HD + 1]
+
+
+def mscore_kernel(counts, q_ref, mk_ref, w_ref, stat_ref):
     mot_start = (MOT_CAP - counts[1]) * FT
     tail = mk_ref.shape[0]
     slot_live = lax.broadcasted_iota(jnp.int32, (1, tail), 1) >= mot_start
@@ -64,12 +65,12 @@
         weights = jnp.exp(masked - top).astype(jnp.bfloat16)
         w_ref[:, h * tail : (h + 1) * tail] = weights
         total = jnp.dot(weights, ones, preferred_element_type=jnp.float32)
-        top_ref[:, h : h + 1] = top
-        tot_ref[:, h : h + 1] = total[:, 0:1]
+        stat_ref[:, h : h + 1] = top
+        stat_ref[:, COLS + h : COLS + h + 1] = total[:, 0:1]
 
 
 def merge_kernel(
-    counts, w_ref, mv_ref, acc_ref, top_ref, tot_ref, mtop_ref, mtot_ref, o_ref
+    counts, w_ref, mv_ref, acc_ref, own_ref, mot_ref, o_ref
 ):
     own_live = counts[0] * FT
     tail = mv_ref.shape[0]
@@ -82,13 +83,14 @@
             mv_ref[:, c],
             preferred_element_type=jnp.float32,
         )
-        top_own = top_ref[:, h : h + 1]
-        top_mot = mtop_ref[:, h : h + 1]
+        top_own = own_ref[:, h : h + 1]
+        top_mot = mot_ref[:, h : h + 1]
         peak = jnp.maximum(top_own, top_mot)
         factor_own = jnp.exp(top_own - peak)
         factor_mot = jnp.exp(top_mot - peak)
         scale = 1.0 / (
-            tot_ref[:, h : h + 1] * factor_own + mtot_ref[:, h : h + 1] * factor_mot
+            own_ref[:, COLS + h : COLS + h + 1] * factor_own
+            + mot_ref[:, COLS + h : COLS + h + 1] * factor_mot
         )
         mixed = (acc_ref[:, c] * factor_own + acc_mot * factor_mot) * scale
         o_ref[:, c] = jnp.where(row_live, mixed, 0.0).astype(o_ref.dtype)
@@ -168,24 +170,24 @@
     span, local = q_heads.shape
     heads = local // HD
     f32 = jnp.float32
-    acc, top, tot = call(
+    acc, own_stat = call(
         own_kernel,
         counts,
         (q_heads, k_heads, v_heads),
         [rows_of(local), whole(span, local), whole(span, local)],
-        [(local, f32), (COLS, f32), (COLS, f32)],
+        [(local, f32), (PAIR, f32)],
         pl.CostEstimate(
             flops=heads * 2 * span * span * 3 * HD,
             transcendentals=heads * span * span,
             bytes_accessed=3 * span * local * 2 + span * local * 4,
         ),
     )
-    w_mot, mtop, mtot = call(
+    w_mot, mot_stat = call(
         mscore_kernel,
         counts,
         (q_heads, k_prior),
         [rows_of(local), whole(tail, local)],
-        [(heads * tail, jnp.bfloat16), (COLS, f32), (COLS, f32)],
+        [(heads * tail, jnp.bfloat16), (PAIR, f32)],
         pl.CostEstimate(
             flops=heads * 2 * span * tail * 2 * HD,
             transcendentals=heads * span * tail,
@@ -195,15 +197,13 @@
     (mixed,) = call(
         merge_kernel,
         counts,
-        (w_mot, v_prior, acc, top, tot, mtop, mtot),
+        (w_mot, v_prior, acc, own_stat, mot_stat),
         [
             rows_of(heads * tail),
             whole(tail, local),
             rows_of(local),
-            rows_of(COLS),
-            rows_of(COLS),
-            rows_of(COLS),
-            rows_of(COLS),
+            rows_of(PAIR),
+            rows_of(PAIR),
         ],
         [(local, jnp.bfloat16)],
         pl.CostEstimate(

time: 134 us -> 135 us (level)
  no operation moved by 1% of the time
where the time goes in v16:
time: 135 us; the launch traced here: 134 us
  waiting for transfers between devices  51.6 us (38%)
  Pallas kernels  26 us (19%)
  starting transfers between devices  23.7 us (18%)
  blocking collectives  20.7 us (15%)
  local copies, waits for them, and re-layouts  8.03 us (6%)
  other arithmetic  3.17 us (2%)
    all_to_all x1, waiting for transfers between devices, body(): lax.all_to_all(kv_send, 'head', split_axis=0, concat_axis=0, tiled=True)  28 us
    pallas_call x3, Pallas kernels, call(): pl.pallas_call(kernel, out_shape=tuple(shapes), grid_spec=pltpu.PrefetchS...  26 us
    ppermute x1, waiting for transfers between devices, body(): lax.ppermute(v_far, 'stretch', first)  23.6 us
    all_to_all x1, blocking collectives, body(): lax.all_to_all(mixed, 'head', split_axis=0, concat_axis=1, tiled=True)  20.7 us
    ppermute x2, starting transfers between devices, from_behind(): return lax.ppermute(shard, axis, pairs)  6.37 us
    all_to_all x1, starting transfers between devices, body(): lax.all_to_all(kv_send, 'head', split_axis=0, concat_axis=0, tiled=True)  5.44 us
    all_to_all x1, starting transfers between devices, body(): lax.all_to_all(queries, 'head', split_axis=1, concat_axis=0, tiled=True)  4.4 us
    ppermute x1, starting transfers between devices, body(): lax.ppermute(v_far, 'stretch', inner)  4.29 us
  transfers between devices with their start and end apart: 7, of which 2 were waited for; matrix products, arithmetic and copies ran while one was open for 4% of the time, Pallas kernels for 14%

profile of v16, /device:TPU:16, one launch (start us, length us, event | category | flops | bytes accessed | tf_op | source)
XLA Modules:
  0.0 134.0 jit_solution(13834730590282180137)
XLA Ops:
  0.0 1.5 %copy.17 = bf16[14,8,8,640]{3,2,1,0:T(8,128)(2,1)S(1)} copy(bf16[14,8,8,640]{3,1,2,0:T(8,128)(2,1)} %bitcast.37) | data formatting | bytes 2293760
  1.8 0.2 pad_maximum_fusion
  2.0 1.7 %copy.13 = bf16[8,2,112,640]{3,2,1,0:T(8,128)(2,1)} copy(bf16[8,2,112,640]{3,0,2,1:T(8,128)(2,1)S(1)} %pad_maximum_fusion) | data formatting | bytes 4587520 | tf_op jit(solution)/shard_map/stack | solution.py:151
  3.7 5.4 %all-to-all-start.1 = ((bf16[8,2,112,640]{3,2,1,0:T(8,128)(2,1)}), bf16[8,2,112,640]{3,2,1,0:T(8,128)(2,1)S(1)}, u32[]{:S(2)}, u32[]{:S(2)}) async-start(bf16[8,2,112,640]{3,2,1,0:T(8,128)(2,1)} %copy.13), calls=%async_computation.1 | async-start | bytes 4587520 | tf_op jit(solution)/shard_map/all_to_all | solution.py:152
  9.2 1.1 copy.20
  10.3 28.0 %all-to-all-done.1 = bf16[8,2,112,640]{3,2,1,0:T(8,128)(2,1)S(1)} async-done(((bf16[8,2,112,640]{3,2,1,0:T(8,128)(2,1)}), bf16[8,2,112,640]{3,2,1,0:T(8,128)(2,1)S(1)}, u32[]{:S(2)}, u32[]{:S(2)}) %all-to-all-start.1) | async-done | bytes 2293792 | tf_op jit(solution)/shard_map/all_to_all | solution.py:152
  38.2 4.4 %all-to-all-start = ((bf16[112,8,640]{2,0,1:T(8,128)(2,1)}), bf16[112,8,640]{2,0,1:T(8,128)(2,1)}, u32[]{:S(2)}, u32[]{:S(2)}) async-start(bf16[112,8,640]{2,0,1:T(8,128)(2,1)} %bitcast.26), calls=%async_computation | async-start | bytes 2293760 | tf_op jit(solution)/shard_map/all_to_all | solution.py:169
  42.7 0.7 dynamic_slice.12
  44.0 0.2 fusion
  44.3 1.3 collective-permute-start.3
  45.6 4.5 %collective-permute-start = (bf16[512,640]{1,0:T(8,128)(2,1)S(1)}, bf16[512,640]{1,0:T(8,128)(2,1)}, u32[]{:S(2)}, u32[]{:S(2)}) collective-permute-start(bf16[512,640]{1,0:T(8,128)(2,1)S(1)} %constant_dynamic-slice_fusion.2), channel_id=1, source_target_pairs={{0,16},{16,32},{32,48},{48,64},{64,80},{80,96},{96,112},{112,128},... | collective-permute-start | bytes 1966088 | tf_op jit(solution)/shard_map/ppermute | solution.py:24
  50.1 0.7 dynamic_slice.13
  50.8 1.9 %pad_add_fusion.counts = s32[2]{0:T(128)} fusion(s32[1]{0:T(128)} %dynamic_slice.13, s32[1]{0:T(128)} %dynamic_slice.12), kind=kLoop, calls=%fused_computation.6 | loop fusion | flops 2 | bytes 16 | tf_op jit(solution)/shard_map/stack | solution.py:142
  52.7 4.3 %collective-permute-start.2 = (bf16[384,640]{1,0:T(8,128)(2,1)S(1)}, bf16[384,640]{1,0:T(8,128)(2,1)S(1)}, u32[]{:S(2)}, u32[]{:S(2)}) collective-permute-start(bf16[384,640]{1,0:T(8,128)(2,1)S(1)} %constant_dynamic-slice_fusion.1), channel_id=1, source_target_pairs={{0,16},{16,32},{32,48},{48,64},{64,80},{80,96},{96,112},{128,144},... | collective-permute-start | bytes 1474568 | tf_op jit(solution)/shard_map/ppermute | solution.py:163
  57.0 23.6 %collective-permute-done.3 = bf16[384,640]{1,0:T(8,128)(2,1)} collective-permute-done((bf16[384,640]{1,0:T(8,128)(2,1)S(1)}, bf16[384,640]{1,0:T(8,128)(2,1)}, u32[]{:S(2)}, u32[]{:S(2)}) %collective-permute-start.3) | collective-permute-done | bytes 491552 | tf_op jit(solution)/shard_map/ppermute | solution.py:164
  80.6 1.9 %collective-permute-start.4 = (bf16[384,640]{1,0:T(8,128)(2,1)}, bf16[384,640]{1,0:T(8,128)(2,1)S(1)}, u32[]{:S(2)}, u32[]{:S(2)}) collective-permute-start(bf16[384,640]{1,0:T(8,128)(2,1)} %collective-permute-done.3), channel_id=1, source_target_pairs={{0,128},{128,256},{256,384},{1,129},{129,257},{257,385},{2,130},{1... | collective-permute-start | bytes 1474568 | tf_op jit(solution)/shard_map/ppermute | solution.py:163
  82.5 0.7 constant_dynamic-slice_fusion
  83.2 1.9 %collective-permute-start.1 = (bf16[128,640]{1,0:T(8,128)(2,1)}, bf16[128,640]{1,0:T(8,128)(2,1)S(1)}, u32[]{:S(2)}, u32[]{:S(2)}) collective-permute-start(bf16[128,640]{1,0:T(8,128)(2,1)} %constant_dynamic-slice_fusion), channel_id=1, source_target_pairs={{0,16},{16,32},{32,48},{48,64},{64,80},{80,96},{96,112},{112,128},... | collective-permute-start | bytes 491528 | tf_op jit(solution)/shard_map/ppermute | solution.py:24
  85.1 11.3 %shard_map.56 = (f32[896,640]{1,0:T(8,128)}, f32[896,16]{1,0:T(8,128)}) custom-call(s32[2]{0:T(128)} %pad_add_fusion.counts, bf16[896,640]{1,0:T(8,128)(2,1)} %bitcast.1.q_ref, bf16[896,640]{1,0:T(8,128)(2,1)} %bitcast.36, bf16[896,640]{1,0:T(8,128)(2,1)} %bitcast.34), custom_call_target="tpu_custom_call" | custom-call | flops 3082813440 | bytes 5734400 | tf_op jit(solution)/shard_map/pallas_call | solution.py:110
  96.4 7.2 %shard_map.55 = (bf16[896,2560]{1,0:T(8,128)(2,1)}, f32[896,16]{1,0:T(8,128)}) custom-call(s32[2]{0:T(128)} %pad_add_fusion.counts, bf16[896,640]{1,0:T(8,128)(2,1)} %bitcast.1.q_ref, bf16[512,640]{1,0:T(8,128)(2,1)} %collective-permute-done.mk_ref), custom_call_target="tpu_custom_call" | custom-call | flops 1174405120 | bytes 6389760 | tf_op jit(solution)/shard_map/pallas_call | solution.py:110
  103.8 0.9 pad_maximum_fusion.1.mv_ref
  104.7 7.5 %shard_map.57 = bf16[896,640]{1,0:T(8,128)(2,1)} custom-call(s32[2]{0:T(128)} %pad_add_fusion.counts, bf16[896,2560]{1,0:T(8,128)(2,1)} %get-tuple-element.9.w_ref, bf16[512,640]{1,0:T(8,128)(2,1)} %pad_maximum_fusion.1.mv_ref, f32[896,640]{1,0:T(8,128)} %get-tuple-element.10.acc_ref, f32[896,16]{1,0:T(8,128)} %get-tuple-element.11.own_ref, ...), custom_call_target="tpu_custom_call" | custom-call | flops 587202560 | bytes 8683520 | tf_op jit(solution)/shard_map/pallas_call | solution.py:110
  112.2 20.7 %all_to_all.43 = bf16[8,112,640]{2,1,0:T(8,128)(2,1)S(1)} all-to-all(bf16[8,112,640]{2,1,0:T(8,128)(2,1)} %bitcast.28), channel_id=1, replica_groups=mesh['stretch'=32,'head'=8,'cfg'=2] {'head'}, dimensions={0} | all-to-all | bytes 2293760 | tf_op jit(solution)/shard_map/all_to_all | solution.py:215
  132.9 1.2 copy.16
  (21 shorter events, 0.5 us)
Async XLA Ops:
  0.0 1.6 %copy-start.2 = (bf16[112,5120]{1,0:T(8,128)(2,1)S(1)}, bf16[112,5120]{1,0:T(8,128)(2,1)}, u32[]{:S(2)}) copy-start(bf16[112,5120]{1,0:T(8,128)(2,1)} %param.7) | copy-start | bytes 3440644
  3.7 5.4 %copy-start.3 = (bf16[112,5120]{1,0:T(8,128)(2,1)S(1)}, bf16[112,5120]{1,0:T(8,128)(2,1)}, u32[]{:S(2)}) copy-start(bf16[112,5120]{1,0:T(8,128)(2,1)} %param.5) | copy-start | bytes 3440644
  3.7 34.5 %all-to-all-start.1 = ((bf16[8,2,112,640]{3,2,1,0:T(8,128)(2,1)}), bf16[8,2,112,640]{3,2,1,0:T(8,128)(2,1)S(1)}, u32[]{:S(2)}, u32[]{:S(2)}) async-start(bf16[8,2,112,640]{3,2,1,0:T(8,128)(2,1)} %copy.13), calls=%async_computation.1 | async-start | bytes 4587520 | tf_op jit(solution)/shard_map/all_to_all | solution.py:152
  38.2 4.4 %copy-start.4 = (s32[32]{0:T(128)S(1)}, s32[32]{0:T(128)}, u32[]{:S(2)}) copy-start(s32[32]{0:T(128)} %param.8) | copy-start | bytes 388
  38.2 46.9 %all-to-all-start = ((bf16[112,8,640]{2,0,1:T(8,128)(2,1)}), bf16[112,8,640]{2,0,1:T(8,128)(2,1)}, u32[]{:S(2)}, u32[]{:S(2)}) async-start(bf16[112,8,640]{2,0,1:T(8,128)(2,1)} %bitcast.26), calls=%async_computation | async-start | bytes 2293760 | tf_op jit(solution)/shard_map/all_to_all | solution.py:169
  44.2 1.5 %copy-start.1 = (bf16[1,8,112,640]{3,2,0,1:T(8,128)(2,1)}, bf16[1,8,112,640]{3,2,0,1:T(8,128)(2,1)S(1)}, u32[]{:S(2)}) copy-start(bf16[1,8,112,640]{3,2,0,1:T(8,128)(2,1)S(1)} %get-tuple-element.14) | copy-start | bytes 3440644
  44.2 38.3 %copy-start = (bf16[1,8,112,640]{3,2,0,1:T(8,128)(2,1)}, bf16[1,8,112,640]{3,2,0,1:T(8,128)(2,1)S(1)}, u32[]{:S(2)}) copy-start(bf16[1,8,112,640]{3,2,0,1:T(8,128)(2,1)S(1)} %get-tuple-element.13) | copy-start | bytes 3440644
  44.2 5.9 %copy-start.5 = (s32[32]{0:T(128)S(1)}, s32[32]{0:T(128)}, u32[]{:S(2)}) copy-start(s32[32]{0:T(128)} %param.9) | copy-start | bytes 388
  44.3 36.3 %collective-permute-start.3 = (bf16[384,640]{1,0:T(8,128)(2,1)S(1)}, bf16[384,640]{1,0:T(8,128)(2,1)}, u32[]{:S(2)}, u32[]{:S(2)}) collective-permute-start(bf16[384,640]{1,0:T(8,128)(2,1)S(1)} %constant_dynamic-slice_fusion.1), channel_id=1, source_target_pairs={{112,0},{240,128},{368,256},{113,1},{241,129},{369,257},{114,2},{2... | collective-permute-start | bytes 1474568 | tf_op jit(solution)/shard_map/ppermute | solution.py:164
  45.6 50.8 %collective-permute-start = (bf16[512,640]{1,0:T(8,128)(2,1)S(1)}, bf16[512,640]{1,0:T(8,128)(2,1)}, u32[]{:S(2)}, u32[]{:S(2)}) collective-permute-start(bf16[512,640]{1,0:T(8,128)(2,1)S(1)} %constant_dynamic-slice_fusion.2), channel_id=1, source_target_pairs={{0,16},{16,32},{32,48},{48,64},{64,80},{80,96},{96,112},{112,128},... | collective-permute-start | bytes 1966088 | tf_op jit(solution)/shard_map/ppermute | solution.py:24
  52.7 50.9 %collective-permute-start.2 = (bf16[384,640]{1,0:T(8,128)(2,1)S(1)}, bf16[384,640]{1,0:T(8,128)(2,1)S(1)}, u32[]{:S(2)}, u32[]{:S(2)}) collective-permute-start(bf16[384,640]{1,0:T(8,128)(2,1)S(1)} %constant_dynamic-slice_fusion.1), channel_id=1, source_target_pairs={{0,16},{16,32},{32,48},{48,64},{64,80},{80,96},{96,112},{128,144},... | collective-permute-start | bytes 1474568 | tf_op jit(solution)/shard_map/ppermute | solution.py:163
  80.6 23.1 %collective-permute-start.4 = (bf16[384,640]{1,0:T(8,128)(2,1)}, bf16[384,640]{1,0:T(8,128)(2,1)S(1)}, u32[]{:S(2)}, u32[]{:S(2)}) collective-permute-start(bf16[384,640]{1,0:T(8,128)(2,1)} %collective-permute-done.3), channel_id=1, source_target_pairs={{0,128},{128,256},{256,384},{1,129},{129,257},{257,385},{2,130},{1... | collective-permute-start | bytes 1474568 | tf_op jit(solution)/shard_map/ppermute | solution.py:163
  83.2 20.6 %collective-permute-start.1 = (bf16[128,640]{1,0:T(8,128)(2,1)}, bf16[128,640]{1,0:T(8,128)(2,1)S(1)}, u32[]{:S(2)}, u32[]{:S(2)}) collective-permute-start(bf16[128,640]{1,0:T(8,128)(2,1)} %constant_dynamic-slice_fusion), channel_id=1, source_target_pairs={{0,16},{16,32},{32,48},{48,64},{64,80},{80,96},{96,112},{112,128},... | collective-permute-start | bytes 491528 | tf_op jit(solution)/shard_map/ppermute | solution.py:24

commit v17 on v13

--- a/solution.py
+++ b/solution.py
@@ -47,7 +47,7 @@
         v = v_ref[:, c]
         v_ext = jnp.concatenate([v, jnp.ones_like(v)], axis=1)
         both = jnp.dot(weights, v_ext, preferred_element_type=jnp.float32)
-        acc_ref[:, c] = both[:, :HD]
+        acc_ref[:, c] = both[:, :HD].astype(acc_ref.dtype)
         top_ref[:, h : h + 1] = top
         tot_ref[:, h : h + 1] = both[:, HD : HD + 1]
 
@@ -90,7 +90,7 @@
         scale = 1.0 / (
             tot_ref[:, h : h + 1] * factor_own + mtot_ref[:, h : h + 1] * factor_mot
         )
-        mixed = (acc_ref[:, c] * factor_own + acc_mot * factor_mot) * scale
+        mixed = (acc_ref[:, c].astype(jnp.float32) * factor_own + acc_mot * factor_mot) * scale
         o_ref[:, c] = jnp.where(row_live, mixed, 0.0).astype(o_ref.dtype)
 
 
@@ -173,7 +173,7 @@
         counts,
         (q_heads, k_heads, v_heads),
         [rows_of(local), whole(span, local), whole(span, local)],
-        [(local, f32), (COLS, f32), (COLS, f32)],
+        [(local, jnp.bfloat16), (COLS, f32), (COLS, f32)],
         pl.CostEstimate(
             flops=heads * 2 * span * span * 3 * HD,
             transcendentals=heads * span * span,

time: 134 us -> 133 us (level)
  no operation moved by 1% of the time
where the time goes in v17:
time: 133 us
  waiting for transfers between devices  51.6 us (39%)
  Pallas kernels  24.6 us (18%)
  starting transfers between devices  23.6 us (18%)
  blocking collectives  20.9 us (16%)
  local copies, waits for them, and re-layouts  8 us (6%)
  other arithmetic  3.15 us (2%)
    all_to_all x1, waiting for transfers between devices, body(): lax.all_to_all(kv_send, 'head', split_axis=0, concat_axis=0, tiled=True)  28 us
    pallas_call x3, Pallas kernels, call(): pl.pallas_call(kernel, out_shape=tuple(shapes), grid_spec=pltpu.PrefetchS...  24.6 us
    ppermute x1, waiting for transfers between devices, body(): lax.ppermute(v_far, 'stretch', first)  23.7 us
    all_to_all x1, blocking collectives, body(): lax.all_to_all(mixed, 'head', split_axis=0, concat_axis=1, tiled=True)  20.9 us
    ppermute x2, starting transfers between devices, from_behind(): return lax.ppermute(shard, axis, pairs)  6.32 us
    all_to_all x1, starting transfers between devices, body(): lax.all_to_all(kv_send, 'head', split_axis=0, concat_axis=0, tiled=True)  5.44 us
    all_to_all x1, starting transfers between devices, body(): lax.all_to_all(queries, 'head', split_axis=1, concat_axis=0, tiled=True)  4.38 us
    ppermute x1, starting transfers between devices, body(): lax.ppermute(v_far, 'stretch', inner)  4.29 us
  transfers between devices with their start and end apart: 7, of which 2 were waited for; matrix products, arithmetic and copies ran while one was open for 4% of the time, Pallas kernels for 14%

profile of v17, /device:TPU:16, one launch (start us, length us, event | category | flops | bytes accessed | tf_op | source)
XLA Modules:
  0.0 132.7 jit_solution(6565097931964410690)
XLA Ops:
  0.0 1.5 %copy.17 = bf16[14,8,8,640]{3,2,1,0:T(8,128)(2,1)S(1)} copy(bf16[14,8,8,640]{3,1,2,0:T(8,128)(2,1)} %bitcast.37) | data formatting | bytes 2293760
  1.8 0.2 pad_maximum_fusion
  2.0 1.7 %copy.13 = bf16[8,2,112,640]{3,2,1,0:T(8,128)(2,1)} copy(bf16[8,2,112,640]{3,0,2,1:T(8,128)(2,1)S(1)} %pad_maximum_fusion) | data formatting | bytes 4587520 | tf_op jit(solution)/shard_map/stack | solution.py:149
  3.7 5.4 %all-to-all-start.1 = ((bf16[8,2,112,640]{3,2,1,0:T(8,128)(2,1)}), bf16[8,2,112,640]{3,2,1,0:T(8,128)(2,1)S(1)}, u32[]{:S(2)}, u32[]{:S(2)}) async-start(bf16[8,2,112,640]{3,2,1,0:T(8,128)(2,1)} %copy.13), calls=%async_computation.1 | async-start | bytes 4587520 | tf_op jit(solution)/shard_map/all_to_all | solution.py:150
  9.2 1.1 copy.20
  10.3 28.0 %all-to-all-done.1 = bf16[8,2,112,640]{3,2,1,0:T(8,128)(2,1)S(1)} async-done(((bf16[8,2,112,640]{3,2,1,0:T(8,128)(2,1)}), bf16[8,2,112,640]{3,2,1,0:T(8,128)(2,1)S(1)}, u32[]{:S(2)}, u32[]{:S(2)}) %all-to-all-start.1) | async-done | bytes 2293792 | tf_op jit(solution)/shard_map/all_to_all | solution.py:150
  38.2 4.4 %all-to-all-start = ((bf16[112,8,640]{2,0,1:T(8,128)(2,1)}), bf16[112,8,640]{2,0,1:T(8,128)(2,1)}, u32[]{:S(2)}, u32[]{:S(2)}) async-start(bf16[112,8,640]{2,0,1:T(8,128)(2,1)} %bitcast.26), calls=%async_computation | async-start | bytes 2293760 | tf_op jit(solution)/shard_map/all_to_all | solution.py:167
  42.6 0.6 dynamic_slice.12
  43.9 0.2 fusion
  44.2 1.3 collective-permute-start.3
  45.6 4.4 %collective-permute-start = (bf16[512,640]{1,0:T(8,128)(2,1)S(1)}, bf16[512,640]{1,0:T(8,128)(2,1)}, u32[]{:S(2)}, u32[]{:S(2)}) collective-permute-start(bf16[512,640]{1,0:T(8,128)(2,1)S(1)} %constant_dynamic-slice_fusion.2), channel_id=1, source_target_pairs={{0,16},{16,32},{32,48},{48,64},{64,80},{80,96},{96,112},{112,128},... | collective-permute-start | bytes 1966088 | tf_op jit(solution)/shard_map/ppermute | solution.py:23
  50.0 0.7 dynamic_slice.13
  50.7 1.9 %pad_add_fusion.counts = s32[2]{0:T(128)} fusion(s32[1]{0:T(128)} %dynamic_slice.13, s32[1]{0:T(128)} %dynamic_slice.12), kind=kLoop, calls=%fused_computation.6 | loop fusion | flops 2 | bytes 16 | tf_op jit(solution)/shard_map/stack | solution.py:140
  52.5 4.3 %collective-permute-start.2 = (bf16[384,640]{1,0:T(8,128)(2,1)S(1)}, bf16[384,640]{1,0:T(8,128)(2,1)S(1)}, u32[]{:S(2)}, u32[]{:S(2)}) collective-permute-start(bf16[384,640]{1,0:T(8,128)(2,1)S(1)} %constant_dynamic-slice_fusion.1), channel_id=1, source_target_pairs={{0,16},{16,32},{32,48},{48,64},{64,80},{80,96},{96,112},{128,144},... | collective-permute-start | bytes 1474568 | tf_op jit(solution)/shard_map/ppermute | solution.py:161
  56.8 23.7 %collective-permute-done.3 = bf16[384,640]{1,0:T(8,128)(2,1)} collective-permute-done((bf16[384,640]{1,0:T(8,128)(2,1)S(1)}, bf16[384,640]{1,0:T(8,128)(2,1)}, u32[]{:S(2)}, u32[]{:S(2)}) %collective-permute-start.3) | collective-permute-done | bytes 491552 | tf_op jit(solution)/shard_map/ppermute | solution.py:162
  80.5 1.9 %collective-permute-start.4 = (bf16[384,640]{1,0:T(8,128)(2,1)}, bf16[384,640]{1,0:T(8,128)(2,1)S(1)}, u32[]{:S(2)}, u32[]{:S(2)}) collective-permute-start(bf16[384,640]{1,0:T(8,128)(2,1)} %collective-permute-done.3), channel_id=1, source_target_pairs={{0,128},{128,256},{256,384},{1,129},{129,257},{257,385},{2,130},{1... | collective-permute-start | bytes 1474568 | tf_op jit(solution)/shard_map/ppermute | solution.py:161
  82.4 0.7 constant_dynamic-slice_fusion
  83.1 1.9 %collective-permute-start.1 = (bf16[128,640]{1,0:T(8,128)(2,1)}, bf16[128,640]{1,0:T(8,128)(2,1)S(1)}, u32[]{:S(2)}, u32[]{:S(2)}) collective-permute-start(bf16[128,640]{1,0:T(8,128)(2,1)} %constant_dynamic-slice_fusion), channel_id=1, source_target_pairs={{0,16},{16,32},{32,48},{48,64},{64,80},{80,96},{96,112},{112,128},... | collective-permute-start | bytes 491528 | tf_op jit(solution)/shard_map/ppermute | solution.py:23
  85.0 11.1 %shard_map.56 = (bf16[896,640]{1,0:T(8,128)(2,1)}, f32[896,8]{1,0:T(8,128)}, f32[896,8]{1,0:T(8,128)}) custom-call(s32[2]{0:T(128)} %pad_add_fusion.counts, bf16[896,640]{1,0:T(8,128)(2,1)} %bitcast.1.q_ref, bf16[896,640]{1,0:T(8,128)(2,1)} %bitcast.36, bf16[896,640]{1,0:T(8,128)(2,1)} %bitcast.34), custom_call_target="tpu_custom_call" | custom-call | flops 3082813440 | bytes 5734400 | tf_op jit(solution)/shard_map/pallas_call | solution.py:108
  96.1 7.2 %shard_map.55 = (bf16[896,2560]{1,0:T(8,128)(2,1)}, f32[896,8]{1,0:T(8,128)}, f32[896,8]{1,0:T(8,128)}) custom-call(s32[2]{0:T(128)} %pad_add_fusion.counts, bf16[896,640]{1,0:T(8,128)(2,1)} %bitcast.1.q_ref, bf16[512,640]{1,0:T(8,128)(2,1)} %collective-permute-done.mk_ref), custom_call_target="tpu_custom_call" | custom-call | flops 1174405120 | bytes 6389760 | tf_op jit(solution)/shard_map/pallas_call | solution.py:108
  103.5 0.9 pad_maximum_fusion.1.mv_ref
  104.4 6.3 %shard_map.57 = bf16[896,640]{1,0:T(8,128)(2,1)} custom-call(s32[2]{0:T(128)} %pad_add_fusion.counts, bf16[896,2560]{1,0:T(8,128)(2,1)} %get-tuple-element.11.w_ref, bf16[512,640]{1,0:T(8,128)(2,1)} %pad_maximum_fusion.1.mv_ref, bf16[896,640]{1,0:T(8,128)(2,1)} %get-tuple-element.12.acc_ref, f32[896,8]{1,0:T(8,128)} %get-tuple-element.13.top_ref, ...), custom_call_target="tpu_custom_call" | custom-call | flops 587202560 | bytes 8683520 | tf_op jit(solution)/shard_map/pallas_call | solution.py:108
  110.7 20.9 %all_to_all.43 = bf16[8,112,640]{2,1,0:T(8,128)(2,1)S(1)} all-to-all(bf16[8,112,640]{2,1,0:T(8,128)(2,1)} %bitcast.28), channel_id=1, replica_groups=mesh['stretch'=32,'head'=8,'cfg'=2] {'head'}, dimensions={0} | all-to-all | bytes 2293760 | tf_op jit(solution)/shard_map/all_to_all | solution.py:215
  131.6 1.2 copy.16
  (21 shorter events, 0.5 us)
Async XLA Ops:
  0.0 1.6 %copy-start.2 = (bf16[112,5120]{1,0:T(8,128)(2,1)S(1)}, bf16[112,5120]{1,0:T(8,128)(2,1)}, u32[]{:S(2)}) copy-start(bf16[112,5120]{1,0:T(8,128)(2,1)} %param.7) | copy-start | bytes 3440644
  3.7 5.4 %copy-start.3 = (bf16[112,5120]{1,0:T(8,128)(2,1)S(1)}, bf16[112,5120]{1,0:T(8,128)(2,1)}, u32[]{:S(2)}) copy-start(bf16[112,5120]{1,0:T(8,128)(2,1)} %param.5) | copy-start | bytes 3440644
  3.7 34.5 %all-to-all-start.1 = ((bf16[8,2,112,640]{3,2,1,0:T(8,128)(2,1)}), bf16[8,2,112,640]{3,2,1,0:T(8,128)(2,1)S(1)}, u32[]{:S(2)}, u32[]{:S(2)}) async-start(bf16[8,2,112,640]{3,2,1,0:T(8,128)(2,1)} %copy.13), calls=%async_computation.1 | async-start | bytes 4587520 | tf_op jit(solution)/shard_map/all_to_all | solution.py:150
  38.2 4.4 %copy-start.4 = (s32[32]{0:T(128)S(1)}, s32[32]{0:T(128)}, u32[]{:S(2)}) copy-start(s32[32]{0:T(128)} %param.8) | copy-start | bytes 388
  38.2 46.8 %all-to-all-start = ((bf16[112,8,640]{2,0,1:T(8,128)(2,1)}), bf16[112,8,640]{2,0,1:T(8,128)(2,1)}, u32[]{:S(2)}, u32[]{:S(2)}) async-start(bf16[112,8,640]{2,0,1:T(8,128)(2,1)} %bitcast.26), calls=%async_computation | async-start | bytes 2293760 | tf_op jit(solution)/shard_map/all_to_all | solution.py:167
  44.1 1.5 %copy-start.1 = (bf16[1,8,112,640]{3,2,0,1:T(8,128)(2,1)}, bf16[1,8,112,640]{3,2,0,1:T(8,128)(2,1)S(1)}, u32[]{:S(2)}) copy-start(bf16[1,8,112,640]{3,2,0,1:T(8,128)(2,1)S(1)} %get-tuple-element.18) | copy-start | bytes 3440644
  44.1 38.3 %copy-start = (bf16[1,8,112,640]{3,2,0,1:T(8,128)(2,1)}, bf16[1,8,112,640]{3,2,0,1:T(8,128)(2,1)S(1)}, u32[]{:S(2)}) copy-start(bf16[1,8,112,640]{3,2,0,1:T(8,128)(2,1)S(1)} %get-tuple-element.17) | copy-start | bytes 3440644
  44.1 5.9 %copy-start.5 = (s32[32]{0:T(128)S(1)}, s32[32]{0:T(128)}, u32[]{:S(2)}) copy-start(s32[32]{0:T(128)} %param.9) | copy-start | bytes 388
  44.2 36.3 %collective-permute-start.3 = (bf16[384,640]{1,0:T(8,128)(2,1)S(1)}, bf16[384,640]{1,0:T(8,128)(2,1)}, u32[]{:S(2)}, u32[]{:S(2)}) collective-permute-start(bf16[384,640]{1,0:T(8,128)(2,1)S(1)} %constant_dynamic-slice_fusion.1), channel_id=1, source_target_pairs={{112,0},{240,128},{368,256},{113,1},{241,129},{369,257},{114,2},{2... | collective-permute-start | bytes 1474568 | tf_op jit(solution)/shard_map/ppermute | solution.py:162
  45.6 50.6 %collective-permute-start = (bf16[512,640]{1,0:T(8,128)(2,1)S(1)}, bf16[512,640]{1,0:T(8,128)(2,1)}, u32[]{:S(2)}, u32[]{:S(2)}) collective-permute-start(bf16[512,640]{1,0:T(8,128)(2,1)S(1)} %constant_dynamic-slice_fusion.2), channel_id=1, source_target_pairs={{0,16},{16,32},{32,48},{48,64},{64,80},{80,96},{96,112},{112,128},... | collective-permute-start | bytes 1966088 | tf_op jit(solution)/shard_map/ppermute | solution.py:23
  52.5 50.8 %collective-permute-start.2 = (bf16[384,640]{1,0:T(8,128)(2,1)S(1)}, bf16[384,640]{1,0:T(8,128)(2,1)S(1)}, u32[]{:S(2)}, u32[]{:S(2)}) collective-permute-start(bf16[384,640]{1,0:T(8,128)(2,1)S(1)} %constant_dynamic-slice_fusion.1), channel_id=1, source_target_pairs={{0,16},{16,32},{32,48},{48,64},{64,80},{80,96},{96,112},{128,144},... | collective-permute-start | bytes 1474568 | tf_op jit(solution)/shard_map/ppermute | solution.py:161
  80.5 22.9 %collective-permute-start.4 = (bf16[384,640]{1,0:T(8,128)(2,1)}, bf16[384,640]{1,0:T(8,128)(2,1)S(1)}, u32[]{:S(2)}, u32[]{:S(2)}) collective-permute-start(bf16[384,640]{1,0:T(8,128)(2,1)} %collective-permute-done.3), channel_id=1, source_target_pairs={{0,128},{128,256},{256,384},{1,129},{129,257},{257,385},{2,130},{1... | collective-permute-start | bytes 1474568 | tf_op jit(solution)/shard_map/ppermute | solution.py:161
  83.1 20.4 %collective-permute-start.1 = (bf16[128,640]{1,0:T(8,128)(2,1)}, bf16[128,640]{1,0:T(8,128)(2,1)S(1)}, u32[]{:S(2)}, u32[]{:S(2)}) collective-permute-start(bf16[128,640]{1,0:T(8,128)(2,1)} %constant_dynamic-slice_fusion), channel_id=1, source_target_pairs={{0,16},{16,32},{32,48},{48,64},{64,80},{80,96},{96,112},{112,128},... | collective-permute-start | bytes 491528 | tf_op jit(solution)/shard_map/ppermute | solution.py:23

commit v18 on v15

--- a/solution.py
+++ b/solution.py
@@ -154,7 +154,7 @@
     v_tail = lax.dynamic_slice_in_dim(v_heads, tail_begin, tail, 0)
     k_prior = from_behind(k_tail, "stretch", 1)
     inner, first, second = plan
-    half = 3 * tail // 8
+    half = 5 * tail // 16
     v_near = from_behind(v_tail[:half], "stretch", 1)
     v_far = v_tail[half:]
     if first:

time: 134 us -> 134 us (level); the launches traced: 134 us -> 133 us
  blocking collectives: 32.4 us -> 27.1 us
  waiting for transfers between devices: 37.6 us -> 41.4 us
    all_to_all x1, blocking collectives: 32.4 us -> 27.1 us  [body(): lax.all_to_all(mixed, 'head', split_axis=0, concat_axis=1, tiled=True)]
    ppermute x2, waiting for transfers between devices: 3.88 us -> 6.09 us  [from_behind(): return lax.ppermute(shard, axis, pairs)]
    ppermute x1, waiting for transfers between devices: 6.92 us -> 8.54 us  [body(): lax.ppermute(lax.ppermute(v_far, 'stretch', first), 'stretch', second)]
where the time goes in v18:
time: 134 us; the launch traced here: 133 us
  waiting for transfers between devices  41.4 us (31%)
  blocking collectives  27.1 us (20%)
  starting transfers between devices  26.3 us (20%)
  Pallas kernels  25.8 us (19%)
  local copies, waits for them, and re-layouts  7.99 us (6%)
  other arithmetic  3.2 us (2%)
    all_to_all x1, blocking collectives, body(): lax.all_to_all(mixed, 'head', split_axis=0, concat_axis=1, tiled=True)  27.1 us
    all_to_all x1, waiting for transfers between devices, body(): lax.all_to_all(kv_send, 'head', split_axis=0, concat_axis=0, tiled=True)  26.8 us
    pallas_call x3, Pallas kernels, call(): pl.pallas_call(kernel, out_shape=tuple(shapes), grid_spec=pltpu.PrefetchS...  25.8 us
    ppermute x1, waiting for transfers between devices, body(): lax.ppermute(lax.ppermute(v_far, 'stretch', first), 'stretch', second)  8.54 us
    ppermute x2, starting transfers between devices, from_behind(): return lax.ppermute(shard, axis, pairs)  7.92 us
    ppermute x2, waiting for transfers between devices, from_behind(): return lax.ppermute(shard, axis, pairs)  6.09 us
    all_to_all x1, starting transfers between devices, body(): lax.all_to_all(kv_send, 'head', split_axis=0, concat_axis=0, tiled=True)  5.89 us
    all_to_all x1, starting transfers between devices, body(): lax.all_to_all(queries, 'head', split_axis=1, concat_axis=0, tiled=True)  5.49 us
  transfers between devices with their start and end apart: 7, of which 3 were waited for; matrix products, arithmetic and copies ran while one was open for 4% of the time, Pallas kernels for 14%

profile of v18, /device:TPU:56, one launch (start us, length us, event | category | flops | bytes accessed | tf_op | source)
XLA Modules:
  0.0 132.5 jit_solution(1832166463802127421)
XLA Ops:
  0.0 1.5 %copy.17 = bf16[14,8,8,640]{3,2,1,0:T(8,128)(2,1)S(1)} copy(bf16[14,8,8,640]{3,1,2,0:T(8,128)(2,1)} %bitcast.37) | data formatting | bytes 2293760
  1.8 0.2 pad_maximum_fusion
  2.0 1.7 %copy.13 = bf16[8,2,112,640]{3,2,1,0:T(8,128)(2,1)} copy(bf16[8,2,112,640]{3,0,2,1:T(8,128)(2,1)S(1)} %pad_maximum_fusion) | data formatting | bytes 4587520 | tf_op jit(solution)/shard_map/stack | solution.py:149
  3.7 5.9 %all-to-all-start.1 = ((bf16[8,2,112,640]{3,2,1,0:T(8,128)(2,1)}), bf16[8,2,112,640]{3,2,1,0:T(8,128)(2,1)S(1)}, u32[]{:S(2)}, u32[]{:S(2)}) async-start(bf16[8,2,112,640]{3,2,1,0:T(8,128)(2,1)} %copy.13), calls=%async_computation.1 | async-start | bytes 4587520 | tf_op jit(solution)/shard_map/all_to_all | solution.py:150
  9.6 1.1 copy.20
  10.7 26.8 %all-to-all-done.1 = bf16[8,2,112,640]{3,2,1,0:T(8,128)(2,1)S(1)} async-done(((bf16[8,2,112,640]{3,2,1,0:T(8,128)(2,1)}), bf16[8,2,112,640]{3,2,1,0:T(8,128)(2,1)S(1)}, u32[]{:S(2)}, u32[]{:S(2)}) %all-to-all-start.1) | async-done | bytes 2293792 | tf_op jit(solution)/shard_map/all_to_all | solution.py:150
  37.5 5.5 %all-to-all-start = ((bf16[112,8,640]{2,0,1:T(8,128)(2,1)}), bf16[112,8,640]{2,0,1:T(8,128)(2,1)}, u32[]{:S(2)}, u32[]{:S(2)}) async-start(bf16[112,8,640]{2,0,1:T(8,128)(2,1)} %bitcast.26), calls=%async_computation | async-start | bytes 2293760 | tf_op jit(solution)/shard_map/all_to_all | solution.py:167
  43.0 0.6 dynamic_slice.12
  44.5 1.4 %collective-permute-start.3 = (bf16[352,640]{1,0:T(8,128)(2,1)S(1)}, bf16[352,640]{1,0:T(8,128)(2,1)}, u32[]{:S(2)}, u32[]{:S(2)}) collective-permute-start(bf16[352,640]{1,0:T(8,128)(2,1)S(1)} %constant_dynamic-slice_fusion.1), channel_id=1, source_target_pairs={{112,0},{240,128},{368,256},{113,1},{241,129},{369,257},{114,2},{2... | collective-permute-start | bytes 1351688 | tf_op jit(solution)/shard_map/ppermute | solution.py:162
  46.0 4.3 %collective-permute-start = (bf16[512,640]{1,0:T(8,128)(2,1)S(1)}, bf16[512,640]{1,0:T(8,128)(2,1)}, u32[]{:S(2)}, u32[]{:S(2)}) collective-permute-start(bf16[512,640]{1,0:T(8,128)(2,1)S(1)} %constant_dynamic-slice_fusion.2), channel_id=1, source_target_pairs={{0,16},{16,32},{32,48},{48,64},{64,80},{80,96},{96,112},{112,128},... | collective-permute-start | bytes 1966088 | tf_op jit(solution)/shard_map/ppermute | solution.py:23
  50.3 0.7 dynamic_slice.13
  51.0 1.9 %pad_add_fusion.counts = s32[2]{0:T(128)} fusion(s32[1]{0:T(128)} %dynamic_slice.13, s32[1]{0:T(128)} %dynamic_slice.12), kind=kLoop, calls=%fused_computation.6 | loop fusion | flops 2 | bytes 16 | tf_op jit(solution)/shard_map/stack | solution.py:140
  52.9 4.3 %collective-permute-start.2 = (bf16[352,640]{1,0:T(8,128)(2,1)S(1)}, bf16[352,640]{1,0:T(8,128)(2,1)S(1)}, u32[]{:S(2)}, u32[]{:S(2)}) collective-permute-start(bf16[352,640]{1,0:T(8,128)(2,1)S(1)} %constant_dynamic-slice_fusion.1), channel_id=1, source_target_pairs={{0,16},{16,32},{32,48},{48,64},{64,80},{80,96},{96,112},{128,144},... | collective-permute-start | bytes 1351688 | tf_op jit(solution)/shard_map/ppermute | solution.py:161
  57.2 1.3 collective-permute-start.4
  58.5 0.7 constant_dynamic-slice_fusion
  59.2 3.6 %collective-permute-start.1 = (bf16[160,640]{1,0:T(8,128)(2,1)}, bf16[160,640]{1,0:T(8,128)(2,1)S(1)}, u32[]{:S(2)}, u32[]{:S(2)}) collective-permute-start(bf16[160,640]{1,0:T(8,128)(2,1)} %constant_dynamic-slice_fusion), channel_id=1, source_target_pairs={{0,16},{16,32},{32,48},{48,64},{64,80},{80,96},{96,112},{112,128},... | collective-permute-start | bytes 614408 | tf_op jit(solution)/shard_map/ppermute | solution.py:23
  62.9 11.3 %shard_map.56 = (f32[896,640]{1,0:T(8,128)}, f32[896,8]{1,0:T(8,128)}, f32[896,8]{1,0:T(8,128)}) custom-call(s32[2]{0:T(128)} %pad_add_fusion.counts, bf16[896,640]{1,0:T(8,128)(2,1)} %bitcast.1.q_ref, bf16[896,640]{1,0:T(8,128)(2,1)} %bitcast.36, bf16[896,640]{1,0:T(8,128)(2,1)} %bitcast.34), custom_call_target="tpu_custom_call" | custom-call | flops 3082813440 | bytes 5734400 | tf_op jit(solution)/shard_map/pallas_call | solution.py:108
  74.2 7.2 %shard_map.55 = (bf16[896,2560]{1,0:T(8,128)(2,1)}, f32[896,8]{1,0:T(8,128)}, f32[896,8]{1,0:T(8,128)}) custom-call(s32[2]{0:T(128)} %pad_add_fusion.counts, bf16[896,640]{1,0:T(8,128)(2,1)} %bitcast.1.q_ref, bf16[512,640]{1,0:T(8,128)(2,1)} %collective-permute-done.mk_ref), custom_call_target="tpu_custom_call" | custom-call | flops 1174405120 | bytes 6389760 | tf_op jit(solution)/shard_map/pallas_call | solution.py:108
  81.4 8.5 %collective-permute-done.4 = bf16[352,640]{1,0:T(8,128)(2,1)S(1)} collective-permute-done((bf16[352,640]{1,0:T(8,128)(2,1)}, bf16[352,640]{1,0:T(8,128)(2,1)S(1)}, u32[]{:S(2)}, u32[]{:S(2)}) %collective-permute-start.4) | collective-permute-done | bytes 450592 | tf_op jit(solution)/shard_map/ppermute | solution.py:161
  90.1 6.1 %collective-permute-done.1 = bf16[160,640]{1,0:T(8,128)(2,1)S(1)} collective-permute-done((bf16[160,640]{1,0:T(8,128)(2,1)}, bf16[160,640]{1,0:T(8,128)(2,1)S(1)}, u32[]{:S(2)}, u32[]{:S(2)}) %collective-permute-start.1) | collective-permute-done | bytes 204832 | tf_op jit(solution)/shard_map/ppermute | solution.py:23
  96.2 0.9 pad_maximum_fusion.1.mv_ref
  97.1 7.2 %shard_map.57 = bf16[896,640]{1,0:T(8,128)(2,1)} custom-call(s32[2]{0:T(128)} %pad_add_fusion.counts, bf16[896,2560]{1,0:T(8,128)(2,1)} %get-tuple-element.11.w_ref, bf16[512,640]{1,0:T(8,128)(2,1)} %pad_maximum_fusion.1.mv_ref, f32[896,640]{1,0:T(8,128)} %get-tuple-element.12.acc_ref, f32[896,8]{1,0:T(8,128)} %get-tuple-element.13.top_ref, ...), custom_call_target="tpu_custom_call" | custom-call | flops 587202560 | bytes 8683520 | tf_op jit(solution)/shard_map/pallas_call | solution.py:108
  104.3 27.1 %all_to_all.43 = bf16[8,112,640]{2,1,0:T(8,128)(2,1)S(1)} all-to-all(bf16[8,112,640]{2,1,0:T(8,128)(2,1)} %bitcast.31), channel_id=1, replica_groups=mesh['stretch'=32,'head'=8,'cfg'=2] {'head'}, dimensions={0} | all-to-all | bytes 2293760 | tf_op jit(solution)/shard_map/all_to_all | solution.py:215
  131.4 1.2 copy.16
  (21 shorter events, 0.7 us)
Async XLA Ops:
  0.0 1.6 %copy-start.2 = (bf16[112,5120]{1,0:T(8,128)(2,1)S(1)}, bf16[112,5120]{1,0:T(8,128)(2,1)}, u32[]{:S(2)}) copy-start(bf16[112,5120]{1,0:T(8,128)(2,1)} %param.7) | copy-start | bytes 3440644
  3.7 5.9 %copy-start.3 = (bf16[112,5120]{1,0:T(8,128)(2,1)S(1)}, bf16[112,5120]{1,0:T(8,128)(2,1)}, u32[]{:S(2)}) copy-start(bf16[112,5120]{1,0:T(8,128)(2,1)} %param.5) | copy-start | bytes 3440644
  3.7 33.8 %all-to-all-start.1 = ((bf16[8,2,112,640]{3,2,1,0:T(8,128)(2,1)}), bf16[8,2,112,640]{3,2,1,0:T(8,128)(2,1)S(1)}, u32[]{:S(2)}, u32[]{:S(2)}) async-start(bf16[8,2,112,640]{3,2,1,0:T(8,128)(2,1)} %copy.13), calls=%async_computation.1 | async-start | bytes 4587520 | tf_op jit(solution)/shard_map/all_to_all | solution.py:150
  37.5 5.5 %copy-start.4 = (s32[32]{0:T(128)S(1)}, s32[32]{0:T(128)}, u32[]{:S(2)}) copy-start(s32[32]{0:T(128)} %param.8) | copy-start | bytes 388
  37.5 25.4 %all-to-all-start = ((bf16[112,8,640]{2,0,1:T(8,128)(2,1)}), bf16[112,8,640]{2,0,1:T(8,128)(2,1)}, u32[]{:S(2)}, u32[]{:S(2)}) async-start(bf16[112,8,640]{2,0,1:T(8,128)(2,1)} %bitcast.26), calls=%async_computation | async-start | bytes 2293760 | tf_op jit(solution)/shard_map/all_to_all | solution.py:167
  44.4 14.8 %copy-start = (bf16[1,8,112,640]{3,2,0,1:T(8,128)(2,1)}, bf16[1,8,112,640]{3,2,0,1:T(8,128)(2,1)S(1)}, u32[]{:S(2)}) copy-start(bf16[1,8,112,640]{3,2,0,1:T(8,128)(2,1)S(1)} %get-tuple-element.17) | copy-start | bytes 3440644
  44.4 14.8 %copy-start.1 = (bf16[1,8,112,640]{3,2,0,1:T(8,128)(2,1)}, bf16[1,8,112,640]{3,2,0,1:T(8,128)(2,1)S(1)}, u32[]{:S(2)}) copy-start(bf16[1,8,112,640]{3,2,0,1:T(8,128)(2,1)S(1)} %get-tuple-element.18) | copy-start | bytes 3440644
  44.4 5.9 %copy-start.5 = (s32[32]{0:T(128)S(1)}, s32[32]{0:T(128)}, u32[]{:S(2)}) copy-start(s32[32]{0:T(128)} %param.9) | copy-start | bytes 388
  44.5 12.7 %collective-permute-start.3 = (bf16[352,640]{1,0:T(8,128)(2,1)S(1)}, bf16[352,640]{1,0:T(8,128)(2,1)}, u32[]{:S(2)}, u32[]{:S(2)}) collective-permute-start(bf16[352,640]{1,0:T(8,128)(2,1)S(1)} %constant_dynamic-slice_fusion.1), channel_id=1, source_target_pairs={{112,0},{240,128},{368,256},{113,1},{241,129},{369,257},{114,2},{2... | collective-permute-start | bytes 1351688 | tf_op jit(solution)/shard_map/ppermute | solution.py:162
  46.0 28.2 %collective-permute-start = (bf16[512,640]{1,0:T(8,128)(2,1)S(1)}, bf16[512,640]{1,0:T(8,128)(2,1)}, u32[]{:S(2)}, u32[]{:S(2)}) collective-permute-start(bf16[512,640]{1,0:T(8,128)(2,1)S(1)} %constant_dynamic-slice_fusion.2), channel_id=1, source_target_pairs={{0,16},{16,32},{32,48},{48,64},{64,80},{80,96},{96,112},{112,128},... | collective-permute-start | bytes 1966088 | tf_op jit(solution)/shard_map/ppermute | solution.py:23
  52.9 28.5 %collective-permute-start.2 = (bf16[352,640]{1,0:T(8,128)(2,1)S(1)}, bf16[352,640]{1,0:T(8,128)(2,1)S(1)}, u32[]{:S(2)}, u32[]{:S(2)}) collective-permute-start(bf16[352,640]{1,0:T(8,128)(2,1)S(1)} %constant_dynamic-slice_fusion.1), channel_id=1, source_target_pairs={{0,16},{16,32},{32,48},{48,64},{64,80},{80,96},{96,112},{128,144},... | collective-permute-start | bytes 1351688 | tf_op jit(solution)/shard_map/ppermute | solution.py:161
  57.2 32.7 %collective-permute-start.4 = (bf16[352,640]{1,0:T(8,128)(2,1)}, bf16[352,640]{1,0:T(8,128)(2,1)S(1)}, u32[]{:S(2)}, u32[]{:S(2)}) collective-permute-start(bf16[352,640]{1,0:T(8,128)(2,1)} %collective-permute-done.3), channel_id=1, source_target_pairs={{0,128},{128,256},{256,384},{1,129},{129,257},{257,385},{2,130},{1... | collective-permute-start | bytes 1351688 | tf_op jit(solution)/shard_map/ppermute | solution.py:161
  59.2 36.9 %collective-permute-start.1 = (bf16[160,640]{1,0:T(8,128)(2,1)}, bf16[160,640]{1,0:T(8,128)(2,1)S(1)}, u32[]{:S(2)}, u32[]{:S(2)}) collective-permute-start(bf16[160,640]{1,0:T(8,128)(2,1)} %constant_dynamic-slice_fusion), channel_id=1, source_target_pairs={{0,16},{16,32},{32,48},{48,64},{64,80},{80,96},{96,112},{112,128},... | collective-permute-start | bytes 614408 | tf_op jit(solution)/shard_map/ppermute | solution.py:23
